TPU v7x, 256 devices: a whole 4x4x8 slice. The times are simulated.
256 devices in a mesh: shard: 64 (over x, z_hi, y), rep: 4 (over z_lo, core).
Axes of the slice: x: 4, y: 4, z: 8 (z_hi: 4, z_lo: 2; z = z_hi * 2 + z_lo), core: 2. Of those that a mesh axis runs over, the one named last changes fastest.
Arguments:
- docs: bfloat16 [32768, 16384], P('shard', 'rep')
- pattern: int32 [256, 128], P('shard', 'rep'), may hold values 0 or 1
- owners: int32 [4], replicated, may hold values from 0 to 63
Outputs:
- scores: bfloat16 [4, 256, 32768], P(None, ('shard', 'rep'))
All inputs are finite; a program needn't handle non-finite values. No bound on the sum of `pattern` on one device may be relied on, other than what follows from the above.
Results may differ from a plain program's by a relative error of at most 0.001.
Values may be sent and summed in bfloat16 or wider, within the bound.
No kernel may reach another device: no remote copies, remote signals or barrier semaphores. Data moves between devices by JAX's collectives and lax.ppermute only.
A program may use at most 128 MiB of HBM per device.

v0:
```python
import math

import jax
import jax.numpy as jnp
from jax import lax
from jax.sharding import PartitionSpec as P

TERMS = 16384
QUERY = 256
STEPS = 4


EPSILON = 1e-06
CLIP_LEVEL = 1.5


def from_root(block, axis, owner):
    block = jnp.where(lax.axis_index(axis) == owner, block, jnp.zeros_like(block))
    return lax.psum(block, axis)


def on_device(docs, pattern, owners):
    n_shard = lax.axis_size("shard")
    n_rep = lax.axis_size("rep")
    shard_index = lax.axis_index("shard")
    rep_index = lax.axis_index("rep")
    doc_rows, term_cols = docs.shape
    tile_edge = 128
    row_share = QUERY // (n_shard * n_rep)
    weights = pattern.astype(jnp.bfloat16)
    masked = (
        docs.reshape(doc_rows // tile_edge, tile_edge, term_cols // tile_edge, tile_edge)
        * weights[:, None, :, None]
    ).reshape(doc_rows, term_cols)
    partial_sq = jnp.einsum("dt,dt->d", masked, masked, preferred_element_type=jnp.float32)
    doc_sq = lax.psum(partial_sq, "rep")
    inverse = lax.rsqrt(doc_sq + EPSILON)
    all_inverse = lax.all_gather(inverse, "shard", axis=0, tiled=True)
    sharpen = math.sqrt(TERMS) * 0.5
    results = []
    for step_index in range(STEPS):
        offset = step_index % (doc_rows // QUERY) * QUERY
        candidate = masked[offset : offset + QUERY]
        queries = from_root(candidate, "shard", owners[step_index])
        offset = step_index % (doc_rows // QUERY) * QUERY
        first_global = owners[step_index] * doc_rows + offset
        query_inv = lax.dynamic_slice_in_dim(all_inverse, first_global, QUERY, 0).reshape(
            n_shard, n_rep, row_share
        )
        similar = lax.dot_general(
            queries, masked, (((1,), (1,)), ((), ())), preferred_element_type=jnp.float32
        )
        summed = lax.psum(similar, "rep").reshape(n_shard, n_rep, row_share, doc_rows)
        own_rows = lax.dynamic_index_in_dim(summed, rep_index, 1, keepdims=False)
        received = lax.all_to_all(own_rows, "shard", split_axis=0, concat_axis=2, tiled=True)[0]
        shard_inv = lax.dynamic_index_in_dim(query_inv, shard_index, 0, keepdims=False)
        row_inv = lax.dynamic_index_in_dim(shard_inv, rep_index, 0, keepdims=False)
        scaled = received * row_inv[:, None] * all_inverse[None, :] * sharpen
        results.append(jnp.clip(scaled, -CLIP_LEVEL, CLIP_LEVEL).astype(jnp.bfloat16))
    return jnp.stack(results)


def solution(mesh):
    return jax.shard_map(
        on_device,
        mesh=mesh,
        in_specs=(P("shard", "rep"), P("shard", "rep"), P()),
        out_specs=P(None, ("shard", "rep"), None),
        check_vma=False,
    )
```

profile of v0, /device:TPU:32, one launch (start us, length us, event | category | flops | bytes accessed | tf_op | source)
XLA Modules:
  0.0 1161.1 jit_solution(10522000148827303313)
XLA Ops:
  6.5 1.5 fusion.2
  10.4 0.7 convert_element_type.19
  11.1 3.4 copy.8
  15.5 6.0 copy_bitcast_fusion.2
  21.6 6.0 copy_bitcast_fusion
  28.5 1.6 copy-done
  30.0 3.7 fusion
  33.8 771.8 %all-reduce.7.cloned.1.call-done = (bf16[256,4096]{1,0:T(8,128)(2,1)}, bf16[256,4096]{1,0:T(8,128)(2,1)}, bf16[256,4096]{1,0:T(8,128)(2,1)}, bf16[256,4096]{1,0:T(8,128)(2,1)}) async-done(((bf16[256,4096]{1,0:T(8,128)(2,1)}, bf16[256,4096]{1,0:T(8,128)(2,1)}, bf16[256,4096]{1,0:T(8,128)(2,1)}, bf16[256,4096]{1,0:T(8,128)(2,1)}), (bf16[256,4096]{1,0:T(8,128)(2,1)}, bf16[256,4096]{1,0:T(8,128)(2,1)}, ...) | async-done | bytes 8388624 | tf_op jit(solution)/shard_map/psum | solution.py:19
  805.5 4.2 fusion.3
  809.8 0.9 reshape.113
  810.7 3.8 fusion.4
  814.5 1.0 reshape.115
  815.5 4.3 fusion.5
  819.8 1.0 reshape.117
  820.8 3.8 fusion.6
  824.6 1.0 reshape.119
  825.6 7.8 psum.65
  833.3 52.9 %all-reduce.5.cloned.1.call-done = (f32[64,4,1,512]{3,1,0,2:T(4,128)}, f32[64,4,1,512]{3,1,0,2:T(4,128)}, f32[64,4,1,512]{3,1,0,2:T(4,128)}, f32[64,4,1,512]{3,1,0,2:T(4,128)}) async-done(((f32[64,4,1,512]{3,1,0,2:T(4,128)}, f32[64,4,1,512]{3,1,0,2:T(4,128)}, f32[64,4,1,512]{3,1,0,2:T(4,128)}, f32[64,4,1,512]{3,1,0,2:T(4,128)}), (f32[64,4,1,512]{3,1,0,2:T(4,128)}, f32[64,4,1,512]{3,1,0,2:T(4,128)}, ...) | async-done | bytes 2097168 | tf_op jit(solution)/shard_map/psum | solution.py:53
  886.2 1.8 dynamic-slice_bitcast_fusion.2
  888.0 13.1 %all-to-all-start.1 = ((f32[64,1,512]{2,1,0:T(1,128)}), f32[64,1,512]{2,1,0:T(1,128)S(1)}, u32[]{:S(2)}, u32[]{:S(2)}) async-start(f32[64,1,512]{2,1,0:T(1,128)} %dynamic-slice_bitcast_fusion.2), calls=%async_computation.1 | async-start | bytes 262144 | tf_op jit(solution)/shard_map/all_to_all | solution.py:55
  901.2 1.8 dynamic-slice_bitcast_fusion.1
  903.0 11.3 all-to-all-done.1
  914.3 4.6 all-to-all-start.2
  918.9 192.4 %all-gather = f32[64,1,512]{2,1,0:T(1,128)S(1)} all-gather(f32[1,1,512]{2,1,0:T(1,128)S(1)} %bitcast.81), channel_id=1, replica_groups=mesh['shard'=64,'rep'=4] {'shard'}, dimensions={0}, use_global_device_ids=true | all-gather | bytes 133120 | tf_op jit(solution)/shard_map/all_gather | solution.py:38
  1114.3 0.7 constant_dynamic-slice_fusion.2
  1115.6 1.8 dynamic-slice_bitcast_fusion
  1117.4 4.6 all-to-all-start.3
  1122.1 1.8 dynamic-slice_bitcast_fusion.3
  1124.5 10.1 all-to-all-done.3
  1134.7 4.6 all-to-all-start
  1140.5 11.4 all-to-all-done
  1152.9 1.3 pad_maximum_fusion
  (29 shorter events, 5.8 us)
Async XLA Ops:
  6.5 799.0 %all-reduce.7.cloned.1.call-start = ((), (), s32[]{:S(2)}) async-start(), calls=%async_computation.5 | async-start | bytes 16777216 | tf_op jit(solution)/shard_map/psum | solution.py:19
  27.6 858.6 %all-reduce.5.cloned.1.call-start = ((), (), s32[]{:S(2)}) async-start(), calls=%async_computation.4 | async-start | bytes 4194304 | tf_op jit(solution)/shard_map/psum | solution.py:53
  27.8 2.2 copy-start
  805.5 5.2 copy-start.2
  815.5 5.2 copy-start.1
  888.0 26.2 %all-to-all-start.1 = ((f32[64,1,512]{2,1,0:T(1,128)}), f32[64,1,512]{2,1,0:T(1,128)S(1)}, u32[]{:S(2)}, u32[]{:S(2)}) async-start(f32[64,1,512]{2,1,0:T(1,128)} %dynamic-slice_bitcast_fusion.2), calls=%async_computation.1 | async-start | bytes 262144 | tf_op jit(solution)/shard_map/all_to_all | solution.py:55
  914.3 203.2 %all-to-all-start.2 = ((f32[64,1,512]{2,1,0:T(1,128)}), f32[64,1,512]{2,1,0:T(1,128)S(1)}, u32[]{:S(2)}, u32[]{:S(2)}) async-start(f32[64,1,512]{2,1,0:T(1,128)} %dynamic-slice_bitcast_fusion.1), calls=%async_computation.2 | async-start | bytes 262144 | tf_op jit(solution)/shard_map/all_to_all | solution.py:55
  1117.4 17.2 %all-to-all-start.3 = ((f32[64,1,512]{2,1,0:T(1,128)}), f32[64,1,512]{2,1,0:T(1,128)S(1)}, u32[]{:S(2)}, u32[]{:S(2)}) async-start(f32[64,1,512]{2,1,0:T(1,128)} %dynamic-slice_bitcast_fusion), calls=%async_computation.3 | async-start | bytes 262144 | tf_op jit(solution)/shard_map/all_to_all | solution.py:55
  1134.7 17.2 %all-to-all-start = ((f32[64,1,512]{2,1,0:T(1,128)}), f32[64,1,512]{2,1,0:T(1,128)S(1)}, u32[]{:S(2)}, u32[]{:S(2)}) async-start(f32[64,1,512]{2,1,0:T(1,128)} %dynamic-slice_bitcast_fusion.3), calls=%async_computation | async-start | bytes 262144 | tf_op jit(solution)/shard_map/all_to_all | solution.py:55
Sparse Core Ops, SparseCore 0:
  27.7 777.7 all-reduce.6
  825.7 60.4 all-reduce.4
where the time goes:
time: 1160 us
  waiting for transfers between devices  857 us (74%)
  blocking collectives  200 us (17%)
  local copies, waits for them, and re-layouts  32.3 us (3%)
  starting transfers between devices  27.2 us (2%)
  between operations  18.5 us (2%)
  matrix products  16.1 us (1%)
    psum x1, waiting for transfers between devices, from_root(): return lax.psum(block, axis)  772 us
    all_gather x1, blocking collectives, on_device(): all_inverse = lax.all_gather(inverse, 'shard', axis=0, tiled=True)  192 us
    psum x1, waiting for transfers between devices, on_device(): lax.psum(similar, 'rep').reshape(n_shard, n_rep, row_share, doc_rows)  52.9 us
    all_to_all x4, waiting for transfers between devices, on_device(): lax.all_to_all(own_rows, 'shard', split_axis=0, concat_axis=2, tiled=True)  32.8 us
    all_to_all x4, starting transfers between devices, on_device(): lax.all_to_all(own_rows, 'shard', split_axis=0, concat_axis=2, tiled=True)  27 us
  transfers between devices with their start and end apart: 6, of which 5 were waited for; matrix products, arithmetic and copies ran while one was open for 1% of the time, Pallas kernels for 0%

commit v1 on v0

v1 whole, which is shorter than its diff:
```python
import math

import jax
import jax.numpy as jnp
from jax import lax
from jax.sharding import Mesh
from jax.sharding import PartitionSpec as P

TERMS = 16384
QUERY = 256
STEPS = 4


EPSILON = 1e-06
CLIP_LEVEL = 1.5

AX = ("x", "zh", "y")
RP = ("zl", "c")


def scatter_from_owner(cand, owners, sizes):
    steps, rows, terms = cand.shape
    nx, nz, ny = sizes
    coord = {"x": owners // (nz * ny), "zh": (owners // ny) % nz, "y": owners % ny}
    buf = cand.reshape(steps, nx, nz, ny, rows // (nx * nz * ny), terms)
    for name in ("y", "x", "zh"):
        dim = 1 + AX.index(name)
        got = lax.all_to_all(buf, name, split_axis=dim, concat_axis=dim, tiled=True)
        buf = jnp.stack(
            [lax.dynamic_slice_in_dim(got[s], coord[name][s], 1, axis=dim - 1) for s in range(steps)]
        )
    return buf.reshape(steps, rows // (nx * nz * ny), terms)


def on_device(docs, pattern, owners, sizes):
    nx, nz, ny = sizes
    n_shard = nx * nz * ny
    n_rep = lax.axis_size(RP)
    rep_index = lax.axis_index(RP)
    doc_rows, term_cols = docs.shape
    tile_edge = 128
    weights = pattern.astype(jnp.bfloat16)
    masked = (
        docs.reshape(doc_rows // tile_edge, tile_edge, term_cols // tile_edge, tile_edge)
        * weights[:, None, :, None]
    ).reshape(doc_rows, term_cols)
    partial_sq = jnp.einsum("dt,dt->d", masked, masked, preferred_element_type=jnp.float32)
    doc_sq = lax.psum(partial_sq, RP)
    inverse = lax.rsqrt(doc_sq + EPSILON)
    sharpen = math.sqrt(TERMS) * 0.5
    cands = jnp.stack(
        [masked[(s % (doc_rows // QUERY)) * QUERY :][:QUERY] for s in range(STEPS)]
    )
    pieces = scatter_from_owner(cands, owners, sizes)
    queries = lax.all_gather(pieces, AX, axis=1, tiled=True)
    q_sq = jnp.einsum("sqt,sqt->sq", queries, queries, preferred_element_type=jnp.float32)
    q_inv = lax.rsqrt(lax.psum(q_sq, RP) + EPSILON)
    similar = jnp.einsum("sqt,dt->sqd", queries, masked, preferred_element_type=jnp.float32)
    row_share = QUERY // (n_shard * n_rep)
    similar = similar.reshape(STEPS, n_shard, n_rep, row_share, doc_rows).transpose(0, 2, 1, 3, 4)
    mine = lax.psum_scatter(similar, RP, scatter_dimension=1, tiled=True)[:, 0]
    my_inv = lax.dynamic_index_in_dim(
        q_inv.reshape(STEPS, n_shard, n_rep, row_share), rep_index, 2, keepdims=False
    )
    scaled = mine * my_inv[..., None] * inverse[None, None, None, :] * sharpen
    scores = jnp.clip(scaled, -CLIP_LEVEL, CLIP_LEVEL).astype(jnp.bfloat16)
    got = lax.all_to_all(scores, AX, split_axis=1, concat_axis=1, tiled=True)
    return got.transpose(0, 2, 1, 3).reshape(STEPS, row_share, n_shard * doc_rows)


def solution(mesh):
    names = dict(zip(("x", "z_hi", "y"), (4, 4, 4)))
    n_shard, n_rep = mesh.devices.shape
    sizes = (names["x"], names["z_hi"], names["y"])
    assert sizes[0] * sizes[1] * sizes[2] == n_shard and n_rep == 4
    mesh5 = Mesh(mesh.devices.reshape(*sizes, 2, 2), AX + RP)
    return jax.shard_map(
        lambda d, p, o: on_device(d, p, o, sizes),
        mesh=mesh5,
        in_specs=(P(AX, RP), P(AX, RP), P()),
        out_specs=P(None, AX + RP, None),
        check_vma=False,
    )
```

time: 1160 us -> 429 us (0.37)
  waiting for transfers between devices: 857 us -> 258 us
  blocking collectives: 200 us -> 35.3 us
  other arithmetic: 9.22 us -> 28 us
  between operations: 18.5 us -> 36.2 us
    psum x2 -> x0, waiting for transfers between devices: 825 us -> none  [the longest x1 772 us: from_root(): return lax.psum(block, axis)]
    all_gather x1 -> x0, blocking collectives: 192 us -> none  [on_device(): all_inverse = lax.all_gather(inverse, 'shard', axis=0, tiled=True)]
    all_gather x0 -> x1, waiting for transfers between devices: none -> 109 us  [on_device(): queries = lax.all_gather(pieces, AX, axis=1, tiled=True)]
    all_to_all x4 -> x3, waiting for transfers between devices: 32.8 us -> 109 us  [scatter_from_owner(): got = lax.all_to_all(buf, name, split_axis=dim, concat_axis=dim, tiled=True)]
    unnamed x2 -> x3, waiting for transfers between devices: 0.03 us -> 39.1 us
    all_to_all x0 -> x1, blocking collectives: none -> 28.6 us  [on_device(): got = lax.all_to_all(scores, AX, split_axis=1, concat_axis=1, tiled=True)]
    another operation x4 -> x6, local copies, waits for them, and re-layouts: 0.28 us -> 16.2 us  [the longest x3 12.2 us: on_device(): jnp.stack([masked[s % (doc_rows // QUERY) * QUERY:][:QUERY] for s in rang...]
    select_n x2 -> x0, local copies, waits for them, and re-layouts: 12.1 us -> none  [from_root(): jnp.where(lax.axis_index(axis) == owner, block, jnp.zeros_like(block))]
  transfers between devices with their start and end apart: 6 -> 5, of which waited for: 5 -> 5; matrix products, arithmetic and copies ran while one was open for 1% -> 4% of each run, Pallas kernels for 0% -> 0%
where the time goes in v1:
time: 429 us; the launch traced here: 427 us
  waiting for transfers between devices  258 us (60%)
  local copies, waits for them, and re-layouts  37.2 us (9%)
  between operations  36.2 us (8%)
  blocking collectives  35.3 us (8%)
  other arithmetic  28 us (7%)
  starting transfers between devices  17.8 us (4%)
  matrix products  15.1 us (4%)
    all_to_all x3, waiting for transfers between devices, scatter_from_owner(): got = lax.all_to_all(buf, name, split_axis=dim, concat_axis=dim, tiled=True)  109 us
    all_gather x1, waiting for transfers between devices, on_device(): queries = lax.all_gather(pieces, AX, axis=1, tiled=True)  109 us
    unnamed x3, waiting for transfers between devices  39.1 us
    all_to_all x1, blocking collectives, on_device(): got = lax.all_to_all(scores, AX, split_axis=1, concat_axis=1, tiled=True)  28.6 us
    all_to_all x3, starting transfers between devices, scatter_from_owner(): got = lax.all_to_all(buf, name, split_axis=dim, concat_axis=dim, tiled=True)  17.6 us
    dot_general x1, matrix products, on_device(): jnp.einsum('sqt,dt->sqd', queries, masked, preferred_element_type=jnp.flo...  15.1 us
    another operation x3, local copies, waits for them, and re-layouts, on_device(): jnp.stack([masked[s % (doc_rows // QUERY) * QUERY:][:QUERY] for s in rang...  12.2 us
    another operation x1, other arithmetic, on_device(): jnp.stack([masked[s % (doc_rows // QUERY) * QUERY:][:QUERY] for s in rang...  9.29 us
  transfers between devices with their start and end apart: 5, of which 5 were waited for; matrix products, arithmetic and copies ran while one was open for 4% of the time, Pallas kernels for 0%

profile of v1, /device:TPU:32, one launch (start us, length us, event | category | flops | bytes accessed | tf_op | source)
XLA Modules:
  0.0 427.5 jit_solution(3865099011559679779)
XLA Ops:
  6.5 0.7 convert_element_type.14
  7.2 3.4 copy.25
  11.0 2.3 fusion.17
  13.3 3.9 stack.13
  17.2 2.0 stack.12
  19.2 9.3 %pad_maximum_fusion = bf16[4,4,4,4,4,4096]{5,4,3,2,1,0:T(4,128)(2,1)S(1)} fusion(bf16[1,4,4,4,4,4096]{5,4,3,2,1,0:T(4,128)(2,1)} %stack.13, bf16[1,4,4,4,4,4096]{5,4,3,2,1,0:T(4,128)(2,1)} %stack.12), kind=kLoop, calls=%fused_computation.2 | loop fusion | flops 12582912 | bytes 12582912 | tf_op jit(solution)/shard_map/stack | solution.py:51
  28.5 6.2 %copy.7 = bf16[4,4,4,4,4,4096]{5,4,2,1,0,3:T(4,128)(2,1)} copy(bf16[4,4,4,4,4,4096]{5,4,3,2,1,0:T(4,128)(2,1)S(1)} %pad_maximum_fusion) | data formatting | bytes 16777216 | tf_op jit(solution)/shard_map/stack | solution.py:51
  34.8 5.8 %all-to-all-start = ((bf16[4,4,4,4,4,4096]{5,4,2,1,0,3:T(4,128)(2,1)}), bf16[4,4,4,4,4,4096]{5,4,2,1,0,3:T(4,128)(2,1)}, u32[]{:S(2)}, u32[]{:S(2)}) async-start(bf16[4,4,4,4,4,4096]{5,4,2,1,0,3:T(4,128)(2,1)} %copy.7), calls=%async_computation | async-start | bytes 16777216 | tf_op jit(solution)/shard_map/all_to_all | solution.py:28
  40.6 0.7 fusion.22
  48.8 85.8 %all-to-all-done = bf16[4,4,4,4,4,4096]{5,4,2,1,0,3:T(4,128)(2,1)} async-done(((bf16[4,4,4,4,4,4096]{5,4,2,1,0,3:T(4,128)(2,1)}), bf16[4,4,4,4,4,4096]{5,4,2,1,0,3:T(4,128)(2,1)}, u32[]{:S(2)}, u32[]{:S(2)}) %all-to-all-start) | async-done | bytes 8388640 | tf_op jit(solution)/shard_map/all_to_all | solution.py:28
  134.6 6.2 %fusion.16 = (bf16[1,4,4,4,4,4096]{5,4,2,1,0,3:T(4,128)(2,1)S(1)}, bf16[1,4,4,4,4,4096]{5,4,2,1,0,3:T(4,128)(2,1)S(1)}, bf16[1,4,4,4,4,4096]{5,4,2,1,0,3:T(4,128)(2,1)S(1)}, bf16[1,4,4,4,4,4096]{5,4,2,1,0,3:T(4,128)(2,1)S(1)}) fusion(bf16[4,4,4,4,4,4096]{5,4,2,1,0,3:T(4,128)(2,1)} %all-to-all-done), kind=kLoop, calls=%fused_computation.48 | loop fusion | bytes 16777216 | tf_op jit(solution)/shard_map/slice | solution.py:30
  141.7 2.0 pad_maximum_fusion.1
  143.7 2.2 copy.8
  145.9 4.3 %all-to-all-start.1 = ((bf16[4,4,4,1,4,4096]{5,4,3,2,0,1:T(4,128)(2,1)}), bf16[4,4,4,1,4,4096]{5,4,3,2,0,1:T(4,128)(2,1)S(1)}, u32[]{:S(2)}, u32[]{:S(2)}) async-start(bf16[4,4,4,1,4,4096]{5,4,3,2,0,1:T(4,128)(2,1)} %copy.8), calls=%async_computation.1 | async-start | bytes 4194304 | tf_op jit(solution)/shard_map/all_to_all | solution.py:28
  150.2 0.7 fusion.20
  158.3 17.4 %all-to-all-done.1 = bf16[4,4,4,1,4,4096]{5,4,3,2,0,1:T(4,128)(2,1)S(1)} async-done(((bf16[4,4,4,1,4,4096]{5,4,3,2,0,1:T(4,128)(2,1)}), bf16[4,4,4,1,4,4096]{5,4,3,2,0,1:T(4,128)(2,1)S(1)}, u32[]{:S(2)}, u32[]{:S(2)}) %all-to-all-start.1) | async-done | bytes 2097184 | tf_op jit(solution)/shard_map/all_to_all | solution.py:28
  175.7 0.9 fusion.18
  177.3 1.0 copy.9
  178.3 7.6 %all-to-all-start.2 = ((bf16[4,1,4,1,4,4096]{5,4,3,1,0,2:T(4,128)(2,1)}), bf16[4,1,4,1,4,4096]{5,4,3,1,0,2:T(4,128)(2,1)S(1)}, u32[]{:S(2)}, u32[]{:S(2)}) async-start(bf16[4,1,4,1,4,4096]{5,4,3,1,0,2:T(4,128)(2,1)} %copy.9), calls=%async_computation.2 | async-start | bytes 1048576 | tf_op jit(solution)/shard_map/all_to_all | solution.py:28
  193.4 6.2 %all-to-all-done.2 = bf16[4,1,4,1,4,4096]{5,4,3,1,0,2:T(4,128)(2,1)S(1)} async-done(((bf16[4,1,4,1,4,4096]{5,4,3,1,0,2:T(4,128)(2,1)}), bf16[4,1,4,1,4,4096]{5,4,3,1,0,2:T(4,128)(2,1)S(1)}, u32[]{:S(2)}, u32[]{:S(2)}) %all-to-all-start.2) | async-done | bytes 524320 | tf_op jit(solution)/shard_map/all_to_all | solution.py:28
  200.0 0.8 copy.10
  201.0 109.3 %all-gather.3.cloned.1.call-done = bf16[4,1,1,1,256,4096]{5,0,3,2,1,4:T(4,128)(2,1)} async-done(((bf16[4,1,1,1,4,4096]{5,0,3,2,1,4:T(4,128)(2,1)}), bf16[4,1,1,1,256,4096]{5,0,3,2,1,4:T(4,128)(2,1)}) %all-gather.3.cloned.1.call-update) | async-done | bytes 8388624 | tf_op jit(solution)/shard_map/all_gather | solution.py:55
  310.9 2.1 copy-done
  313.0 1.0 copy-done.1
  314.0 15.1 %fusion.5 = f32[4,4,64,1,512]{4,2,1,0,3:T(8,128)} fusion(bf16[4,64,4,4096]{3,0,2,1:T(4,128)(2,1)} %bitcast.70, bf16[512,4096]{1,0:T(8,128)(2,1)S(1)} %copy-done.1, bf16[64,8,32,128]{3,2,1,0:T(8,128)(2,1)S(1)} %bitcast.66), kind=kOutput, calls=%fused_computation.11 | convolution fusion | flops 4297064448 | bytes 18874368 | tf_op jit(solution)/shard_map/sqt,dt->sqd/dot_general | solution.py:58
  329.8 5.5 %fusion.1 = f32[512]{0:T(512)S(1)} fusion(bf16[512,4096]{1,0:T(8,128)(2,1)} %param.3, bf16[64,8,32,128]{3,2,1,0:T(8,128)(2,1)} %bitcast.67), kind=kLoop, calls=%fused_computation.4 | loop fusion | flops 8388096 | bytes 8390656 | tf_op jit(solution)/shard_map/dt,dt->d/dot_general | solution.py:47
  335.3 7.8 %fusion = f32[4,256]{0,1:T(8,128)S(1)} fusion(bf16[4,1,1,1,256,4096]{5,0,3,2,1,4:T(4,128)(2,1)} %all-gather.3.cloned.1.call-done), kind=kLoop, calls=%fused_computation.1 | loop fusion | flops 12581888 | bytes 8392704
  343.1 6.8 %all-reduce.1 = (f32[512]{0:T(512)S(1)}, f32[4,256]{1,0:T(4,128)S(1)}) all-reduce(f32[512]{0:T(512)S(1)} %fusion.1, f32[4,256]{1,0:T(4,128)S(1)} %copy.17), channel_id=1, replica_groups=mesh['x'=4,'zh'=4,'y'=4,'zl'=2,'c'=2] {'zl','c'}, use_global_device_ids=true, to_apply=%region_2.3 | all-reduce | flops 1536 | bytes 12288 | tf_op jit(solution)/shard_map/psum | solution.py:48
  350.2 39.1 %all-reduce.4.cloned.1.call-done = f32[4,4,64,1,512]{4,2,1,0,3:T(8,128)} async-done(((f32[4,4,64,1,512]{4,2,1,0,3:T(8,128)}), f32[4,4,64,1,512]{4,2,1,0,3:T(8,128)}) %all-reduce.4.cloned.1.call-update) | async-done | bytes 2097168
  389.3 1.8 fusion.14
  391.4 28.6 %all_to_all.20 = bf16[4,64,1,512]{3,0,2,1:T(4,128)(2,1)S(1)} all-to-all(bf16[4,64,1,512]{3,0,2,1:T(4,128)(2,1)S(1)} %copy.12), channel_id=1, replica_groups=mesh['x'=4,'zh'=4,'y'=4,'zl'=2,'c'=2] {'x','zh','y'}, dimensions={1} | all-to-all | bytes 524288 | tf_op jit(solution)/shard_map/all_to_all | solution.py:67
  419.9 0.7 copy.39
  (33 shorter events, 4.4 us)
Async XLA Ops:
  34.8 5.8 %copy-start.2 = (s32[4]{0:T(128)S(1)}, s32[4]{0:T(128)}, u32[]{:S(2)}) copy-start(s32[4]{0:T(128)} %param.5) | copy-start | bytes 52
  34.8 99.9 %all-to-all-start = ((bf16[4,4,4,4,4,4096]{5,4,2,1,0,3:T(4,128)(2,1)}), bf16[4,4,4,4,4,4096]{5,4,2,1,0,3:T(4,128)(2,1)}, u32[]{:S(2)}, u32[]{:S(2)}) async-start(bf16[4,4,4,4,4,4096]{5,4,2,1,0,3:T(4,128)(2,1)} %copy.7), calls=%async_computation | async-start | bytes 16777216 | tf_op jit(solution)/shard_map/all_to_all | solution.py:28
  145.9 29.8 %all-to-all-start.1 = ((bf16[4,4,4,1,4,4096]{5,4,3,2,0,1:T(4,128)(2,1)}), bf16[4,4,4,1,4,4096]{5,4,3,2,0,1:T(4,128)(2,1)S(1)}, u32[]{:S(2)}, u32[]{:S(2)}) async-start(bf16[4,4,4,1,4,4096]{5,4,3,2,0,1:T(4,128)(2,1)} %copy.8), calls=%async_computation.1 | async-start | bytes 4194304 | tf_op jit(solution)/shard_map/all_to_all | solution.py:28
  178.3 21.2 %all-to-all-start.2 = ((bf16[4,1,4,1,4,4096]{5,4,3,1,0,2:T(4,128)(2,1)}), bf16[4,1,4,1,4,4096]{5,4,3,1,0,2:T(4,128)(2,1)S(1)}, u32[]{:S(2)}, u32[]{:S(2)}) async-start(bf16[4,1,4,1,4,4096]{5,4,3,1,0,2:T(4,128)(2,1)} %copy.9), calls=%async_computation.2 | async-start | bytes 1048576 | tf_op jit(solution)/shard_map/all_to_all | solution.py:28
  185.9 124.4 %all-gather.3.cloned.1.call-start = ((), (), s32[]{:S(2)}) async-start(), calls=%async_computation.4 | async-start | bytes 8519680 | tf_op jit(solution)/shard_map/all_gather | solution.py:55
  200.8 188.5 %all-reduce.4.cloned.1.call-start = ((), (), s32[]{:S(2)}) async-start(), calls=%async_computation.5 | async-start | bytes 4194304
  310.3 3.7 copy-start.1
  310.9 2.1 copy-start
  314.0 15.2 %copy-start.3 = (u32[256]{0:T(256)S(1)}, u32[256]{0:T(256)}, u32[]{:S(2)}) copy-start(u32[256]{0:T(256)} %constant.81) | copy-start | bytes 3076
Sparse Core Ops, SparseCore 0:
  200.9 109.3 all-gather.2
  329.3 59.9 all-reduce.3

commit v2 on v1

v2 whole, which is shorter than its diff:
```python
import math

import jax
import jax.numpy as jnp
from jax import lax
from jax.sharding import Mesh
from jax.sharding import PartitionSpec as P

TERMS = 16384
QUERY = 256
STEPS = 4


EPSILON = 1e-06
CLIP_LEVEL = 1.5

AX = ("x", "zh", "y")
RP = ("zl", "c")
ORDERS = (("y", "x", "zh"), ("x", "y", "zh"))


def exchange(buf, name, dim):
    return lax.all_to_all(buf, name, split_axis=dim, concat_axis=dim, tiled=True)


def broadcast_from_owner(cand, owners, sizes, order):
    steps = cand.shape[0]
    nx, nz, ny = sizes
    coord = {"x": owners // (nz * ny), "zh": (owners // ny) % nz, "y": owners % ny}
    buf = cand
    for name in order:
        dim = 1 + AX.index(name)
        got = exchange(buf, name, dim)
        buf = jnp.stack(
            [lax.dynamic_slice_in_dim(got[s], coord[name][s], 1, axis=dim - 1) for s in range(steps)]
        )
    for name in reversed(order):
        dim = 1 + AX.index(name)
        shape = list(buf.shape)
        shape[dim] = sizes[AX.index(name)]
        buf = exchange(jnp.broadcast_to(buf, shape), name, dim)
    return buf


def on_device(docs, pattern, owners, sizes):
    nx, nz, ny = sizes
    n_shard = nx * nz * ny
    n_rep = lax.axis_size(RP)
    doc_rows, term_cols = docs.shape
    tile_edge = 128
    weights = pattern.astype(jnp.bfloat16)
    masked = (
        docs.reshape(doc_rows // tile_edge, tile_edge, term_cols // tile_edge, tile_edge)
        * weights[:, None, :, None]
    ).reshape(doc_rows, term_cols)
    partial_sq = jnp.einsum("dt,dt->d", masked, masked, preferred_element_type=jnp.float32)
    doc_sq = lax.psum(partial_sq, RP)
    inverse = lax.rsqrt(doc_sq + EPSILON)
    sharpen = math.sqrt(TERMS) * 0.5
    row_piece = QUERY // n_shard
    cands = jnp.stack(
        [masked[(s % (doc_rows // QUERY)) * QUERY :][:QUERY] for s in range(STEPS)]
    ).reshape(STEPS, nx, nz, ny, row_piece, term_cols)
    share = term_cols // len(ORDERS)
    parts = [
        broadcast_from_owner(cands[..., k * share : (k + 1) * share], owners, sizes, order)
        for k, order in enumerate(ORDERS)
    ]
    queries = jnp.concatenate(parts, axis=-1).reshape(STEPS, QUERY, term_cols)
    q_sq = jnp.einsum("sqt,sqt->sq", queries, queries, preferred_element_type=jnp.float32)
    q_inv = lax.rsqrt(lax.psum(q_sq, RP) + EPSILON)
    similar = jnp.einsum("sqt,dt->sqd", queries, masked, preferred_element_type=jnp.float32)
    row_share = QUERY // (n_shard * n_rep)
    similar = similar.reshape(STEPS, n_shard, 2, 2, row_share, doc_rows).transpose(0, 2, 3, 1, 4, 5)
    similar = jnp.sum(exchange(similar, "c", 2), axis=2)
    mine = jnp.sum(exchange(similar, "zl", 1), axis=1)
    rep_index = lax.axis_index(RP)
    my_inv = lax.dynamic_index_in_dim(
        q_inv.reshape(STEPS, n_shard, n_rep, row_share), rep_index, 2, keepdims=False
    )
    scaled = mine * my_inv[..., None] * inverse[None, None, None, :] * sharpen
    scores = jnp.clip(scaled, -CLIP_LEVEL, CLIP_LEVEL).astype(jnp.bfloat16)
    scores = scores.reshape(STEPS, nx, nz, ny, row_share, doc_rows)
    for name in ("y", "x", "zh"):
        scores = exchange(scores, name, 1 + AX.index(name))
    return scores.transpose(0, 4, 1, 2, 3, 5).reshape(STEPS, row_share, n_shard * doc_rows)


def solution(mesh):
    names = dict(zip(("x", "z_hi", "y"), (4, 4, 4)))
    n_shard, n_rep = mesh.devices.shape
    sizes = (names["x"], names["z_hi"], names["y"])
    assert sizes[0] * sizes[1] * sizes[2] == n_shard and n_rep == 4
    mesh5 = Mesh(mesh.devices.reshape(*sizes, 2, 2), AX + RP)
    return jax.shard_map(
        lambda d, p, o: on_device(d, p, o, sizes),
        mesh=mesh5,
        in_specs=(P(AX, RP), P(AX, RP), P()),
        out_specs=P(None, AX + RP, None),
        check_vma=False,
    )
```

time: 429 us -> 475 us (1.11)
  waiting for transfers between devices: 258 us -> 130 us
  blocking collectives: 35.3 us -> 124 us
  local copies, waits for them, and re-layouts: 37.2 us -> 118 us
  starting transfers between devices: 17.8 us -> 50.2 us
  other arithmetic: 28 us -> 13.8 us
  between operations: 36.2 us -> 22.8 us
  matrix products: 15.1 us -> 9.79 us
    all_gather x1 -> x0, waiting for transfers between devices: 109 us -> none  [on_device(): queries = lax.all_gather(pieces, AX, axis=1, tiled=True)]
    all_to_all x1 -> x8, blocking collectives: 28.6 us -> 117 us  [exchange(): lax.all_to_all(buf, name, split_axis=dim, concat_axis=dim, tiled=True)]
    unnamed x3 -> x0, waiting for transfers between devices: 39.1 us -> none
    all_to_all x3 -> x9, starting transfers between devices: 17.6 us -> 50.2 us  [exchange(): lax.all_to_all(buf, name, split_axis=dim, concat_axis=dim, tiled=True)]
    concatenate x0 -> x3, local copies, waits for them, and re-layouts: none -> 26.4 us  [on_device(): queries = jnp.concatenate(parts, axis=-1).reshape(STEPS, QUERY, term_cols)]
    all_to_all x3 -> x9, waiting for transfers between devices: 109 us -> 130 us  [exchange(): lax.all_to_all(buf, name, split_axis=dim, concat_axis=dim, tiled=True)]
    slice x5 -> x11, local copies, waits for them, and re-layouts: 8.62 us -> 28.6 us  [the longest x3 19 us: on_device(): cands[..., k * share:(k + 1) * share]]
    dot_general x0 -> x1, local copies, waits for them, and re-layouts: none -> 12.5 us  [on_device(): jnp.einsum('sqt,dt->sqd', queries, masked, preferred_element_type=jnp.flo...]
  transfers between devices with their start and end apart: 5 -> 9, of which waited for: 5 -> 8; matrix products, arithmetic and copies ran while one was open for 4% -> 9% of each run, Pallas kernels for 0% -> 0%
where the time goes in v2:
time: 475 us; the launch traced here: 469 us
  waiting for transfers between devices  130 us (27%)
  blocking collectives  124 us (26%)
  local copies, waits for them, and re-layouts  118 us (25%)
  starting transfers between devices  50.2 us (11%)
  between operations  22.8 us (5%)
  other arithmetic  13.8 us (3%)
  matrix products  9.79 us (2%)
    all_to_all x9, waiting for transfers between devices, exchange(): lax.all_to_all(buf, name, split_axis=dim, concat_axis=dim, tiled=True)  130 us
    all_to_all x8, blocking collectives, exchange(): lax.all_to_all(buf, name, split_axis=dim, concat_axis=dim, tiled=True)  117 us
    all_to_all x9, starting transfers between devices, exchange(): lax.all_to_all(buf, name, split_axis=dim, concat_axis=dim, tiled=True)  50.2 us
    concatenate x3, local copies, waits for them, and re-layouts, on_device(): queries = jnp.concatenate(parts, axis=-1).reshape(STEPS, QUERY, term_cols)  26.4 us
    unnamed x17, local copies, waits for them, and re-layouts  20.1 us
    slice x3, local copies, waits for them, and re-layouts, on_device(): cands[..., k * share:(k + 1) * share]  19 us
    dot_general x1, local copies, waits for them, and re-layouts, on_device(): jnp.einsum('sqt,dt->sqd', queries, masked, preferred_element_type=jnp.flo...  12.5 us
    dot_general x1, matrix products, on_device(): jnp.einsum('sqt,dt->sqd', queries, masked, preferred_element_type=jnp.flo...  9.79 us
  transfers between devices with their start and end apart: 9, of which 8 were waited for; matrix products, arithmetic and copies ran while one was open for 9% of the time, Pallas kernels for 0%

profile of v2, /device:TPU:32, one launch (start us, length us, event | category | flops | bytes accessed | tf_op | source)
XLA Modules:
  0.0 468.8 jit_solution(520191886185761009)
XLA Ops:
  16.2 4.6 constant_dynamic-update-slice_fusion.2
  25.3 7.9 %fusion.8 = (bf16[4,4,4,4,4,2048]{5,4,3,2,1,0:T(4,128)(2,1)S(1)}, bf16[4,4,4,4,4,2048]{5,4,3,2,1,0:T(4,128)(2,1)}) fusion(bf16[4,4,4,4,4,4096]{5,4,3,2,1,0:T(4,128)(2,1)} %constant_dynamic-update-slice_fusion), kind=kLoop, calls=%fused_computation.62 | loop fusion | bytes 16777216 | tf_op jit(solution)/shard_map/slice | solution.py:66
  37.2 4.9 %all-to-all-start.6 = ((bf16[4,4,4,4,4,2048]{5,4,3,2,0,1:T(4,128)(2,1)}), bf16[4,4,4,4,4,2048]{5,4,3,2,0,1:T(4,128)(2,1)}, u32[]{:S(2)}, u32[]{:S(2)}) async-start(bf16[4,4,4,4,4,2048]{5,4,3,2,0,1:T(4,128)(2,1)} %copy.43), calls=%async_computation.6 | async-start | bytes 8388608 | tf_op jit(solution)/shard_map/all_to_all | solution.py:23
  42.1 7.1 %copy.39 = bf16[4,4,4,4,4,2048]{5,4,2,1,0,3:T(4,128)(2,1)} copy(bf16[4,4,4,4,4,2048]{5,4,3,2,1,0:T(4,128)(2,1)} %get-tuple-element.8) | data formatting | bytes 8388608 | tf_op jit(solution)/shard_map/slice | solution.py:66
  49.2 42.0 %all-to-all-done.6 = bf16[4,4,4,4,4,2048]{5,4,3,2,0,1:T(4,128)(2,1)} async-done(((bf16[4,4,4,4,4,2048]{5,4,3,2,0,1:T(4,128)(2,1)}), bf16[4,4,4,4,4,2048]{5,4,3,2,0,1:T(4,128)(2,1)}, u32[]{:S(2)}, u32[]{:S(2)}) %all-to-all-start.6) | async-done | bytes 4194336 | tf_op jit(solution)/shard_map/all_to_all | solution.py:23
  91.2 5.2 %all-to-all-start = ((bf16[4,4,4,4,4,2048]{5,4,2,1,0,3:T(4,128)(2,1)}), bf16[4,4,4,4,4,2048]{5,4,2,1,0,3:T(4,128)(2,1)}, u32[]{:S(2)}, u32[]{:S(2)}) async-start(bf16[4,4,4,4,4,2048]{5,4,2,1,0,3:T(4,128)(2,1)} %copy.39), calls=%async_computation | async-start | bytes 8388608 | tf_op jit(solution)/shard_map/all_to_all | solution.py:23
  126.2 18.5 %all-to-all-done = bf16[4,4,4,4,4,2048]{5,4,2,1,0,3:T(4,128)(2,1)} async-done(((bf16[4,4,4,4,4,2048]{5,4,2,1,0,3:T(4,128)(2,1)}), bf16[4,4,4,4,4,2048]{5,4,2,1,0,3:T(4,128)(2,1)}, u32[]{:S(2)}, u32[]{:S(2)}) %all-to-all-start) | async-done | bytes 4194336 | tf_op jit(solution)/shard_map/all_to_all | solution.py:23
  154.8 7.1 %all-to-all-done.7 = bf16[4,1,4,4,4,2048]{5,4,2,1,0,3:T(4,128)(2,1)S(1)} async-done(((bf16[4,1,4,4,4,2048]{5,4,2,1,0,3:T(4,128)(2,1)}), bf16[4,1,4,4,4,2048]{5,4,2,1,0,3:T(4,128)(2,1)S(1)}, u32[]{:S(2)}, u32[]{:S(2)}) %all-to-all-start.7) | async-done | bytes 1048608 | tf_op jit(solution)/shard_map/all_to_all | solution.py:23
  167.0 10.8 %all-to-all-done.1 = bf16[4,4,4,1,4,2048]{5,4,3,2,0,1:T(4,128)(2,1)S(1)} async-done(((bf16[4,4,4,1,4,2048]{5,4,3,2,0,1:T(4,128)(2,1)}), bf16[4,4,4,1,4,2048]{5,4,3,2,0,1:T(4,128)(2,1)S(1)}, u32[]{:S(2)}, u32[]{:S(2)}) %all-to-all-start.1) | async-done | bytes 1048608 | tf_op jit(solution)/shard_map/all_to_all | solution.py:23
  177.9 7.6 %all-to-all-start.8 = ((bf16[4,1,4,1,4,2048]{5,4,3,1,0,2:T(4,128)(2,1)}), bf16[4,1,4,1,4,2048]{5,4,3,1,0,2:T(4,128)(2,1)S(1)}, u32[]{:S(2)}, u32[]{:S(2)}) async-start(bf16[4,1,4,1,4,2048]{5,4,3,1,0,2:T(4,128)(2,1)} %copy.45), calls=%async_computation.8 | async-start | bytes 524288 | tf_op jit(solution)/shard_map/all_to_all | solution.py:23
  187.1 7.6 %all-to-all-done.8 = bf16[4,1,4,1,4,2048]{5,4,3,1,0,2:T(4,128)(2,1)S(1)} async-done(((bf16[4,1,4,1,4,2048]{5,4,3,1,0,2:T(4,128)(2,1)}), bf16[4,1,4,1,4,2048]{5,4,3,1,0,2:T(4,128)(2,1)S(1)}, u32[]{:S(2)}, u32[]{:S(2)}) %all-to-all-start.8) | async-done | bytes 262176 | tf_op jit(solution)/shard_map/all_to_all | solution.py:23
  198.4 9.0 %all-to-all-done.2 = bf16[4,1,4,1,4,2048]{5,4,3,1,0,2:T(4,128)(2,1)S(1)} async-done(((bf16[4,1,4,1,4,2048]{5,4,3,1,0,2:T(4,128)(2,1)}), bf16[4,1,4,1,4,2048]{5,4,3,1,0,2:T(4,128)(2,1)S(1)}, u32[]{:S(2)}, u32[]{:S(2)}) %all-to-all-start.2) | async-done | bytes 262176 | tf_op jit(solution)/shard_map/all_to_all | solution.py:23
  212.0 9.0 %all-to-all-done.9 = bf16[4,1,4,1,4,2048]{5,0,4,3,1,2:T(4,128)(2,1)S(1)} async-done(((bf16[4,1,4,1,4,2048]{5,0,4,3,1,2:T(4,128)(2,1)}), bf16[4,1,4,1,4,2048]{5,0,4,3,1,2:T(4,128)(2,1)S(1)}, u32[]{:S(2)}, u32[]{:S(2)}) %all-to-all-start.9) | async-done | bytes 262176 | tf_op jit(solution)/shard_map/all_to_all | solution.py:23
  221.0 13.1 %all_to_all.85 = bf16[4,1,4,1,4,2048]{5,0,4,3,1,2:T(4,128)(2,1)S(1)} all-to-all(bf16[4,1,4,1,4,2048]{5,0,4,3,1,2:T(4,128)(2,1)S(1)} %broadcast_in_dim.46), channel_id=1, replica_groups=mesh['x'=4,'zh'=4,'y'=4,'zl'=2,'c'=2] {'zh'}, dimensions={2} | all-to-all | bytes 524288 | tf_op jit(solution)/shard_map/all_to_all | solution.py:23
  234.6 13.3 %all_to_all.86 = bf16[4,1,4,4,4,2048]{5,0,4,2,1,3:T(4,128)(2,1)S(1)} all-to-all(bf16[4,1,4,4,4,2048]{5,0,4,2,1,3:T(4,128)(2,1)S(1)} %broadcast_in_dim.54), channel_id=1, replica_groups=mesh['x'=4,'zh'=4,'y'=4,'zl'=2,'c'=2] {'y'}, dimensions={3} | all-to-all | bytes 2097152 | tf_op jit(solution)/shard_map/all_to_all | solution.py:23
  248.4 13.3 %all_to_all.87 = bf16[4,4,4,1,4,2048]{5,0,4,2,3,1:T(4,128)(2,1)S(1)} all-to-all(bf16[4,4,4,1,4,2048]{5,0,4,2,3,1:T(4,128)(2,1)S(1)} %broadcast_in_dim.48), channel_id=1, replica_groups=mesh['x'=4,'zh'=4,'y'=4,'zl'=2,'c'=2] {'x'}, dimensions={1} | all-to-all | bytes 2097152 | tf_op jit(solution)/shard_map/all_to_all | solution.py:23
  264.0 40.6 %all_to_all.88 = bf16[4,4,4,4,4,2048]{5,0,4,2,1,3:T(4,128)(2,1)} all-to-all(bf16[4,4,4,4,4,2048]{5,0,4,2,1,3:T(4,128)(2,1)S(1)} %broadcast_in_dim.50), channel_id=1, replica_groups=mesh['x'=4,'zh'=4,'y'=4,'zl'=2,'c'=2] {'y'}, dimensions={3} | all-to-all | bytes 8388608 | tf_op jit(solution)/shard_map/all_to_all | solution.py:23
  304.6 4.1 broadcast_in_dim.56
  308.7 13.6 %all-to-all-start.11 = ((bf16[4,4,4,4,4,2048]{5,0,4,2,3,1:T(4,128)(2,1)}), bf16[4,4,4,4,4,2048]{5,0,4,2,3,1:T(4,128)(2,1)}, u32[]{:S(2)}, u32[]{:S(2)}) async-start(bf16[4,4,4,4,4,2048]{5,0,4,2,3,1:T(4,128)(2,1)} %broadcast_in_dim.56), calls=%async_computation.11 | async-start | bytes 8388608 | tf_op jit(solution)/shard_map/all_to_all | solution.py:23
  332.4 25.8 %all-to-all-done.11 = bf16[4,4,4,4,4,2048]{5,0,4,2,3,1:T(4,128)(2,1)} async-done(((bf16[4,4,4,4,4,2048]{5,0,4,2,3,1:T(4,128)(2,1)}), bf16[4,4,4,4,4,2048]{5,0,4,2,3,1:T(4,128)(2,1)}, u32[]{:S(2)}, u32[]{:S(2)}) %all-to-all-start.11) | async-done | bytes 4194336 | tf_op jit(solution)/shard_map/all_to_all | solution.py:23
  358.2 7.9 %copy_dynamic-update-slice_fusion = bf16[4,4,4,4,4,4096]{5,0,4,2,1,3:T(4,128)(2,1)} fusion(bf16[4,4,4,4,4,4096]{5,0,4,2,1,3:T(4,128)(2,1)} %constant_dynamic-update-slice_fusion.4, bf16[4,4,4,4,4,2048]{5,0,4,2,3,1:T(4,128)(2,1)} %all-to-all-done.11), kind=kLoop, calls=%fused_computation.8 | loop fusion | bytes 8388608 | tf_op jit(solution)/shard_map/concatenate | solution.py:69
  366.1 12.4 %copy.48 = bf16[4,4,4,4,4,4096]{5,3,2,1,4,0:T(4,128)(2,1)} copy(bf16[4,4,4,4,4,4096]{5,0,4,2,1,3:T(4,128)(2,1)} %copy_dynamic-update-slice_fusion) | data formatting | bytes 16777216 | tf_op jit(solution)/shard_map/concatenate | solution.py:69
  378.5 6.2 %copy.52 = bf16[4,4,4,4,4,4096]{5,0,4,3,2,1:T(4,128)(2,1)} copy(bf16[4,4,4,4,4,4096]{5,0,4,2,1,3:T(4,128)(2,1)S(1)} %copy-done) | data formatting | bytes 16777216 | tf_op jit(solution)/shard_map/concatenate | solution.py:69
  384.6 12.5 %dot_general.13 = bf16[4,64,2,2,4096]{4,1,3,2,0:T(8,128)(2,1)} reshape(bf16[4,4,4,4,4,4096]{5,3,2,1,4,0:T(4,128)(2,1)} %copy.48) | data formatting | bytes 16777216 | tf_op jit(solution)/shard_map/sqt,dt->sqd/dot_general | solution.py:72
  397.2 9.8 %fusion.4 = f32[4,2,2,64,1,512]{5,3,2,1,0,4:T(8,128)S(1)} fusion(bf16[4,64,2,2,4096]{4,1,3,2,0:T(8,128)(2,1)} %dot_general.13, bf16[512,4096]{1,0:T(8,128)(2,1)} %param.3, bf16[64,8,32,128]{3,2,1,0:T(8,128)(2,1)} %bitcast.60), kind=kOutput, calls=%fused_computation.9 | convolution fusion | flops 4297064448 | bytes 18874368 | tf_op jit(solution)/shard_map/sqt,dt->sqd/dot_general | solution.py:72
  407.2 5.4 %all_to_all.89 = f32[4,2,2,64,1,512]{5,3,1,0,4,2:T(8,128)S(1)} all-to-all(f32[4,2,2,64,1,512]{5,3,1,0,4,2:T(8,128)S(1)} %copy.49), channel_id=1, replica_groups=mesh['x'=4,'zh'=4,'y'=4,'zl'=2,'c'=2] {'c'}, dimensions={2} | all-to-all | bytes 4194304 | tf_op jit(solution)/shard_map/all_to_all | solution.py:23
  414.0 5.2 %all-to-all-start.13 = ((f32[4,2,64,1,512]{4,2,0,3,1:T(8,128)}), f32[4,2,64,1,512]{4,2,0,3,1:T(8,128)S(1)}, u32[]{:S(2)}, u32[]{:S(2)}) async-start(f32[4,2,64,1,512]{4,2,0,3,1:T(8,128)} %copy.50), calls=%async_computation.13 | async-start | bytes 2097152 | tf_op jit(solution)/shard_map/all_to_all | solution.py:23
  419.2 7.8 %fusion = f32[4,256]{0,1:T(8,128)S(1)} fusion(bf16[4,256,4096]{2,0,1:T(4,128)(2,1)} %bitcast.58), kind=kLoop, calls=%fused_computation.1 | loop fusion | flops 12581888 | bytes 8392704
  427.0 7.5 %all-reduce = (f32[512]{0:T(512)S(1)}, f32[4,256]{1,0:T(4,128)S(1)}) all-reduce(f32[512]{0:T(512)S(1)} %fusion.1, f32[4,256]{1,0:T(4,128)S(1)} %copy.62), channel_id=1, replica_groups=mesh['x'=4,'zh'=4,'y'=4,'zl'=2,'c'=2] {'zl','c'}, use_global_device_ids=true, to_apply=%region_3.4 | all-reduce | flops 1536 | bytes 12288 | tf_op jit(solution)/shard_map/psum | solution.py:57
  436.3 9.1 %all_to_all.90 = bf16[4,4,4,4,1,512]{5,2,1,0,4,3:T(4,128)(2,1)S(1)} all-to-all(bf16[4,4,4,4,1,512]{5,2,1,0,4,3:T(4,128)(2,1)S(1)} %copy.54), channel_id=1, replica_groups=mesh['x'=4,'zh'=4,'y'=4,'zl'=2,'c'=2] {'y'}, dimensions={3} | all-to-all | bytes 524288 | tf_op jit(solution)/shard_map/all_to_all | solution.py:23
  445.5 9.1 %all_to_all.91 = bf16[4,4,4,4,1,512]{5,3,2,0,4,1:T(4,128)(2,1)S(1)} all-to-all(bf16[4,4,4,4,1,512]{5,3,2,0,4,1:T(4,128)(2,1)S(1)} %copy.55), channel_id=1, replica_groups=mesh['x'=4,'zh'=4,'y'=4,'zl'=2,'c'=2] {'x'}, dimensions={1} | all-to-all | bytes 524288 | tf_op jit(solution)/shard_map/all_to_all | solution.py:23
  454.7 12.8 %all_to_all.92 = bf16[4,4,4,4,1,512]{5,3,1,0,4,2:T(4,128)(2,1)S(1)} all-to-all(bf16[4,4,4,4,1,512]{5,3,1,0,4,2:T(4,128)(2,1)S(1)} %copy.56), channel_id=1, replica_groups=mesh['x'=4,'zh'=4,'y'=4,'zl'=2,'c'=2] {'zh'}, dimensions={2} | all-to-all | bytes 524288 | tf_op jit(solution)/shard_map/all_to_all | solution.py:23
  (95 shorter events, 75.4 us)
Async XLA Ops:
  16.2 6.9 %copy-start.1 = (bf16[1,4,4,4,4,4096]{5,4,3,2,1,0:T(4,128)(2,1)S(1)}, bf16[1,4,4,4,4,4096]{5,4,3,2,1,0:T(4,128)(2,1)}, u32[]{:S(2)}) copy-start(bf16[1,4,4,4,4,4096]{5,4,3,2,1,0:T(4,128)(2,1)} %stack.19) | copy-start | bytes 6291460
  37.2 54.0 %all-to-all-start.6 = ((bf16[4,4,4,4,4,2048]{5,4,3,2,0,1:T(4,128)(2,1)}), bf16[4,4,4,4,4,2048]{5,4,3,2,0,1:T(4,128)(2,1)}, u32[]{:S(2)}, u32[]{:S(2)}) async-start(bf16[4,4,4,4,4,2048]{5,4,3,2,0,1:T(4,128)(2,1)} %copy.43), calls=%async_computation.6 | async-start | bytes 8388608 | tf_op jit(solution)/shard_map/all_to_all | solution.py:23
  49.2 47.2 %copy-start.5 = (s32[4]{0:T(128)S(1)}, s32[4]{0:T(128)}, u32[]{:S(2)}) copy-start(s32[4]{0:T(128)} %param.5) | copy-start | bytes 52
  91.2 53.5 %all-to-all-start = ((bf16[4,4,4,4,4,2048]{5,4,2,1,0,3:T(4,128)(2,1)}), bf16[4,4,4,4,4,2048]{5,4,2,1,0,3:T(4,128)(2,1)}, u32[]{:S(2)}, u32[]{:S(2)}) async-start(bf16[4,4,4,4,4,2048]{5,4,2,1,0,3:T(4,128)(2,1)} %copy.39), calls=%async_computation | async-start | bytes 8388608 | tf_op jit(solution)/shard_map/all_to_all | solution.py:23
  144.7 17.2 %all-to-all-start.7 = ((bf16[4,1,4,4,4,2048]{5,4,2,1,0,3:T(4,128)(2,1)}), bf16[4,1,4,4,4,2048]{5,4,2,1,0,3:T(4,128)(2,1)S(1)}, u32[]{:S(2)}, u32[]{:S(2)}) async-start(bf16[4,1,4,4,4,2048]{5,4,2,1,0,3:T(4,128)(2,1)} %copy.44), calls=%async_computation.7 | async-start | bytes 2097152 | tf_op jit(solution)/shard_map/all_to_all | solution.py:23
  161.9 16.0 %all-to-all-start.1 = ((bf16[4,4,4,1,4,2048]{5,4,3,2,0,1:T(4,128)(2,1)}), bf16[4,4,4,1,4,2048]{5,4,3,2,0,1:T(4,128)(2,1)S(1)}, u32[]{:S(2)}, u32[]{:S(2)}) async-start(bf16[4,4,4,1,4,2048]{5,4,3,2,0,1:T(4,128)(2,1)} %copy.40), calls=%async_computation.1 | async-start | bytes 2097152 | tf_op jit(solution)/shard_map/all_to_all | solution.py:23
  177.9 16.8 %all-to-all-start.8 = ((bf16[4,1,4,1,4,2048]{5,4,3,1,0,2:T(4,128)(2,1)}), bf16[4,1,4,1,4,2048]{5,4,3,1,0,2:T(4,128)(2,1)S(1)}, u32[]{:S(2)}, u32[]{:S(2)}) async-start(bf16[4,1,4,1,4,2048]{5,4,3,1,0,2:T(4,128)(2,1)} %copy.45), calls=%async_computation.8 | async-start | bytes 524288 | tf_op jit(solution)/shard_map/all_to_all | solution.py:23
  194.7 12.7 %all-to-all-start.2 = ((bf16[4,1,4,1,4,2048]{5,4,3,1,0,2:T(4,128)(2,1)}), bf16[4,1,4,1,4,2048]{5,4,3,1,0,2:T(4,128)(2,1)S(1)}, u32[]{:S(2)}, u32[]{:S(2)}) async-start(bf16[4,1,4,1,4,2048]{5,4,3,1,0,2:T(4,128)(2,1)} %copy.41), calls=%async_computation.2 | async-start | bytes 524288 | tf_op jit(solution)/shard_map/all_to_all | solution.py:23
  208.2 12.7 %all-to-all-start.9 = ((bf16[4,1,4,1,4,2048]{5,0,4,3,1,2:T(4,128)(2,1)}), bf16[4,1,4,1,4,2048]{5,0,4,3,1,2:T(4,128)(2,1)S(1)}, u32[]{:S(2)}, u32[]{:S(2)}) async-start(bf16[4,1,4,1,4,2048]{5,0,4,3,1,2:T(4,128)(2,1)} %broadcast_in_dim.52), calls=%async_computation.9 | async-start | bytes 524288 | tf_op jit(solution)/shard_map/all_to_all | solution.py:23
  308.7 49.5 %all-to-all-start.11 = ((bf16[4,4,4,4,4,2048]{5,0,4,2,3,1:T(4,128)(2,1)}), bf16[4,4,4,4,4,2048]{5,0,4,2,3,1:T(4,128)(2,1)}, u32[]{:S(2)}, u32[]{:S(2)}) async-start(bf16[4,4,4,4,4,2048]{5,0,4,2,3,1:T(4,128)(2,1)} %broadcast_in_dim.56), calls=%async_computation.11 | async-start | bytes 8388608 | tf_op jit(solution)/shard_map/all_to_all | solution.py:23
  322.4 3.7 copy-start.3
  323.0 2.1 copy-start.2
  326.1 2.2 copy-start.4
  366.1 12.4 %copy-start = (bf16[4,4,4,4,4,4096]{5,0,4,2,1,3:T(4,128)(2,1)S(1)}, bf16[4,4,4,4,4,4096]{5,0,4,2,1,3:T(4,128)(2,1)}, u32[]{:S(2)}) copy-start(bf16[4,4,4,4,4,4096]{5,0,4,2,1,3:T(4,128)(2,1)} %copy_dynamic-update-slice_fusion) | copy-start | bytes 25165828
  414.0 21.3 %all-to-all-start.13 = ((f32[4,2,64,1,512]{4,2,0,3,1:T(8,128)}), f32[4,2,64,1,512]{4,2,0,3,1:T(8,128)S(1)}, u32[]{:S(2)}, u32[]{:S(2)}) async-start(f32[4,2,64,1,512]{4,2,0,3,1:T(8,128)} %copy.50), calls=%async_computation.13 | async-start | bytes 2097152 | tf_op jit(solution)/shard_map/all_to_all | solution.py:23

commit v3 on v1

--- a/solution.py
+++ b/solution.py
@@ -18,18 +18,29 @@
 RP = ("zl", "c")
 
 
-def scatter_from_owner(cand, owners, sizes):
-    steps, rows, terms = cand.shape
+def exchange(buf, name, dim):
+    return lax.all_to_all(buf, name, split_axis=dim, concat_axis=dim, tiled=True)
+
+
+def scatter_from_owner(cands, owners, sizes):
+    rows, terms = cands[0].shape
     nx, nz, ny = sizes
     coord = {"x": owners // (nz * ny), "zh": (owners // ny) % nz, "y": owners % ny}
-    buf = cand.reshape(steps, nx, nz, ny, rows // (nx * nz * ny), terms)
-    for name in ("y", "x", "zh"):
+    bufs = [c.reshape(nx, nz, ny, rows // (nx * nz * ny), terms) for c in cands]
+    dim = AX.index("y")
+    buf = jnp.stack(
+        [
+            lax.dynamic_slice_in_dim(exchange(b, "y", dim), coord["y"][s], 1, axis=dim)
+            for s, b in enumerate(bufs)
+        ]
+    )
+    for name in ("x", "zh"):
         dim = 1 + AX.index(name)
-        got = lax.all_to_all(buf, name, split_axis=dim, concat_axis=dim, tiled=True)
+        got = exchange(buf, name, dim)
         buf = jnp.stack(
-            [lax.dynamic_slice_in_dim(got[s], coord[name][s], 1, axis=dim - 1) for s in range(steps)]
+            [lax.dynamic_slice_in_dim(got[s], coord[name][s], 1, axis=dim - 1) for s in range(len(cands))]
         )
-    return buf.reshape(steps, rows // (nx * nz * ny), terms)
+    return buf.reshape(len(cands), rows // (nx * nz * ny), terms)
 
 
 def on_device(docs, pattern, owners, sizes):
@@ -48,17 +59,16 @@
     doc_sq = lax.psum(partial_sq, RP)
     inverse = lax.rsqrt(doc_sq + EPSILON)
     sharpen = math.sqrt(TERMS) * 0.5
-    cands = jnp.stack(
-        [masked[(s % (doc_rows // QUERY)) * QUERY :][:QUERY] for s in range(STEPS)]
-    )
+    cands = [masked[(s % (doc_rows // QUERY)) * QUERY :][:QUERY] for s in range(STEPS)]
     pieces = scatter_from_owner(cands, owners, sizes)
     queries = lax.all_gather(pieces, AX, axis=1, tiled=True)
     q_sq = jnp.einsum("sqt,sqt->sq", queries, queries, preferred_element_type=jnp.float32)
     q_inv = lax.rsqrt(lax.psum(q_sq, RP) + EPSILON)
     similar = jnp.einsum("sqt,dt->sqd", queries, masked, preferred_element_type=jnp.float32)
     row_share = QUERY // (n_shard * n_rep)
-    similar = similar.reshape(STEPS, n_shard, n_rep, row_share, doc_rows).transpose(0, 2, 1, 3, 4)
-    mine = lax.psum_scatter(similar, RP, scatter_dimension=1, tiled=True)[:, 0]
+    similar = similar.reshape(STEPS, n_shard, 2, 2, row_share, doc_rows).transpose(0, 2, 3, 1, 4, 5)
+    similar = jnp.sum(exchange(similar, "c", 2), axis=2)
+    mine = jnp.sum(exchange(similar, "zl", 1), axis=1)
     my_inv = lax.dynamic_index_in_dim(
         q_inv.reshape(STEPS, n_shard, n_rep, row_share), rep_index, 2, keepdims=False
     )

time: 429 us -> 331 us (0.77)
  waiting for transfers between devices: 258 us -> 163 us
  other arithmetic: 28 us -> 13.7 us
  matrix products: 15.1 us -> 24.2 us
  starting transfers between devices: 17.8 us -> 24.4 us
  local copies, waits for them, and re-layouts: 37.2 us -> 30.8 us
    all_to_all x3 -> x5, waiting for transfers between devices: 109 us -> 59.3 us  [exchange(): lax.all_to_all(buf, name, split_axis=dim, concat_axis=dim, tiled=True)]
    unnamed x3 -> x1, waiting for transfers between devices: 39.1 us -> 0.02 us
    reshape x0 -> x4, local copies, waits for them, and re-layouts: none -> 9.54 us  [scatter_from_owner(): bufs = [c.reshape(nx, nz, ny, rows // (nx * nz * ny), terms) for c in cands]]
    dot_general x1, matrix products: 15.1 us -> 24.2 us  [on_device(): jnp.einsum('sqt,dt->sqd', queries, masked, preferred_element_type=jnp.flo...]
    another operation x3, local copies, waits for them, and re-layouts: 12.2 us -> 4.31 us  [scatter_from_owner(): jnp.stack([lax.dynamic_slice_in_dim(exchange(b, 'y', dim), coord['y'][s],...]
    another operation x1, other arithmetic: 9.29 us -> 1.96 us  [scatter_from_owner(): jnp.stack([lax.dynamic_slice_in_dim(exchange(b, 'y', dim), coord['y'][s],...]
    all_to_all x3 -> x5, starting transfers between devices: 17.6 us -> 24.4 us  [exchange(): lax.all_to_all(buf, name, split_axis=dim, concat_axis=dim, tiled=True)]
    slice x3 -> x2, local copies, waits for them, and re-layouts: 7.31 us -> 1.1 us  [scatter_from_owner(): got[s]]
  transfers between devices with their start and end apart: 5 -> 6, of which waited for: 5 -> 5; matrix products, arithmetic and copies ran while one was open for 4% -> 6% of each run, Pallas kernels for 0% -> 0%
where the time goes in v3:
time: 331 us; the launch traced here: 329 us
  waiting for transfers between devices  163 us (49%)
  blocking collectives  36.8 us (11%)
  between operations  36.3 us (11%)
  local copies, waits for them, and re-layouts  30.8 us (9%)
  starting transfers between devices  24.4 us (7%)
  matrix products  24.2 us (7%)
  other arithmetic  13.7 us (4%)
    all_gather x1, waiting for transfers between devices, on_device(): queries = lax.all_gather(pieces, AX, axis=1, tiled=True)  104 us
    all_to_all x5, waiting for transfers between devices, exchange(): lax.all_to_all(buf, name, split_axis=dim, concat_axis=dim, tiled=True)  59.3 us
    all_to_all x5, starting transfers between devices, exchange(): lax.all_to_all(buf, name, split_axis=dim, concat_axis=dim, tiled=True)  24.4 us
    dot_general x1, matrix products, on_device(): jnp.einsum('sqt,dt->sqd', queries, masked, preferred_element_type=jnp.flo...  24.2 us
    all_to_all x1, blocking collectives, on_device(): got = lax.all_to_all(scores, AX, split_axis=1, concat_axis=1, tiled=True)  23.9 us
    reshape x4, local copies, waits for them, and re-layouts, scatter_from_owner(): bufs = [c.reshape(nx, nz, ny, rows // (nx * nz * ny), terms) for c in cands]  9.54 us
    unnamed x1, other arithmetic  7.76 us
    psum x1, blocking collectives, on_device(): doc_sq = lax.psum(partial_sq, RP)  7.51 us
  transfers between devices with their start and end apart: 6, of which 5 were waited for; matrix products, arithmetic and copies ran while one was open for 6% of the time, Pallas kernels for 0%

profile of v3, /device:TPU:32, one launch (start us, length us, event | category | flops | bytes accessed | tf_op | source)
XLA Modules:
  0.0 329.5 jit_solution(7317208222158802450)
XLA Ops:
  7.2 3.4 %copy.38 = bf16[64,8,32,128]{3,2,1,0:T(8,128)(2,1)S(1)} copy(bf16[64,8,32,128]{3,1,2,0:T(8,128)(2,1)} %bitcast.66) | data formatting | bytes 8388608
  11.0 2.7 fusion.15
  13.8 2.5 reshape.78
  16.3 2.2 copy.19
  18.5 4.5 %all-to-all-start = ((bf16[4,4,4,4,4096]{4,3,1,0,2:T(4,128)(2,1)}), bf16[4,4,4,4,4096]{4,3,1,0,2:T(4,128)(2,1)}, u32[]{:S(2)}, u32[]{:S(2)}) async-start(bf16[4,4,4,4,4096]{4,3,1,0,2:T(4,128)(2,1)} %copy.19), calls=%async_computation | async-start | bytes 4194304 | tf_op jit(solution)/shard_map/all_to_all | solution.py:22
  23.0 2.5 reshape.79
  25.6 2.2 copy.20
  27.8 21.9 %all-to-all-done = bf16[4,4,4,4,4096]{4,3,1,0,2:T(4,128)(2,1)} async-done(((bf16[4,4,4,4,4096]{4,3,1,0,2:T(4,128)(2,1)}), bf16[4,4,4,4,4096]{4,3,1,0,2:T(4,128)(2,1)}, u32[]{:S(2)}, u32[]{:S(2)}) %all-to-all-start) | async-done | bytes 2097184 | tf_op jit(solution)/shard_map/all_to_all | solution.py:22
  49.7 3.6 %all-to-all-start.1 = ((bf16[4,4,4,4,4096]{4,3,1,0,2:T(4,128)(2,1)}), bf16[4,4,4,4,4096]{4,3,1,0,2:T(4,128)(2,1)S(1)}, u32[]{:S(2)}, u32[]{:S(2)}) async-start(bf16[4,4,4,4,4096]{4,3,1,0,2:T(4,128)(2,1)} %copy.20), calls=%async_computation.1 | async-start | bytes 4194304 | tf_op jit(solution)/shard_map/all_to_all | solution.py:22
  61.2 1.6 dynamic-slice_bitcast_fusion.3
  62.8 16.1 %all-to-all-done.1 = bf16[4,4,4,4,4096]{4,3,1,0,2:T(4,128)(2,1)S(1)} async-done(((bf16[4,4,4,4,4096]{4,3,1,0,2:T(4,128)(2,1)}), bf16[4,4,4,4,4096]{4,3,1,0,2:T(4,128)(2,1)S(1)}, u32[]{:S(2)}, u32[]{:S(2)}) %all-to-all-start.1) | async-done | bytes 2097184 | tf_op jit(solution)/shard_map/all_to_all | solution.py:22
  79.3 2.0 pad_maximum_fusion
  81.3 2.3 copy.21
  83.6 4.3 %all-to-all-start.2 = ((bf16[4,4,4,1,4,4096]{5,4,2,3,0,1:T(4,128)(2,1)}), bf16[4,4,4,1,4,4096]{5,4,2,3,0,1:T(4,128)(2,1)S(1)}, u32[]{:S(2)}, u32[]{:S(2)}) async-start(bf16[4,4,4,1,4,4096]{5,4,2,3,0,1:T(4,128)(2,1)} %copy.21), calls=%async_computation.2 | async-start | bytes 4194304 | tf_op jit(solution)/shard_map/all_to_all | solution.py:22
  96.1 16.3 %all-to-all-done.2 = bf16[4,4,4,1,4,4096]{5,4,2,3,0,1:T(4,128)(2,1)S(1)} async-done(((bf16[4,4,4,1,4,4096]{5,4,2,3,0,1:T(4,128)(2,1)}), bf16[4,4,4,1,4,4096]{5,4,2,3,0,1:T(4,128)(2,1)S(1)}, u32[]{:S(2)}, u32[]{:S(2)}) %all-to-all-start.2) | async-done | bytes 2097184 | tf_op jit(solution)/shard_map/all_to_all | solution.py:22
  112.4 0.9 fusion.16
  114.1 1.0 copy.22
  115.1 7.6 %all-to-all-start.3 = ((bf16[4,1,4,1,4,4096]{5,4,1,3,0,2:T(4,128)(2,1)}), bf16[4,1,4,1,4,4096]{5,4,1,3,0,2:T(4,128)(2,1)S(1)}, u32[]{:S(2)}, u32[]{:S(2)}) async-start(bf16[4,1,4,1,4,4096]{5,4,1,3,0,2:T(4,128)(2,1)} %copy.22), calls=%async_computation.3 | async-start | bytes 1048576 | tf_op jit(solution)/shard_map/all_to_all | solution.py:22
  130.4 5.1 %all-to-all-done.3 = bf16[4,1,4,1,4,4096]{5,4,1,3,0,2:T(4,128)(2,1)S(1)} async-done(((bf16[4,1,4,1,4,4096]{5,4,1,3,0,2:T(4,128)(2,1)}), bf16[4,1,4,1,4,4096]{5,4,1,3,0,2:T(4,128)(2,1)S(1)}, u32[]{:S(2)}, u32[]{:S(2)}) %all-to-all-start.3) | async-done | bytes 524320 | tf_op jit(solution)/shard_map/all_to_all | solution.py:22
  135.9 0.8 copy.23
  137.3 2.1 copy-done
  139.4 0.9 copy-done.1
  140.4 1.8 fusion.1
  142.2 103.9 %all-gather.3.cloned.1.call-done = bf16[4,1,1,1,256,4096]{5,0,3,2,1,4:T(4,128)(2,1)} async-done(((bf16[4,1,1,1,4,4096]{5,0,3,2,1,4:T(4,128)(2,1)}), bf16[4,1,1,1,256,4096]{5,0,3,2,1,4:T(4,128)(2,1)}) %all-gather.3.cloned.1.call-update) | async-done | bytes 8388624 | tf_op jit(solution)/shard_map/all_gather | solution.py:64
  246.1 24.2 %fusion.5 = f32[4,2,2,64,1,512]{5,3,2,1,0,4:T(8,128)S(1)} fusion(bf16[4,64,2,2,4096]{4,0,3,2,1:T(4,128)(2,1)} %bitcast.68, bf16[512,4096]{1,0:T(8,128)(2,1)} %param.3, bf16[64,8,32,128]{3,2,1,0:T(8,128)(2,1)} %bitcast.65), kind=kOutput, calls=%fused_computation.10 | convolution fusion | flops 4297064448 | bytes 18874368 | tf_op jit(solution)/shard_map/sqt,dt->sqd/dot_general | solution.py:67
  270.5 5.4 %all_to_all.37 = f32[4,2,2,64,1,512]{5,3,1,0,4,2:T(8,128)S(1)} all-to-all(f32[4,2,2,64,1,512]{5,3,1,0,4,2:T(8,128)S(1)} %copy.25), channel_id=1, replica_groups=mesh['x'=4,'zh'=4,'y'=4,'zl'=2,'c'=2] {'c'}, dimensions={2} | all-to-all | bytes 4194304 | tf_op jit(solution)/shard_map/all_to_all | solution.py:22
  276.2 1.2 copy.26
  277.4 4.5 %all-to-all-start.5 = ((f32[4,2,64,1,512]{4,2,0,3,1:T(8,128)}), f32[4,2,64,1,512]{4,2,0,3,1:T(8,128)S(1)}, u32[]{:S(2)}, u32[]{:S(2)}) async-start(f32[4,2,64,1,512]{4,2,0,3,1:T(8,128)} %copy.26), calls=%async_computation.5 | async-start | bytes 2097152 | tf_op jit(solution)/shard_map/all_to_all | solution.py:22
  281.9 7.8 %fusion = f32[4,256]{0,1:T(8,128)S(1)} fusion(bf16[4,1,1,1,256,4096]{5,0,3,2,1,4:T(4,128)(2,1)} %all-gather.3.cloned.1.call-done), kind=kLoop, calls=%fused_computation.1 | loop fusion | flops 12581888 | bytes 8392704
  289.7 7.5 %all-reduce = (f32[512]{0:T(512)S(1)}, f32[4,256]{1,0:T(4,128)S(1)}) all-reduce(f32[512]{0:T(512)S(1)} %fusion.1, f32[4,256]{1,0:T(4,128)S(1)} %copy.32), channel_id=1, replica_groups=mesh['x'=4,'zh'=4,'y'=4,'zl'=2,'c'=2] {'zl','c'}, use_global_device_ids=true, to_apply=%region_3.4 | all-reduce | flops 1536 | bytes 12288 | tf_op jit(solution)/shard_map/psum | solution.py:59
  298.1 23.9 %all_to_all.38 = bf16[4,64,1,512]{3,0,2,1:T(4,128)(2,1)S(1)} all-to-all(bf16[4,64,1,512]{3,0,2,1:T(4,128)(2,1)S(1)} %copy.27), channel_id=1, replica_groups=mesh['x'=4,'zh'=4,'y'=4,'zl'=2,'c'=2] {'x','zh','y'}, dimensions={1} | all-to-all | bytes 524288 | tf_op jit(solution)/shard_map/all_to_all | solution.py:77
  321.9 0.7 copy.51
  (35 shorter events, 5.8 us)
Async XLA Ops:
  18.5 31.1 %all-to-all-start = ((bf16[4,4,4,4,4096]{4,3,1,0,2:T(4,128)(2,1)}), bf16[4,4,4,4,4096]{4,3,1,0,2:T(4,128)(2,1)}, u32[]{:S(2)}, u32[]{:S(2)}) async-start(bf16[4,4,4,4,4096]{4,3,1,0,2:T(4,128)(2,1)} %copy.19), calls=%async_computation | async-start | bytes 4194304 | tf_op jit(solution)/shard_map/all_to_all | solution.py:22
  25.5 27.7 %copy-start.2 = (s32[4]{0:T(128)S(1)}, s32[4]{0:T(128)}, u32[]{:S(2)}) copy-start(s32[4]{0:T(128)} %param.5) | copy-start | bytes 52
  49.7 29.3 %all-to-all-start.1 = ((bf16[4,4,4,4,4096]{4,3,1,0,2:T(4,128)(2,1)}), bf16[4,4,4,4,4096]{4,3,1,0,2:T(4,128)(2,1)S(1)}, u32[]{:S(2)}, u32[]{:S(2)}) async-start(bf16[4,4,4,4,4096]{4,3,1,0,2:T(4,128)(2,1)} %copy.20), calls=%async_computation.1 | async-start | bytes 4194304 | tf_op jit(solution)/shard_map/all_to_all | solution.py:22
  83.6 28.8 %all-to-all-start.2 = ((bf16[4,4,4,1,4,4096]{5,4,2,3,0,1:T(4,128)(2,1)}), bf16[4,4,4,1,4,4096]{5,4,2,3,0,1:T(4,128)(2,1)S(1)}, u32[]{:S(2)}, u32[]{:S(2)}) async-start(bf16[4,4,4,1,4,4096]{5,4,2,3,0,1:T(4,128)(2,1)} %copy.21), calls=%async_computation.2 | async-start | bytes 4194304 | tf_op jit(solution)/shard_map/all_to_all | solution.py:22
  115.1 20.4 %all-to-all-start.3 = ((bf16[4,1,4,1,4,4096]{5,4,1,3,0,2:T(4,128)(2,1)}), bf16[4,1,4,1,4,4096]{5,4,1,3,0,2:T(4,128)(2,1)S(1)}, u32[]{:S(2)}, u32[]{:S(2)}) async-start(bf16[4,1,4,1,4,4096]{5,4,1,3,0,2:T(4,128)(2,1)} %copy.22), calls=%async_computation.3 | async-start | bytes 1048576 | tf_op jit(solution)/shard_map/all_to_all | solution.py:22
  122.6 123.5 %all-gather.3.cloned.1.call-start = ((), (), s32[]{:S(2)}) async-start(), calls=%async_computation.7 | async-start | bytes 8519680 | tf_op jit(solution)/shard_map/all_gather | solution.py:64
  136.7 3.7 %copy-start.1 = (bf16[512,4096]{1,0:T(8,128)(2,1)S(1)}, bf16[512,4096]{1,0:T(8,128)(2,1)}, u32[]{:S(2)}) copy-start(bf16[512,4096]{1,0:T(8,128)(2,1)} %param.3) | copy-start | bytes 12582916
  137.3 2.1 copy-start
  277.4 20.2 %all-to-all-start.5 = ((f32[4,2,64,1,512]{4,2,0,3,1:T(8,128)}), f32[4,2,64,1,512]{4,2,0,3,1:T(8,128)S(1)}, u32[]{:S(2)}, u32[]{:S(2)}) async-start(f32[4,2,64,1,512]{4,2,0,3,1:T(8,128)} %copy.26), calls=%async_computation.5 | async-start | bytes 2097152 | tf_op jit(solution)/shard_map/all_to_all | solution.py:22
Sparse Core Ops, SparseCore 0:
  136.8 109.2 all-gather.2

commit v4 on v3

--- a/solution.py
+++ b/solution.py
@@ -64,7 +64,10 @@
     queries = lax.all_gather(pieces, AX, axis=1, tiled=True)
     q_sq = jnp.einsum("sqt,sqt->sq", queries, queries, preferred_element_type=jnp.float32)
     q_inv = lax.rsqrt(lax.psum(q_sq, RP) + EPSILON)
-    similar = jnp.einsum("sqt,dt->sqd", queries, masked, preferred_element_type=jnp.float32)
+    flat_queries, stored = lax.optimization_barrier((queries.reshape(STEPS * QUERY, term_cols), masked))
+    similar = lax.optimization_barrier(
+        lax.dot_general(flat_queries, stored, (((1,), (1,)), ((), ())), preferred_element_type=jnp.float32)
+    )
     row_share = QUERY // (n_shard * n_rep)
     similar = similar.reshape(STEPS, n_shard, 2, 2, row_share, doc_rows).transpose(0, 2, 3, 1, 4, 5)
     similar = jnp.sum(exchange(similar, "c", 2), axis=2)

time: 331 us -> 330 us (level)
  matrix products: 24.2 us -> 8.32 us
  local copies, waits for them, and re-layouts: 30.8 us -> 41.9 us
  other arithmetic: 13.7 us -> 18.3 us
    dot_general x1, matrix products: 24.2 us -> 8.32 us  [on_device(): lax.dot_general(flat_queries, stored, (((1,), (1,)), ((), ())), preferred...]
    all_gather x0 -> x1, local copies, waits for them, and re-layouts: none -> 11.4 us  [on_device(): queries = lax.all_gather(pieces, AX, axis=1, tiled=True)]
    reshape x0 -> x2, local copies, waits for them, and re-layouts: none -> 3.57 us  [on_device(): similar.reshape(STEPS, n_shard, 2, 2, row_share, doc_rows)]
where the time goes in v4:
time: 330 us; the launch traced here: 329 us
  waiting for transfers between devices  163 us (49%)
  local copies, waits for them, and re-layouts  41.9 us (13%)
  blocking collectives  36.7 us (11%)
  between operations  36.3 us (11%)
  starting transfers between devices  24.4 us (7%)
  other arithmetic  18.3 us (6%)
  matrix products  8.32 us (3%)
    all_gather x1, waiting for transfers between devices, on_device(): queries = lax.all_gather(pieces, AX, axis=1, tiled=True)  104 us
    all_to_all x5, waiting for transfers between devices, exchange(): lax.all_to_all(buf, name, split_axis=dim, concat_axis=dim, tiled=True)  59.4 us
    all_to_all x5, starting transfers between devices, exchange(): lax.all_to_all(buf, name, split_axis=dim, concat_axis=dim, tiled=True)  24.4 us
    all_to_all x1, blocking collectives, on_device(): got = lax.all_to_all(scores, AX, split_axis=1, concat_axis=1, tiled=True)  23.7 us
    all_gather x1, local copies, waits for them, and re-layouts, on_device(): queries = lax.all_gather(pieces, AX, axis=1, tiled=True)  11.4 us
    reshape x4, local copies, waits for them, and re-layouts, scatter_from_owner(): bufs = [c.reshape(nx, nz, ny, rows // (nx * nz * ny), terms) for c in cands]  9.53 us
    dot_general x1, matrix products, on_device(): lax.dot_general(flat_queries, stored, (((1,), (1,)), ((), ())), preferred...  8.32 us
    unnamed x1, other arithmetic  7.76 us
  transfers between devices with their start and end apart: 6, of which 5 were waited for; matrix products, arithmetic and copies ran while one was open for 6% of the time, Pallas kernels for 0%

profile of v4, /device:TPU:32, one launch (start us, length us, event | category | flops | bytes accessed | tf_op | source)
XLA Modules:
  0.0 328.8 jit_solution(5505052815434453769)
XLA Ops:
  7.2 3.4 %copy.38 = bf16[64,8,32,128]{3,2,1,0:T(8,128)(2,1)S(1)} copy(bf16[64,8,32,128]{3,1,2,0:T(8,128)(2,1)} %bitcast.54) | data formatting | bytes 8388608
  11.0 2.7 fusion.7
  13.7 2.5 reshape.78
  16.3 2.2 copy.19
  18.5 4.5 %all-to-all-start = ((bf16[4,4,4,4,4096]{4,3,1,0,2:T(4,128)(2,1)}), bf16[4,4,4,4,4096]{4,3,1,0,2:T(4,128)(2,1)}, u32[]{:S(2)}, u32[]{:S(2)}) async-start(bf16[4,4,4,4,4096]{4,3,1,0,2:T(4,128)(2,1)} %copy.19), calls=%async_computation | async-start | bytes 4194304 | tf_op jit(solution)/shard_map/all_to_all | solution.py:22
  23.0 2.5 reshape.79
  25.5 2.2 copy.20
  27.8 21.9 %all-to-all-done = bf16[4,4,4,4,4096]{4,3,1,0,2:T(4,128)(2,1)} async-done(((bf16[4,4,4,4,4096]{4,3,1,0,2:T(4,128)(2,1)}), bf16[4,4,4,4,4096]{4,3,1,0,2:T(4,128)(2,1)}, u32[]{:S(2)}, u32[]{:S(2)}) %all-to-all-start) | async-done | bytes 2097184 | tf_op jit(solution)/shard_map/all_to_all | solution.py:22
  49.7 3.6 %all-to-all-start.1 = ((bf16[4,4,4,4,4096]{4,3,1,0,2:T(4,128)(2,1)}), bf16[4,4,4,4,4096]{4,3,1,0,2:T(4,128)(2,1)S(1)}, u32[]{:S(2)}, u32[]{:S(2)}) async-start(bf16[4,4,4,4,4096]{4,3,1,0,2:T(4,128)(2,1)} %copy.20), calls=%async_computation.1 | async-start | bytes 4194304 | tf_op jit(solution)/shard_map/all_to_all | solution.py:22
  61.5 1.6 dynamic-slice_bitcast_fusion.3
  63.1 15.9 %all-to-all-done.1 = bf16[4,4,4,4,4096]{4,3,1,0,2:T(4,128)(2,1)S(1)} async-done(((bf16[4,4,4,4,4096]{4,3,1,0,2:T(4,128)(2,1)}), bf16[4,4,4,4,4096]{4,3,1,0,2:T(4,128)(2,1)S(1)}, u32[]{:S(2)}, u32[]{:S(2)}) %all-to-all-start.1) | async-done | bytes 2097184 | tf_op jit(solution)/shard_map/all_to_all | solution.py:22
  79.4 2.9 pad_maximum_fusion
  82.3 4.3 %all-to-all-start.2 = ((bf16[4,4,4,1,4,4096]{5,4,2,3,0,1:T(4,128)(2,1)}), bf16[4,4,4,1,4,4096]{5,4,2,3,0,1:T(4,128)(2,1)S(1)}, u32[]{:S(2)}, u32[]{:S(2)}) async-start(bf16[4,4,4,1,4,4096]{5,4,2,3,0,1:T(4,128)(2,1)} %pad_maximum_fusion), calls=%async_computation.2 | async-start | bytes 4194304 | tf_op jit(solution)/shard_map/all_to_all | solution.py:22
  94.7 16.5 %all-to-all-done.2 = bf16[4,4,4,1,4,4096]{5,4,2,3,0,1:T(4,128)(2,1)S(1)} async-done(((bf16[4,4,4,1,4,4096]{5,4,2,3,0,1:T(4,128)(2,1)}), bf16[4,4,4,1,4,4096]{5,4,2,3,0,1:T(4,128)(2,1)S(1)}, u32[]{:S(2)}, u32[]{:S(2)}) %all-to-all-start.2) | async-done | bytes 2097184 | tf_op jit(solution)/shard_map/all_to_all | solution.py:22
  111.2 0.9 fusion.8
  112.8 1.0 copy.21
  113.8 7.6 %all-to-all-start.3 = ((bf16[4,1,4,1,4,4096]{5,4,1,3,0,2:T(4,128)(2,1)}), bf16[4,1,4,1,4,4096]{5,4,1,3,0,2:T(4,128)(2,1)S(1)}, u32[]{:S(2)}, u32[]{:S(2)}) async-start(bf16[4,1,4,1,4,4096]{5,4,1,3,0,2:T(4,128)(2,1)} %copy.21), calls=%async_computation.3 | async-start | bytes 1048576 | tf_op jit(solution)/shard_map/all_to_all | solution.py:22
  129.1 5.1 %all-to-all-done.3 = bf16[4,1,4,1,4,4096]{5,4,1,3,0,2:T(4,128)(2,1)S(1)} async-done(((bf16[4,1,4,1,4,4096]{5,4,1,3,0,2:T(4,128)(2,1)}), bf16[4,1,4,1,4,4096]{5,4,1,3,0,2:T(4,128)(2,1)S(1)}, u32[]{:S(2)}, u32[]{:S(2)}) %all-to-all-start.3) | async-done | bytes 524320 | tf_op jit(solution)/shard_map/all_to_all | solution.py:22
  136.1 1.6 copy-done
  137.6 3.7 %fusion.1 = (f32[512]{0:T(512)S(1)}, bf16[512,4096]{1,0:T(8,128)(2,1)}) fusion(bf16[512,4096]{1,0:T(8,128)(2,1)S(1)} %copy-done, bf16[64,8,32,128]{3,2,1,0:T(8,128)(2,1)S(1)} %bitcast.55), kind=kLoop, calls=%fused_computation.3 | loop fusion | flops 8388096 | bytes 12584960 | tf_op jit(solution)/shard_map/dt,dt->d/dot_general | solution.py:58
  141.3 103.5 %all-gather.3.cloned.1.call-done = bf16[4,1,1,1,256,4096]{5,0,3,2,1,4:T(4,128)(2,1)} async-done(((bf16[4,1,1,1,4,4096]{5,0,3,2,1,4:T(4,128)(2,1)}), bf16[4,1,1,1,256,4096]{5,0,3,2,1,4:T(4,128)(2,1)}) %all-gather.3.cloned.1.call-update) | async-done | bytes 8388624 | tf_op jit(solution)/shard_map/all_gather | solution.py:64
  244.9 11.4 %copy.23 = bf16[4,1,1,1,256,4096]{5,4,0,3,2,1:T(8,128)(2,1)} copy(bf16[4,1,1,1,256,4096]{5,0,3,2,1,4:T(4,128)(2,1)} %all-gather.3.cloned.1.call-done) | data formatting | bytes 16777216 | tf_op jit(solution)/shard_map/all_gather | solution.py:64
  256.2 8.3 %fusion.13 = f32[1024,512]{1,0:T(8,128)} fusion(bf16[1024,4096]{1,0:T(8,128)(2,1)} %bitcast.57, bf16[512,4096]{1,0:T(8,128)(2,1)S(1)} %copy-done.1), kind=kOutput, calls=%fused_computation.49 | convolution fusion | flops 4294967296 | bytes 14680064 | tf_op jit(solution)/shard_map/dot_general | solution.py:69
  264.6 2.5 reshape.82
  267.1 1.1 copy.43
  268.1 5.4 %all_to_all.37 = f32[4,2,2,64,1,512]{5,1,3,0,4,2:T(2,128)S(1)} all-to-all(f32[4,2,2,64,1,512]{5,1,3,0,4,2:T(2,128)S(1)} %bitcast.58), channel_id=1, replica_groups=mesh['x'=4,'zh'=4,'y'=4,'zl'=2,'c'=2] {'c'}, dimensions={2} | all-to-all | bytes 4194304 | tf_op jit(solution)/shard_map/all_to_all | solution.py:22
  273.6 2.0 reduce_sum.22
  275.6 1.2 copy.26
  276.8 4.5 %all-to-all-start.5 = ((f32[4,2,64,1,512]{4,2,0,3,1:T(8,128)}), f32[4,2,64,1,512]{4,2,0,3,1:T(8,128)S(1)}, u32[]{:S(2)}, u32[]{:S(2)}) async-start(f32[4,2,64,1,512]{4,2,0,3,1:T(8,128)} %copy.26), calls=%async_computation.5 | async-start | bytes 2097152 | tf_op jit(solution)/shard_map/all_to_all | solution.py:22
  281.3 7.8 %fusion = f32[4,256]{0,1:T(8,128)S(1)} fusion(bf16[4,1,1,1,256,4096]{5,0,3,2,1,4:T(4,128)(2,1)} %all-gather.3.cloned.1.call-done), kind=kLoop, calls=%fused_computation.1 | loop fusion | flops 12581888 | bytes 8392704
  289.1 7.6 %all-reduce = (f32[512]{0:T(512)S(1)}, f32[4,256]{1,0:T(4,128)S(1)}) all-reduce(f32[512]{0:T(512)S(1)} %get-tuple-element.11, f32[4,256]{1,0:T(4,128)S(1)} %copy.31), channel_id=1, replica_groups=mesh['x'=4,'zh'=4,'y'=4,'zl'=2,'c'=2] {'zl','c'}, use_global_device_ids=true, to_apply=%region_3.4 | all-reduce | flops 1536 | bytes 12288 | tf_op jit(solution)/shard_map/psum | solution.py:59
  297.6 23.7 %all_to_all.38 = bf16[4,64,1,512]{3,0,2,1:T(4,128)(2,1)S(1)} all-to-all(bf16[4,64,1,512]{3,0,2,1:T(4,128)(2,1)S(1)} %copy.27), channel_id=1, replica_groups=mesh['x'=4,'zh'=4,'y'=4,'zl'=2,'c'=2] {'x','zh','y'}, dimensions={1} | all-to-all | bytes 524288 | tf_op jit(solution)/shard_map/all_to_all | solution.py:80
  (36 shorter events, 6.8 us)
Async XLA Ops:
  18.5 31.1 %all-to-all-start = ((bf16[4,4,4,4,4096]{4,3,1,0,2:T(4,128)(2,1)}), bf16[4,4,4,4,4096]{4,3,1,0,2:T(4,128)(2,1)}, u32[]{:S(2)}, u32[]{:S(2)}) async-start(bf16[4,4,4,4,4096]{4,3,1,0,2:T(4,128)(2,1)} %copy.19), calls=%async_computation | async-start | bytes 4194304 | tf_op jit(solution)/shard_map/all_to_all | solution.py:22
  27.8 25.5 %copy-start.2 = (s32[4]{0:T(128)S(1)}, s32[4]{0:T(128)}, u32[]{:S(2)}) copy-start(s32[4]{0:T(128)} %param.5) | copy-start | bytes 52
  49.7 29.3 %all-to-all-start.1 = ((bf16[4,4,4,4,4096]{4,3,1,0,2:T(4,128)(2,1)}), bf16[4,4,4,4,4096]{4,3,1,0,2:T(4,128)(2,1)S(1)}, u32[]{:S(2)}, u32[]{:S(2)}) async-start(bf16[4,4,4,4,4096]{4,3,1,0,2:T(4,128)(2,1)} %copy.20), calls=%async_computation.1 | async-start | bytes 4194304 | tf_op jit(solution)/shard_map/all_to_all | solution.py:22
  82.3 28.9 %all-to-all-start.2 = ((bf16[4,4,4,1,4,4096]{5,4,2,3,0,1:T(4,128)(2,1)}), bf16[4,4,4,1,4,4096]{5,4,2,3,0,1:T(4,128)(2,1)S(1)}, u32[]{:S(2)}, u32[]{:S(2)}) async-start(bf16[4,4,4,1,4,4096]{5,4,2,3,0,1:T(4,128)(2,1)} %pad_maximum_fusion), calls=%async_computation.2 | async-start | bytes 4194304 | tf_op jit(solution)/shard_map/all_to_all | solution.py:22
  113.8 20.4 %all-to-all-start.3 = ((bf16[4,1,4,1,4,4096]{5,4,1,3,0,2:T(4,128)(2,1)}), bf16[4,1,4,1,4,4096]{5,4,1,3,0,2:T(4,128)(2,1)S(1)}, u32[]{:S(2)}, u32[]{:S(2)}) async-start(bf16[4,1,4,1,4,4096]{5,4,1,3,0,2:T(4,128)(2,1)} %copy.21), calls=%async_computation.3 | async-start | bytes 1048576 | tf_op jit(solution)/shard_map/all_to_all | solution.py:22
  121.4 123.5 %all-gather.3.cloned.1.call-start = ((), (), s32[]{:S(2)}) async-start(), calls=%async_computation.7 | async-start | bytes 8519680 | tf_op jit(solution)/shard_map/all_gather | solution.py:64
  135.4 2.2 copy-start
  244.9 11.4 %copy-start.1 = (bf16[512,4096]{1,0:T(8,128)(2,1)S(1)}, bf16[512,4096]{1,0:T(8,128)(2,1)}, u32[]{:S(2)}) copy-start(bf16[512,4096]{1,0:T(8,128)(2,1)} %get-tuple-element.8) | copy-start | bytes 12582916
  276.8 20.3 %all-to-all-start.5 = ((f32[4,2,64,1,512]{4,2,0,3,1:T(8,128)}), f32[4,2,64,1,512]{4,2,0,3,1:T(8,128)S(1)}, u32[]{:S(2)}, u32[]{:S(2)}) async-start(f32[4,2,64,1,512]{4,2,0,3,1:T(8,128)} %copy.26), calls=%async_computation.5 | async-start | bytes 2097152 | tf_op jit(solution)/shard_map/all_to_all | solution.py:22
Sparse Core Ops, SparseCore 0:
  135.6 109.2 all-gather.2

commit v5 on v4

--- a/solution.py
+++ b/solution.py
@@ -61,24 +61,23 @@
     sharpen = math.sqrt(TERMS) * 0.5
     cands = [masked[(s % (doc_rows // QUERY)) * QUERY :][:QUERY] for s in range(STEPS)]
     pieces = scatter_from_owner(cands, owners, sizes)
-    queries = lax.all_gather(pieces, AX, axis=1, tiled=True)
-    q_sq = jnp.einsum("sqt,sqt->sq", queries, queries, preferred_element_type=jnp.float32)
-    q_inv = lax.rsqrt(lax.psum(q_sq, RP) + EPSILON)
-    flat_queries, stored = lax.optimization_barrier((queries.reshape(STEPS * QUERY, term_cols), masked))
+    piece = pieces.shape[1]
+    flat_queries = lax.all_gather(pieces.reshape(STEPS * piece, term_cols), AX, axis=0, tiled=True)
+    q_sq = jnp.einsum("qt,qt->q", flat_queries, flat_queries, preferred_element_type=jnp.float32)
+    q_inv = lax.rsqrt(lax.psum(q_sq, RP) + EPSILON).reshape(n_shard, STEPS, piece)
+    flat_queries, stored = lax.optimization_barrier((flat_queries, masked))
     similar = lax.optimization_barrier(
         lax.dot_general(flat_queries, stored, (((1,), (1,)), ((), ())), preferred_element_type=jnp.float32)
     )
-    row_share = QUERY // (n_shard * n_rep)
-    similar = similar.reshape(STEPS, n_shard, 2, 2, row_share, doc_rows).transpose(0, 2, 3, 1, 4, 5)
-    similar = jnp.sum(exchange(similar, "c", 2), axis=2)
-    mine = jnp.sum(exchange(similar, "zl", 1), axis=1)
-    my_inv = lax.dynamic_index_in_dim(
-        q_inv.reshape(STEPS, n_shard, n_rep, row_share), rep_index, 2, keepdims=False
-    )
+    row_share = piece // n_rep
+    similar = similar.reshape(n_shard, STEPS, 2, 2, row_share, doc_rows)
+    similar = jnp.sum(exchange(similar, "c", 3), axis=3)
+    mine = jnp.sum(exchange(similar, "zl", 2), axis=2)
+    my_inv = lax.dynamic_slice_in_dim(q_inv, rep_index * row_share, row_share, axis=2)
     scaled = mine * my_inv[..., None] * inverse[None, None, None, :] * sharpen
     scores = jnp.clip(scaled, -CLIP_LEVEL, CLIP_LEVEL).astype(jnp.bfloat16)
-    got = lax.all_to_all(scores, AX, split_axis=1, concat_axis=1, tiled=True)
-    return got.transpose(0, 2, 1, 3).reshape(STEPS, row_share, n_shard * doc_rows)
+    got = exchange(scores, AX, 0)
+    return got.transpose(1, 2, 0, 3).reshape(STEPS, row_share, n_shard * doc_rows)
 
 
 def solution(mesh):

time: 330 us -> 321 us (0.973)
  local copies, waits for them, and re-layouts: 41.9 us -> 30.6 us
    all_to_all x1 -> x2, blocking collectives: 5.42 us -> 29.3 us  [exchange(): lax.all_to_all(buf, name, split_axis=dim, concat_axis=dim, tiled=True)]
    all_to_all x1 -> x0, blocking collectives: 23.7 us -> none  [on_device(): got = lax.all_to_all(scores, AX, split_axis=1, concat_axis=1, tiled=True)]
    all_gather x1 -> x0, local copies, waits for them, and re-layouts: 11.4 us -> none  [on_device(): queries = lax.all_gather(pieces, AX, axis=1, tiled=True)]
    unnamed x1 -> x0, other arithmetic: 7.76 us -> none
    dot_general x0 -> x1, other arithmetic: none -> 5.07 us  [on_device(): jnp.einsum('qt,qt->q', flat_queries, flat_queries, preferred_element_type...]
where the time goes in v5:
time: 321 us; the launch traced here: 320 us
  waiting for transfers between devices  163 us (51%)
  blocking collectives  39.6 us (12%)
  between operations  36.3 us (11%)
  local copies, waits for them, and re-layouts  30.6 us (10%)
  starting transfers between devices  24.4 us (8%)
  other arithmetic  16.2 us (5%)
  matrix products  10.4 us (3%)
    all_gather x1, waiting for transfers between devices, on_device(): lax.all_gather(pieces.reshape(STEPS * piece, term_cols), AX, axis=0, tile...  104 us
    all_to_all x5, waiting for transfers between devices, exchange(): lax.all_to_all(buf, name, split_axis=dim, concat_axis=dim, tiled=True)  59.2 us
    all_to_all x2, blocking collectives, exchange(): lax.all_to_all(buf, name, split_axis=dim, concat_axis=dim, tiled=True)  29.3 us
    all_to_all x5, starting transfers between devices, exchange(): lax.all_to_all(buf, name, split_axis=dim, concat_axis=dim, tiled=True)  24.4 us
    dot_general x1, matrix products, on_device(): lax.dot_general(flat_queries, stored, (((1,), (1,)), ((), ())), preferred...  10.4 us
    psum x1, blocking collectives, on_device(): doc_sq = lax.psum(partial_sq, RP)  10.3 us
    reshape x4, local copies, waits for them, and re-layouts, scatter_from_owner(): bufs = [c.reshape(nx, nz, ny, rows // (nx * nz * ny), terms) for c in cands]  9.55 us
  transfers between devices with their start and end apart: 6, of which 5 were waited for; matrix products, arithmetic and copies ran while one was open for 6% of the time, Pallas kernels for 0%

profile of v5, /device:TPU:32, one launch (start us, length us, event | category | flops | bytes accessed | tf_op | source)
XLA Modules:
  0.0 320.3 jit_solution(16881043758785304228)
XLA Ops:
  7.2 3.4 %copy.30 = bf16[64,8,32,128]{3,2,1,0:T(8,128)(2,1)S(1)} copy(bf16[64,8,32,128]{3,1,2,0:T(8,128)(2,1)} %bitcast.53) | data formatting | bytes 8388608
  11.0 2.7 fusion.7
  13.8 2.5 reshape.76
  16.3 2.2 copy.15
  18.5 4.5 %all-to-all-start = ((bf16[4,4,4,4,4096]{4,3,1,0,2:T(4,128)(2,1)}), bf16[4,4,4,4,4096]{4,3,1,0,2:T(4,128)(2,1)}, u32[]{:S(2)}, u32[]{:S(2)}) async-start(bf16[4,4,4,4,4096]{4,3,1,0,2:T(4,128)(2,1)} %copy.15), calls=%async_computation | async-start | bytes 4194304 | tf_op jit(solution)/shard_map/all_to_all | solution.py:22
  23.0 2.5 reshape.77
  25.6 2.2 copy.16
  27.8 21.9 %all-to-all-done = bf16[4,4,4,4,4096]{4,3,1,0,2:T(4,128)(2,1)} async-done(((bf16[4,4,4,4,4096]{4,3,1,0,2:T(4,128)(2,1)}), bf16[4,4,4,4,4096]{4,3,1,0,2:T(4,128)(2,1)}, u32[]{:S(2)}, u32[]{:S(2)}) %all-to-all-start) | async-done | bytes 2097184 | tf_op jit(solution)/shard_map/all_to_all | solution.py:22
  49.7 3.6 %all-to-all-start.1 = ((bf16[4,4,4,4,4096]{4,3,1,0,2:T(4,128)(2,1)}), bf16[4,4,4,4,4096]{4,3,1,0,2:T(4,128)(2,1)S(1)}, u32[]{:S(2)}, u32[]{:S(2)}) async-start(bf16[4,4,4,4,4096]{4,3,1,0,2:T(4,128)(2,1)} %copy.16), calls=%async_computation.1 | async-start | bytes 4194304 | tf_op jit(solution)/shard_map/all_to_all | solution.py:22
  61.7 1.6 dynamic-slice_bitcast_fusion.3
  63.4 15.6 %all-to-all-done.1 = bf16[4,4,4,4,4096]{4,3,1,0,2:T(4,128)(2,1)S(1)} async-done(((bf16[4,4,4,4,4096]{4,3,1,0,2:T(4,128)(2,1)}), bf16[4,4,4,4,4096]{4,3,1,0,2:T(4,128)(2,1)S(1)}, u32[]{:S(2)}, u32[]{:S(2)}) %all-to-all-start.1) | async-done | bytes 2097184 | tf_op jit(solution)/shard_map/all_to_all | solution.py:22
  79.4 2.9 pad_maximum_fusion
  82.3 4.3 %all-to-all-start.2 = ((bf16[4,4,4,1,4,4096]{5,4,2,3,0,1:T(4,128)(2,1)}), bf16[4,4,4,1,4,4096]{5,4,2,3,0,1:T(4,128)(2,1)S(1)}, u32[]{:S(2)}, u32[]{:S(2)}) async-start(bf16[4,4,4,1,4,4096]{5,4,2,3,0,1:T(4,128)(2,1)} %pad_maximum_fusion), calls=%async_computation.2 | async-start | bytes 4194304 | tf_op jit(solution)/shard_map/all_to_all | solution.py:22
  94.5 16.6 %all-to-all-done.2 = bf16[4,4,4,1,4,4096]{5,4,2,3,0,1:T(4,128)(2,1)S(1)} async-done(((bf16[4,4,4,1,4,4096]{5,4,2,3,0,1:T(4,128)(2,1)}), bf16[4,4,4,1,4,4096]{5,4,2,3,0,1:T(4,128)(2,1)S(1)}, u32[]{:S(2)}, u32[]{:S(2)}) %all-to-all-start.2) | async-done | bytes 2097184 | tf_op jit(solution)/shard_map/all_to_all | solution.py:22
  111.2 0.9 fusion.8
  112.8 1.0 copy.17
  113.8 7.6 %all-to-all-start.3 = ((bf16[4,1,4,1,4,4096]{5,4,1,3,0,2:T(4,128)(2,1)}), bf16[4,1,4,1,4,4096]{5,4,1,3,0,2:T(4,128)(2,1)S(1)}, u32[]{:S(2)}, u32[]{:S(2)}) async-start(bf16[4,1,4,1,4,4096]{5,4,1,3,0,2:T(4,128)(2,1)} %copy.17), calls=%async_computation.3 | async-start | bytes 1048576 | tf_op jit(solution)/shard_map/all_to_all | solution.py:22
  129.0 5.2 %all-to-all-done.3 = bf16[4,1,4,1,4,4096]{5,4,1,3,0,2:T(4,128)(2,1)S(1)} async-done(((bf16[4,1,4,1,4,4096]{5,4,1,3,0,2:T(4,128)(2,1)}), bf16[4,1,4,1,4,4096]{5,4,1,3,0,2:T(4,128)(2,1)S(1)}, u32[]{:S(2)}, u32[]{:S(2)}) %all-to-all-start.3) | async-done | bytes 524320 | tf_op jit(solution)/shard_map/all_to_all | solution.py:22
  136.0 1.6 copy-done
  137.5 3.7 %fusion.1 = (f32[512]{0:T(512)S(1)}, bf16[512,4096]{1,0:T(8,128)(2,1)}) fusion(bf16[512,4096]{1,0:T(8,128)(2,1)S(1)} %copy-done, bf16[64,8,32,128]{3,2,1,0:T(8,128)(2,1)S(1)} %bitcast.54), kind=kLoop, calls=%fused_computation.3 | loop fusion | flops 8388096 | bytes 12584960 | tf_op jit(solution)/shard_map/dt,dt->d/dot_general | solution.py:58
  141.3 103.5 %all-gather.2.cloned.1.call-done = bf16[1024,4096]{1,0:T(8,128)(2,1)} async-done(((bf16[16,4096]{1,0:T(8,128)(2,1)}), bf16[1024,4096]{1,0:T(8,128)(2,1)}) %all-gather.2.cloned.1.call-update) | async-done | bytes 8388624 | tf_op jit(solution)/shard_map/all_gather | solution.py:65
  244.8 10.4 %fusion.13 = f32[1024,512]{1,0:T(8,128)} fusion(bf16[1024,4096]{1,0:T(8,128)(2,1)} %all-gather.2.cloned.1.call-done, bf16[512,4096]{1,0:T(8,128)(2,1)} %get-tuple-element.8), kind=kOutput, calls=%fused_computation.48 | convolution fusion | flops 4294967296 | bytes 14680064 | tf_op jit(solution)/shard_map/dot_general | solution.py:70
  255.2 2.5 reshape.78
  257.7 1.2 copy.18
  258.9 5.4 %all_to_all.37 = f32[64,4,2,2,1,512]{5,2,1,0,4,3:T(2,128)S(1)} all-to-all(f32[64,4,2,2,1,512]{5,2,1,0,4,3:T(2,128)S(1)} %copy.18), channel_id=1, replica_groups=mesh['x'=4,'zh'=4,'y'=4,'zl'=2,'c'=2] {'c'}, dimensions={3} | all-to-all | bytes 4194304 | tf_op jit(solution)/shard_map/all_to_all | solution.py:22
  264.3 2.1 reduce_sum.22
  266.4 1.3 copy.19
  267.7 4.5 %all-to-all-start.5 = ((f32[64,4,2,1,512]{4,1,0,3,2:T(4,128)}), f32[64,4,2,1,512]{4,1,0,3,2:T(4,128)S(1)}, u32[]{:S(2)}, u32[]{:S(2)}) async-start(f32[64,4,2,1,512]{4,1,0,3,2:T(4,128)} %copy.19), calls=%async_computation.5 | async-start | bytes 2097152 | tf_op jit(solution)/shard_map/all_to_all | solution.py:22
  272.2 5.1 %fusion = f32[1024]{0:T(1024)S(1)} fusion(bf16[1024,4096]{1,0:T(8,128)(2,1)} %all-gather.2.cloned.1.call-done), kind=kLoop, calls=%fused_computation.1 | loop fusion | flops 12581888 | bytes 8392704 | tf_op jit(solution)/shard_map/qt,qt->q/dot_general | solution.py:66
  277.3 10.3 %all-reduce = (f32[512]{0:T(512)S(1)}, f32[1024]{0:T(1024)S(1)}) all-reduce(f32[512]{0:T(512)S(1)} %get-tuple-element.11, f32[1024]{0:T(1024)S(1)} %fusion), channel_id=1, replica_groups=mesh['x'=4,'zh'=4,'y'=4,'zl'=2,'c'=2] {'zl','c'}, use_global_device_ids=true, to_apply=%region_3.4 | all-reduce | flops 1536 | bytes 12288 | tf_op jit(solution)/shard_map/psum | solution.py:59
  288.8 23.9 %all_to_all.38 = bf16[64,4,1,512]{3,1,2,0:T(4,128)(2,1)S(1)} all-to-all(bf16[64,4,1,512]{3,1,2,0:T(4,128)(2,1)S(1)} %fusion.5), channel_id=1, replica_groups=mesh['x'=4,'zh'=4,'y'=4,'zl'=2,'c'=2] {'x','zh','y'}, dimensions={0} | all-to-all | bytes 524288 | tf_op jit(solution)/shard_map/all_to_all | solution.py:22
  312.7 0.7 copy.35
  (33 shorter events, 6.4 us)
Async XLA Ops:
  18.5 31.1 %all-to-all-start = ((bf16[4,4,4,4,4096]{4,3,1,0,2:T(4,128)(2,1)}), bf16[4,4,4,4,4096]{4,3,1,0,2:T(4,128)(2,1)}, u32[]{:S(2)}, u32[]{:S(2)}) async-start(bf16[4,4,4,4,4096]{4,3,1,0,2:T(4,128)(2,1)} %copy.15), calls=%async_computation | async-start | bytes 4194304 | tf_op jit(solution)/shard_map/all_to_all | solution.py:22
  27.8 25.5 %copy-start.1 = (s32[4]{0:T(128)S(1)}, s32[4]{0:T(128)}, u32[]{:S(2)}) copy-start(s32[4]{0:T(128)} %param.5) | copy-start | bytes 52
  49.7 29.3 %all-to-all-start.1 = ((bf16[4,4,4,4,4096]{4,3,1,0,2:T(4,128)(2,1)}), bf16[4,4,4,4,4096]{4,3,1,0,2:T(4,128)(2,1)S(1)}, u32[]{:S(2)}, u32[]{:S(2)}) async-start(bf16[4,4,4,4,4096]{4,3,1,0,2:T(4,128)(2,1)} %copy.16), calls=%async_computation.1 | async-start | bytes 4194304 | tf_op jit(solution)/shard_map/all_to_all | solution.py:22
  82.3 28.9 %all-to-all-start.2 = ((bf16[4,4,4,1,4,4096]{5,4,2,3,0,1:T(4,128)(2,1)}), bf16[4,4,4,1,4,4096]{5,4,2,3,0,1:T(4,128)(2,1)S(1)}, u32[]{:S(2)}, u32[]{:S(2)}) async-start(bf16[4,4,4,1,4,4096]{5,4,2,3,0,1:T(4,128)(2,1)} %pad_maximum_fusion), calls=%async_computation.2 | async-start | bytes 4194304 | tf_op jit(solution)/shard_map/all_to_all | solution.py:22
  113.8 20.4 %all-to-all-start.3 = ((bf16[4,1,4,1,4,4096]{5,4,1,3,0,2:T(4,128)(2,1)}), bf16[4,1,4,1,4,4096]{5,4,1,3,0,2:T(4,128)(2,1)S(1)}, u32[]{:S(2)}, u32[]{:S(2)}) async-start(bf16[4,1,4,1,4,4096]{5,4,1,3,0,2:T(4,128)(2,1)} %copy.17), calls=%async_computation.3 | async-start | bytes 1048576 | tf_op jit(solution)/shard_map/all_to_all | solution.py:22
  121.3 123.4 %all-gather.2.cloned.1.call-start = ((), (), s32[]{:S(2)}) async-start(), calls=%async_computation.7 | async-start | bytes 8519680 | tf_op jit(solution)/shard_map/all_gather | solution.py:65
  135.3 2.2 copy-start
  267.7 20.4 %all-to-all-start.5 = ((f32[64,4,2,1,512]{4,1,0,3,2:T(4,128)}), f32[64,4,2,1,512]{4,1,0,3,2:T(4,128)S(1)}, u32[]{:S(2)}, u32[]{:S(2)}) async-start(f32[64,4,2,1,512]{4,1,0,3,2:T(4,128)} %copy.19), calls=%async_computation.5 | async-start | bytes 2097152 | tf_op jit(solution)/shard_map/all_to_all | solution.py:22
Sparse Core Ops, SparseCore 0:
  135.4 109.2 all-gather.1

commit v6 on v5

--- a/solution.py
+++ b/solution.py
@@ -22,25 +22,23 @@
     return lax.all_to_all(buf, name, split_axis=dim, concat_axis=dim, tiled=True)
 
 
-def scatter_from_owner(cands, owners, sizes):
-    rows, terms = cands[0].shape
+def scatter_from_owner(blocks, block_of, owners, sizes):
+    rows, terms = blocks[0].shape
     nx, nz, ny = sizes
+    steps = len(block_of)
     coord = {"x": owners // (nz * ny), "zh": (owners // ny) % nz, "y": owners % ny}
-    bufs = [c.reshape(nx, nz, ny, rows // (nx * nz * ny), terms) for c in cands]
     dim = AX.index("y")
+    got = [exchange(blk.reshape(nx, nz, ny, rows // (nx * nz * ny), terms), "y", dim) for blk in blocks]
     buf = jnp.stack(
-        [
-            lax.dynamic_slice_in_dim(exchange(b, "y", dim), coord["y"][s], 1, axis=dim)
-            for s, b in enumerate(bufs)
-        ]
+        [lax.dynamic_slice_in_dim(got[block_of[s]], coord["y"][s], 1, axis=dim) for s in range(steps)]
     )
     for name in ("x", "zh"):
         dim = 1 + AX.index(name)
         got = exchange(buf, name, dim)
         buf = jnp.stack(
-            [lax.dynamic_slice_in_dim(got[s], coord[name][s], 1, axis=dim - 1) for s in range(len(cands))]
+            [lax.dynamic_slice_in_dim(got[s], coord[name][s], 1, axis=dim - 1) for s in range(steps)]
         )
-    return buf.reshape(len(cands), rows // (nx * nz * ny), terms)
+    return buf.reshape(steps, rows // (nx * nz * ny), terms)
 
 
 def on_device(docs, pattern, owners, sizes):
@@ -59,8 +57,9 @@
     doc_sq = lax.psum(partial_sq, RP)
     inverse = lax.rsqrt(doc_sq + EPSILON)
     sharpen = math.sqrt(TERMS) * 0.5
-    cands = [masked[(s % (doc_rows // QUERY)) * QUERY :][:QUERY] for s in range(STEPS)]
-    pieces = scatter_from_owner(cands, owners, sizes)
+    blocks = [masked[k * QUERY :][:QUERY] for k in range(doc_rows // QUERY)]
+    block_of = [s % (doc_rows // QUERY) for s in range(STEPS)]
+    pieces = scatter_from_owner(blocks, block_of, owners, sizes)
     piece = pieces.shape[1]
     flat_queries = lax.all_gather(pieces.reshape(STEPS * piece, term_cols), AX, axis=0, tiled=True)
     q_sq = jnp.einsum("qt,qt->q", flat_queries, flat_queries, preferred_element_type=jnp.float32)

time: 321 us -> 321 us (level)
  no operation moved by 1% of the time
where the time goes in v6:
time: 321 us; the launch traced here: 320 us
  waiting for transfers between devices  163 us (51%)
  blocking collectives  39.6 us (12%)
  between operations  36.3 us (11%)
  local copies, waits for them, and re-layouts  30.6 us (10%)
  starting transfers between devices  24.4 us (8%)
  other arithmetic  16.2 us (5%)
  matrix products  10.4 us (3%)
    all_gather x1, waiting for transfers between devices, on_device(): lax.all_gather(pieces.reshape(STEPS * piece, term_cols), AX, axis=0, tile...  104 us
    all_to_all x5, waiting for transfers between devices, exchange(): lax.all_to_all(buf, name, split_axis=dim, concat_axis=dim, tiled=True)  59.2 us
    all_to_all x2, blocking collectives, exchange(): lax.all_to_all(buf, name, split_axis=dim, concat_axis=dim, tiled=True)  29.3 us
    all_to_all x5, starting transfers between devices, exchange(): lax.all_to_all(buf, name, split_axis=dim, concat_axis=dim, tiled=True)  24.4 us
    dot_general x1, matrix products, on_device(): lax.dot_general(flat_queries, stored, (((1,), (1,)), ((), ())), preferred...  10.4 us
    psum x1, blocking collectives, on_device(): doc_sq = lax.psum(partial_sq, RP)  10.3 us
    reshape x4, local copies, waits for them, and re-layouts, scatter_from_owner(): blk.reshape(nx, nz, ny, rows // (nx * nz * ny), terms)  9.55 us
  transfers between devices with their start and end apart: 6, of which 5 were waited for; matrix products, arithmetic and copies ran while one was open for 6% of the time, Pallas kernels for 0%

profile of v6, /device:TPU:32, one launch (start us, length us, event | category | flops | bytes accessed | tf_op | source)
XLA Modules:
  0.0 320.3 jit_solution(16881043758785304228)
XLA Ops:
  7.2 3.4 %copy.30 = bf16[64,8,32,128]{3,2,1,0:T(8,128)(2,1)S(1)} copy(bf16[64,8,32,128]{3,1,2,0:T(8,128)(2,1)} %bitcast.53) | data formatting | bytes 8388608
  11.0 2.7 fusion.7
  13.8 2.5 reshape.74
  16.3 2.2 copy.15
  18.5 4.5 %all-to-all-start = ((bf16[4,4,4,4,4096]{4,3,1,0,2:T(4,128)(2,1)}), bf16[4,4,4,4,4096]{4,3,1,0,2:T(4,128)(2,1)}, u32[]{:S(2)}, u32[]{:S(2)}) async-start(bf16[4,4,4,4,4096]{4,3,1,0,2:T(4,128)(2,1)} %copy.15), calls=%async_computation | async-start | bytes 4194304 | tf_op jit(solution)/shard_map/all_to_all | solution.py:22
  23.0 2.5 reshape.75
  25.6 2.2 copy.16
  27.8 21.9 %all-to-all-done = bf16[4,4,4,4,4096]{4,3,1,0,2:T(4,128)(2,1)} async-done(((bf16[4,4,4,4,4096]{4,3,1,0,2:T(4,128)(2,1)}), bf16[4,4,4,4,4096]{4,3,1,0,2:T(4,128)(2,1)}, u32[]{:S(2)}, u32[]{:S(2)}) %all-to-all-start) | async-done | bytes 2097184 | tf_op jit(solution)/shard_map/all_to_all | solution.py:22
  49.7 3.6 %all-to-all-start.1 = ((bf16[4,4,4,4,4096]{4,3,1,0,2:T(4,128)(2,1)}), bf16[4,4,4,4,4096]{4,3,1,0,2:T(4,128)(2,1)S(1)}, u32[]{:S(2)}, u32[]{:S(2)}) async-start(bf16[4,4,4,4,4096]{4,3,1,0,2:T(4,128)(2,1)} %copy.16), calls=%async_computation.1 | async-start | bytes 4194304 | tf_op jit(solution)/shard_map/all_to_all | solution.py:22
  61.7 1.6 dynamic-slice_bitcast_fusion.3
  63.4 15.6 %all-to-all-done.1 = bf16[4,4,4,4,4096]{4,3,1,0,2:T(4,128)(2,1)S(1)} async-done(((bf16[4,4,4,4,4096]{4,3,1,0,2:T(4,128)(2,1)}), bf16[4,4,4,4,4096]{4,3,1,0,2:T(4,128)(2,1)S(1)}, u32[]{:S(2)}, u32[]{:S(2)}) %all-to-all-start.1) | async-done | bytes 2097184 | tf_op jit(solution)/shard_map/all_to_all | solution.py:22
  79.4 2.9 pad_maximum_fusion
  82.3 4.3 %all-to-all-start.2 = ((bf16[4,4,4,1,4,4096]{5,4,2,3,0,1:T(4,128)(2,1)}), bf16[4,4,4,1,4,4096]{5,4,2,3,0,1:T(4,128)(2,1)S(1)}, u32[]{:S(2)}, u32[]{:S(2)}) async-start(bf16[4,4,4,1,4,4096]{5,4,2,3,0,1:T(4,128)(2,1)} %pad_maximum_fusion), calls=%async_computation.2 | async-start | bytes 4194304 | tf_op jit(solution)/shard_map/all_to_all | solution.py:22
  94.5 16.6 %all-to-all-done.2 = bf16[4,4,4,1,4,4096]{5,4,2,3,0,1:T(4,128)(2,1)S(1)} async-done(((bf16[4,4,4,1,4,4096]{5,4,2,3,0,1:T(4,128)(2,1)}), bf16[4,4,4,1,4,4096]{5,4,2,3,0,1:T(4,128)(2,1)S(1)}, u32[]{:S(2)}, u32[]{:S(2)}) %all-to-all-start.2) | async-done | bytes 2097184 | tf_op jit(solution)/shard_map/all_to_all | solution.py:22
  111.2 0.9 fusion.8
  112.8 1.0 copy.17
  113.8 7.6 %all-to-all-start.3 = ((bf16[4,1,4,1,4,4096]{5,4,1,3,0,2:T(4,128)(2,1)}), bf16[4,1,4,1,4,4096]{5,4,1,3,0,2:T(4,128)(2,1)S(1)}, u32[]{:S(2)}, u32[]{:S(2)}) async-start(bf16[4,1,4,1,4,4096]{5,4,1,3,0,2:T(4,128)(2,1)} %copy.17), calls=%async_computation.3 | async-start | bytes 1048576 | tf_op jit(solution)/shard_map/all_to_all | solution.py:22
  129.0 5.2 %all-to-all-done.3 = bf16[4,1,4,1,4,4096]{5,4,1,3,0,2:T(4,128)(2,1)S(1)} async-done(((bf16[4,1,4,1,4,4096]{5,4,1,3,0,2:T(4,128)(2,1)}), bf16[4,1,4,1,4,4096]{5,4,1,3,0,2:T(4,128)(2,1)S(1)}, u32[]{:S(2)}, u32[]{:S(2)}) %all-to-all-start.3) | async-done | bytes 524320 | tf_op jit(solution)/shard_map/all_to_all | solution.py:22
  136.0 1.6 copy-done
  137.5 3.7 %fusion.1 = (f32[512]{0:T(512)S(1)}, bf16[512,4096]{1,0:T(8,128)(2,1)}) fusion(bf16[512,4096]{1,0:T(8,128)(2,1)S(1)} %copy-done, bf16[64,8,32,128]{3,2,1,0:T(8,128)(2,1)S(1)} %bitcast.54), kind=kLoop, calls=%fused_computation.3 | loop fusion | flops 8388096 | bytes 12584960 | tf_op jit(solution)/shard_map/dt,dt->d/dot_general | solution.py:56
  141.3 103.5 %all-gather.2.cloned.1.call-done = bf16[1024,4096]{1,0:T(8,128)(2,1)} async-done(((bf16[16,4096]{1,0:T(8,128)(2,1)}), bf16[1024,4096]{1,0:T(8,128)(2,1)}) %all-gather.2.cloned.1.call-update) | async-done | bytes 8388624 | tf_op jit(solution)/shard_map/all_gather | solution.py:64
  244.8 10.4 %fusion.13 = f32[1024,512]{1,0:T(8,128)} fusion(bf16[1024,4096]{1,0:T(8,128)(2,1)} %all-gather.2.cloned.1.call-done, bf16[512,4096]{1,0:T(8,128)(2,1)} %get-tuple-element.8), kind=kOutput, calls=%fused_computation.48 | convolution fusion | flops 4294967296 | bytes 14680064 | tf_op jit(solution)/shard_map/dot_general | solution.py:69
  255.2 2.5 reshape.76
  257.7 1.2 copy.18
  258.9 5.4 %all_to_all.35 = f32[64,4,2,2,1,512]{5,2,1,0,4,3:T(2,128)S(1)} all-to-all(f32[64,4,2,2,1,512]{5,2,1,0,4,3:T(2,128)S(1)} %copy.18), channel_id=1, replica_groups=mesh['x'=4,'zh'=4,'y'=4,'zl'=2,'c'=2] {'c'}, dimensions={3} | all-to-all | bytes 4194304 | tf_op jit(solution)/shard_map/all_to_all | solution.py:22
  264.3 2.1 reduce_sum.22
  266.4 1.3 copy.19
  267.7 4.5 %all-to-all-start.5 = ((f32[64,4,2,1,512]{4,1,0,3,2:T(4,128)}), f32[64,4,2,1,512]{4,1,0,3,2:T(4,128)S(1)}, u32[]{:S(2)}, u32[]{:S(2)}) async-start(f32[64,4,2,1,512]{4,1,0,3,2:T(4,128)} %copy.19), calls=%async_computation.5 | async-start | bytes 2097152 | tf_op jit(solution)/shard_map/all_to_all | solution.py:22
  272.2 5.1 %fusion = f32[1024]{0:T(1024)S(1)} fusion(bf16[1024,4096]{1,0:T(8,128)(2,1)} %all-gather.2.cloned.1.call-done), kind=kLoop, calls=%fused_computation.1 | loop fusion | flops 12581888 | bytes 8392704 | tf_op jit(solution)/shard_map/qt,qt->q/dot_general | solution.py:65
  277.3 10.3 %all-reduce = (f32[512]{0:T(512)S(1)}, f32[1024]{0:T(1024)S(1)}) all-reduce(f32[512]{0:T(512)S(1)} %get-tuple-element.11, f32[1024]{0:T(1024)S(1)} %fusion), channel_id=1, replica_groups=mesh['x'=4,'zh'=4,'y'=4,'zl'=2,'c'=2] {'zl','c'}, use_global_device_ids=true, to_apply=%region_3.4 | all-reduce | flops 1536 | bytes 12288 | tf_op jit(solution)/shard_map/psum | solution.py:57
  288.8 23.9 %all_to_all.36 = bf16[64,4,1,512]{3,1,2,0:T(4,128)(2,1)S(1)} all-to-all(bf16[64,4,1,512]{3,1,2,0:T(4,128)(2,1)S(1)} %fusion.5), channel_id=1, replica_groups=mesh['x'=4,'zh'=4,'y'=4,'zl'=2,'c'=2] {'x','zh','y'}, dimensions={0} | all-to-all | bytes 524288 | tf_op jit(solution)/shard_map/all_to_all | solution.py:22
  312.7 0.7 copy.35
  (33 shorter events, 6.4 us)
Async XLA Ops:
  18.5 31.1 %all-to-all-start = ((bf16[4,4,4,4,4096]{4,3,1,0,2:T(4,128)(2,1)}), bf16[4,4,4,4,4096]{4,3,1,0,2:T(4,128)(2,1)}, u32[]{:S(2)}, u32[]{:S(2)}) async-start(bf16[4,4,4,4,4096]{4,3,1,0,2:T(4,128)(2,1)} %copy.15), calls=%async_computation | async-start | bytes 4194304 | tf_op jit(solution)/shard_map/all_to_all | solution.py:22
  27.8 25.5 %copy-start.1 = (s32[4]{0:T(128)S(1)}, s32[4]{0:T(128)}, u32[]{:S(2)}) copy-start(s32[4]{0:T(128)} %param.5) | copy-start | bytes 52
  49.7 29.3 %all-to-all-start.1 = ((bf16[4,4,4,4,4096]{4,3,1,0,2:T(4,128)(2,1)}), bf16[4,4,4,4,4096]{4,3,1,0,2:T(4,128)(2,1)S(1)}, u32[]{:S(2)}, u32[]{:S(2)}) async-start(bf16[4,4,4,4,4096]{4,3,1,0,2:T(4,128)(2,1)} %copy.16), calls=%async_computation.1 | async-start | bytes 4194304 | tf_op jit(solution)/shard_map/all_to_all | solution.py:22
  82.3 28.9 %all-to-all-start.2 = ((bf16[4,4,4,1,4,4096]{5,4,2,3,0,1:T(4,128)(2,1)}), bf16[4,4,4,1,4,4096]{5,4,2,3,0,1:T(4,128)(2,1)S(1)}, u32[]{:S(2)}, u32[]{:S(2)}) async-start(bf16[4,4,4,1,4,4096]{5,4,2,3,0,1:T(4,128)(2,1)} %pad_maximum_fusion), calls=%async_computation.2 | async-start | bytes 4194304 | tf_op jit(solution)/shard_map/all_to_all | solution.py:22
  113.8 20.4 %all-to-all-start.3 = ((bf16[4,1,4,1,4,4096]{5,4,1,3,0,2:T(4,128)(2,1)}), bf16[4,1,4,1,4,4096]{5,4,1,3,0,2:T(4,128)(2,1)S(1)}, u32[]{:S(2)}, u32[]{:S(2)}) async-start(bf16[4,1,4,1,4,4096]{5,4,1,3,0,2:T(4,128)(2,1)} %copy.17), calls=%async_computation.3 | async-start | bytes 1048576 | tf_op jit(solution)/shard_map/all_to_all | solution.py:22
  121.3 123.4 %all-gather.2.cloned.1.call-start = ((), (), s32[]{:S(2)}) async-start(), calls=%async_computation.7 | async-start | bytes 8519680 | tf_op jit(solution)/shard_map/all_gather | solution.py:64
  135.3 2.2 copy-start
  267.7 20.4 %all-to-all-start.5 = ((f32[64,4,2,1,512]{4,1,0,3,2:T(4,128)}), f32[64,4,2,1,512]{4,1,0,3,2:T(4,128)S(1)}, u32[]{:S(2)}, u32[]{:S(2)}) async-start(f32[64,4,2,1,512]{4,1,0,3,2:T(4,128)} %copy.19), calls=%async_computation.5 | async-start | bytes 2097152 | tf_op jit(solution)/shard_map/all_to_all | solution.py:22
Sparse Core Ops, SparseCore 0:
  135.4 109.2 all-gather.1

commit v7 on v6

--- a/solution.py
+++ b/solution.py
@@ -54,8 +54,6 @@
         * weights[:, None, :, None]
     ).reshape(doc_rows, term_cols)
     partial_sq = jnp.einsum("dt,dt->d", masked, masked, preferred_element_type=jnp.float32)
-    doc_sq = lax.psum(partial_sq, RP)
-    inverse = lax.rsqrt(doc_sq + EPSILON)
     sharpen = math.sqrt(TERMS) * 0.5
     blocks = [masked[k * QUERY :][:QUERY] for k in range(doc_rows // QUERY)]
     block_of = [s % (doc_rows // QUERY) for s in range(STEPS)]
@@ -63,16 +61,22 @@
     piece = pieces.shape[1]
     flat_queries = lax.all_gather(pieces.reshape(STEPS * piece, term_cols), AX, axis=0, tiled=True)
     q_sq = jnp.einsum("qt,qt->q", flat_queries, flat_queries, preferred_element_type=jnp.float32)
-    q_inv = lax.rsqrt(lax.psum(q_sq, RP) + EPSILON).reshape(n_shard, STEPS, piece)
     flat_queries, stored = lax.optimization_barrier((flat_queries, masked))
     similar = lax.optimization_barrier(
         lax.dot_general(flat_queries, stored, (((1,), (1,)), ((), ())), preferred_element_type=jnp.float32)
     )
     row_share = piece // n_rep
-    similar = similar.reshape(n_shard, STEPS, 2, 2, row_share, doc_rows)
+    block = (n_shard, STEPS, 2, 2, row_share)
+    similar = jnp.concatenate([similar.reshape(*block, doc_rows), q_sq.reshape(*block, 1)], axis=-1)
+    doc_row = jnp.broadcast_to(
+        jnp.concatenate([partial_sq, jnp.zeros((1,), jnp.float32)]), (1, *block[1:], doc_rows + 1)
+    )
+    similar = jnp.concatenate([similar, doc_row], axis=0)
     similar = jnp.sum(exchange(similar, "c", 3), axis=3)
-    mine = jnp.sum(exchange(similar, "zl", 2), axis=2)
-    my_inv = lax.dynamic_slice_in_dim(q_inv, rep_index * row_share, row_share, axis=2)
+    total = jnp.sum(exchange(similar, "zl", 2), axis=2)
+    mine = total[:n_shard, :, :, :doc_rows]
+    inverse = lax.rsqrt(total[n_shard, 0, 0, :doc_rows] + EPSILON)
+    my_inv = lax.rsqrt(total[:n_shard, :, :, doc_rows] + EPSILON)
     scaled = mine * my_inv[..., None] * inverse[None, None, None, :] * sharpen
     scores = jnp.clip(scaled, -CLIP_LEVEL, CLIP_LEVEL).astype(jnp.bfloat16)
     got = exchange(scores, AX, 0)

time: 321 us -> 342 us (1.065)
  blocking collectives: 39.6 us -> 48.9 us
  other arithmetic: 16.2 us -> 24.8 us
  local copies, waits for them, and re-layouts: 30.6 us -> 36.9 us
  starting transfers between devices: 24.4 us -> 19.9 us
    all_to_all x2 -> x3, blocking collectives: 29.3 us -> 48.9 us  [exchange(): lax.all_to_all(buf, name, split_axis=dim, concat_axis=dim, tiled=True)]
    psum x1 -> x0, blocking collectives: 10.3 us -> none  [on_device(): doc_sq = lax.psum(partial_sq, RP)]
    reshape x3 -> x4, local copies, waits for them, and re-layouts: 3.86 us -> 8.85 us  [the longest x2 5.09 us: on_device(): similar.reshape(*block, doc_rows)]
    all_to_all x5 -> x4, starting transfers between devices: 24.4 us -> 19.9 us  [exchange(): lax.all_to_all(buf, name, split_axis=dim, concat_axis=dim, tiled=True)]
    rsqrt x2 -> x1, other arithmetic: 0.02 us -> 4.02 us  [on_device(): inverse = lax.rsqrt(total[n_shard, 0, 0, :doc_rows] + EPSILON)]
    all_to_all x5 -> x4, waiting for transfers between devices: 59.2 us -> 59.4 us  [exchange(): lax.all_to_all(buf, name, split_axis=dim, concat_axis=dim, tiled=True)]
  transfers between devices with their start and end apart: 6 -> 5, of which waited for: 5 -> 5; matrix products, arithmetic and copies ran while one was open for 6% -> 4% of each run, Pallas kernels for 0% -> 0%
where the time goes in v7:
time: 342 us; the launch traced here: 340 us
  waiting for transfers between devices  163 us (48%)
  blocking collectives  48.9 us (14%)
  local copies, waits for them, and re-layouts  36.9 us (11%)
  between operations  36.3 us (11%)
  other arithmetic  24.8 us (7%)
  starting transfers between devices  19.9 us (6%)
  matrix products  10.4 us (3%)
    all_gather x1, waiting for transfers between devices, on_device(): lax.all_gather(pieces.reshape(STEPS * piece, term_cols), AX, axis=0, tile...  104 us
    all_to_all x4, waiting for transfers between devices, exchange(): lax.all_to_all(buf, name, split_axis=dim, concat_axis=dim, tiled=True)  59.4 us
    all_to_all x3, blocking collectives, exchange(): lax.all_to_all(buf, name, split_axis=dim, concat_axis=dim, tiled=True)  48.9 us
    all_to_all x4, starting transfers between devices, exchange(): lax.all_to_all(buf, name, split_axis=dim, concat_axis=dim, tiled=True)  19.9 us
    dot_general x1, matrix products, on_device(): lax.dot_general(flat_queries, stored, (((1,), (1,)), ((), ())), preferred...  10.4 us
    reshape x4, local copies, waits for them, and re-layouts, scatter_from_owner(): blk.reshape(nx, nz, ny, rows // (nx * nz * ny), terms)  9.53 us
  transfers between devices with their start and end apart: 5, of which 5 were waited for; matrix products, arithmetic and copies ran while one was open for 4% of the time, Pallas kernels for 0%

profile of v7, /device:TPU:32, one launch (start us, length us, event | category | flops | bytes accessed | tf_op | source)
XLA Modules:
  0.0 340.0 jit_solution(1408469145700169208)
XLA Ops:
  7.2 3.4 %copy.53 = bf16[64,8,32,128]{3,2,1,0:T(8,128)(2,1)S(1)} copy(bf16[64,8,32,128]{3,1,2,0:T(8,128)(2,1)} %bitcast.45) | data formatting | bytes 8388608
  11.0 2.7 fusion.11
  13.7 2.5 reshape.52
  16.3 2.2 copy.37
  18.5 4.5 %all-to-all-start = ((bf16[4,4,4,4,4096]{4,3,1,0,2:T(4,128)(2,1)}), bf16[4,4,4,4,4096]{4,3,1,0,2:T(4,128)(2,1)}, u32[]{:S(2)}, u32[]{:S(2)}) async-start(bf16[4,4,4,4,4096]{4,3,1,0,2:T(4,128)(2,1)} %copy.37), calls=%async_computation | async-start | bytes 4194304 | tf_op jit(solution)/shard_map/all_to_all | solution.py:22
  23.0 2.5 reshape.53
  25.5 2.2 copy.38
  27.8 21.9 %all-to-all-done = bf16[4,4,4,4,4096]{4,3,1,0,2:T(4,128)(2,1)} async-done(((bf16[4,4,4,4,4096]{4,3,1,0,2:T(4,128)(2,1)}), bf16[4,4,4,4,4096]{4,3,1,0,2:T(4,128)(2,1)}, u32[]{:S(2)}, u32[]{:S(2)}) %all-to-all-start) | async-done | bytes 2097184 | tf_op jit(solution)/shard_map/all_to_all | solution.py:22
  49.7 3.6 %all-to-all-start.1 = ((bf16[4,4,4,4,4096]{4,3,1,0,2:T(4,128)(2,1)}), bf16[4,4,4,4,4096]{4,3,1,0,2:T(4,128)(2,1)S(1)}, u32[]{:S(2)}, u32[]{:S(2)}) async-start(bf16[4,4,4,4,4096]{4,3,1,0,2:T(4,128)(2,1)} %copy.38), calls=%async_computation.1 | async-start | bytes 4194304 | tf_op jit(solution)/shard_map/all_to_all | solution.py:22
  61.5 1.6 dynamic-slice_bitcast_fusion.3
  63.1 15.9 %all-to-all-done.1 = bf16[4,4,4,4,4096]{4,3,1,0,2:T(4,128)(2,1)S(1)} async-done(((bf16[4,4,4,4,4096]{4,3,1,0,2:T(4,128)(2,1)}), bf16[4,4,4,4,4096]{4,3,1,0,2:T(4,128)(2,1)S(1)}, u32[]{:S(2)}, u32[]{:S(2)}) %all-to-all-start.1) | async-done | bytes 2097184 | tf_op jit(solution)/shard_map/all_to_all | solution.py:22
  79.4 2.9 pad_maximum_fusion.1
  82.3 4.3 %all-to-all-start.2 = ((bf16[4,4,4,1,4,4096]{5,4,2,3,0,1:T(4,128)(2,1)}), bf16[4,4,4,1,4,4096]{5,4,2,3,0,1:T(4,128)(2,1)S(1)}, u32[]{:S(2)}, u32[]{:S(2)}) async-start(bf16[4,4,4,1,4,4096]{5,4,2,3,0,1:T(4,128)(2,1)} %pad_maximum_fusion.1), calls=%async_computation.2 | async-start | bytes 4194304 | tf_op jit(solution)/shard_map/all_to_all | solution.py:22
  94.7 16.5 %all-to-all-done.2 = bf16[4,4,4,1,4,4096]{5,4,2,3,0,1:T(4,128)(2,1)S(1)} async-done(((bf16[4,4,4,1,4,4096]{5,4,2,3,0,1:T(4,128)(2,1)}), bf16[4,4,4,1,4,4096]{5,4,2,3,0,1:T(4,128)(2,1)S(1)}, u32[]{:S(2)}, u32[]{:S(2)}) %all-to-all-start.2) | async-done | bytes 2097184 | tf_op jit(solution)/shard_map/all_to_all | solution.py:22
  113.8 7.6 %all-to-all-start.3 = ((bf16[4,1,4,1,4,4096]{5,4,1,3,0,2:T(4,128)(2,1)}), bf16[4,1,4,1,4,4096]{5,4,1,3,0,2:T(4,128)(2,1)S(1)}, u32[]{:S(2)}, u32[]{:S(2)}) async-start(bf16[4,1,4,1,4,4096]{5,4,1,3,0,2:T(4,128)(2,1)} %copy.39), calls=%async_computation.3 | async-start | bytes 1048576 | tf_op jit(solution)/shard_map/all_to_all | solution.py:22
  129.1 5.1 %all-to-all-done.3 = bf16[4,1,4,1,4,4096]{5,4,1,3,0,2:T(4,128)(2,1)S(1)} async-done(((bf16[4,1,4,1,4,4096]{5,4,1,3,0,2:T(4,128)(2,1)}), bf16[4,1,4,1,4,4096]{5,4,1,3,0,2:T(4,128)(2,1)S(1)}, u32[]{:S(2)}, u32[]{:S(2)}) %all-to-all-start.3) | async-done | bytes 524320 | tf_op jit(solution)/shard_map/all_to_all | solution.py:22
  136.0 1.6 copy-done
  137.6 3.7 %fusion.1 = (f32[512]{0:T(512)S(1)}, bf16[512,4096]{1,0:T(8,128)(2,1)}) fusion(bf16[512,4096]{1,0:T(8,128)(2,1)S(1)} %copy-done, bf16[64,8,32,128]{3,2,1,0:T(8,128)(2,1)S(1)} %bitcast.46), kind=kLoop, calls=%fused_computation.3 | loop fusion | flops 8388096 | bytes 12584960 | tf_op jit(solution)/shard_map/dt,dt->d/dot_general | solution.py:56
  141.3 103.5 %all-gather.2.cloned.1.call-done = bf16[1024,4096]{1,0:T(8,128)(2,1)} async-done(((bf16[16,4096]{1,0:T(8,128)(2,1)}), bf16[1024,4096]{1,0:T(8,128)(2,1)}) %all-gather.2.cloned.1.call-update) | async-done | bytes 8388624 | tf_op jit(solution)/shard_map/all_gather | solution.py:62
  244.8 10.4 %fusion.17 = f32[1024,512]{1,0:T(8,128)} fusion(bf16[1024,4096]{1,0:T(8,128)(2,1)} %all-gather.2.cloned.1.call-done, bf16[512,4096]{1,0:T(8,128)(2,1)} %get-tuple-element.8), kind=kOutput, calls=%fused_computation.53 | convolution fusion | flops 4294967296 | bytes 14680064 | tf_op jit(solution)/shard_map/dot_general | solution.py:66
  255.2 2.5 reshape.54
  257.7 2.6 copy.40
  260.3 5.2 %fusion = f32[1024]{0:T(1024)S(1)} fusion(bf16[1024,4096]{1,0:T(8,128)(2,1)} %all-gather.2.cloned.1.call-done), kind=kLoop, calls=%fused_computation.1 | loop fusion | flops 12581888 | bytes 8392704 | tf_op jit(solution)/shard_map/qt,qt->q/dot_general | solution.py:63
  266.0 3.4 copy.41
  269.3 1.3 pad_maximum_fusion
  270.7 5.9 %all_to_all.35 = f32[65,4,2,2,1,513]{5,2,1,0,4,3:T(2,128)S(1)} all-to-all(f32[65,4,2,2,1,513]{5,2,1,0,4,3:T(2,128)S(1)} %pad_maximum_fusion), channel_id=1, replica_groups=mesh['x'=4,'zh'=4,'y'=4,'zl'=2,'c'=2] {'c'}, dimensions={3} | all-to-all | bytes 4268160 | tf_op jit(solution)/shard_map/all_to_all | solution.py:22
  276.6 3.7 %reduce_sum.22 = f32[65,4,2,513]{3,2,1,0:T(2,128)} reduce(f32[65,4,2,2,1,513]{5,2,1,0,4,3:T(2,128)S(1)} %all_to_all.35, f32[]{:T(128)} %constant.61.clone.1), dimensions={3,4}, to_apply=%region_0.1 | reduce | flops 266760 | bytes 3201124 | tf_op jit(solution)/shard_map/reduce_sum | solution.py:75
  280.3 1.7 copy.42
  281.9 19.0 %all_to_all.36 = f32[65,4,2,1,513]{4,1,0,3,2:T(4,128)S(1)} all-to-all(f32[65,4,2,1,513]{4,1,0,3,2:T(4,128)S(1)} %copy.42), channel_id=1, replica_groups=mesh['x'=4,'zh'=4,'y'=4,'zl'=2,'c'=2] {'zl'}, dimensions={2} | all-to-all | bytes 2134080 | tf_op jit(solution)/shard_map/all_to_all | solution.py:22
  302.5 4.0 %fusion.7 = f32[512]{0:T(512)S(1)} fusion(f32[65,4,1,513]{0,1,3,2:T(4,128)S(1)} %bitcast.49), kind=kLoop, calls=%fused_computation.20 | loop fusion | flops 512 | bytes 4096 | tf_op jit(solution)/shard_map/rsqrt | solution.py:78
  306.5 1.5 fusion.5
  308.4 24.0 %all_to_all.37 = bf16[64,4,1,512]{3,1,2,0:T(4,128)(2,1)S(1)} all-to-all(bf16[64,4,1,512]{3,1,2,0:T(4,128)(2,1)S(1)} %copy.44), channel_id=1, replica_groups=mesh['x'=4,'zh'=4,'y'=4,'zl'=2,'c'=2] {'x','zh','y'}, dimensions={0} | all-to-all | bytes 524288 | tf_op jit(solution)/shard_map/all_to_all | solution.py:22
  (36 shorter events, 10.2 us)
Async XLA Ops:
  18.5 31.1 %all-to-all-start = ((bf16[4,4,4,4,4096]{4,3,1,0,2:T(4,128)(2,1)}), bf16[4,4,4,4,4096]{4,3,1,0,2:T(4,128)(2,1)}, u32[]{:S(2)}, u32[]{:S(2)}) async-start(bf16[4,4,4,4,4096]{4,3,1,0,2:T(4,128)(2,1)} %copy.37), calls=%async_computation | async-start | bytes 4194304 | tf_op jit(solution)/shard_map/all_to_all | solution.py:22
  27.8 25.5 %copy-start.2 = (s32[4]{0:T(128)S(1)}, s32[4]{0:T(128)}, u32[]{:S(2)}) copy-start(s32[4]{0:T(128)} %param.5) | copy-start | bytes 52
  49.7 29.3 %all-to-all-start.1 = ((bf16[4,4,4,4,4096]{4,3,1,0,2:T(4,128)(2,1)}), bf16[4,4,4,4,4096]{4,3,1,0,2:T(4,128)(2,1)S(1)}, u32[]{:S(2)}, u32[]{:S(2)}) async-start(bf16[4,4,4,4,4096]{4,3,1,0,2:T(4,128)(2,1)} %copy.38), calls=%async_computation.1 | async-start | bytes 4194304 | tf_op jit(solution)/shard_map/all_to_all | solution.py:22
  82.3 28.9 %all-to-all-start.2 = ((bf16[4,4,4,1,4,4096]{5,4,2,3,0,1:T(4,128)(2,1)}), bf16[4,4,4,1,4,4096]{5,4,2,3,0,1:T(4,128)(2,1)S(1)}, u32[]{:S(2)}, u32[]{:S(2)}) async-start(bf16[4,4,4,1,4,4096]{5,4,2,3,0,1:T(4,128)(2,1)} %pad_maximum_fusion.1), calls=%async_computation.2 | async-start | bytes 4194304 | tf_op jit(solution)/shard_map/all_to_all | solution.py:22
  113.8 20.4 %all-to-all-start.3 = ((bf16[4,1,4,1,4,4096]{5,4,1,3,0,2:T(4,128)(2,1)}), bf16[4,1,4,1,4,4096]{5,4,1,3,0,2:T(4,128)(2,1)S(1)}, u32[]{:S(2)}, u32[]{:S(2)}) async-start(bf16[4,1,4,1,4,4096]{5,4,1,3,0,2:T(4,128)(2,1)} %copy.39), calls=%async_computation.3 | async-start | bytes 1048576 | tf_op jit(solution)/shard_map/all_to_all | solution.py:22
  121.4 123.4 %all-gather.2.cloned.1.call-start = ((), (), s32[]{:S(2)}) async-start(), calls=%async_computation.7 | async-start | bytes 8519680 | tf_op jit(solution)/shard_map/all_gather | solution.py:62
  135.4 2.2 copy-start
  260.3 9.0 %copy-start.1 = (f32[64,4,2,2,1,512]{5,2,1,0,4,3:T(2,128)S(1)}, f32[64,4,2,2,1,512]{5,2,1,0,4,3:T(2,128)}, u32[]{:S(2)}) copy-start(f32[64,4,2,2,1,512]{5,2,1,0,4,3:T(2,128)} %copy.40) | copy-start | bytes 6291460
Sparse Core Ops, SparseCore 0:
  135.5 109.2 all-gather.1

commit v8 on v6

--- a/solution.py
+++ b/solution.py
@@ -32,13 +32,9 @@
     buf = jnp.stack(
         [lax.dynamic_slice_in_dim(got[block_of[s]], coord["y"][s], 1, axis=dim) for s in range(steps)]
     )
-    for name in ("x", "zh"):
-        dim = 1 + AX.index(name)
-        got = exchange(buf, name, dim)
-        buf = jnp.stack(
-            [lax.dynamic_slice_in_dim(got[s], coord[name][s], 1, axis=dim - 1) for s in range(steps)]
-        )
-    return buf.reshape(steps, rows // (nx * nz * ny), terms)
+    plane = coord["x"] * nz + coord["zh"]
+    got = exchange(buf.reshape(steps, nx * nz, rows // (nx * nz * ny), terms), ("x", "zh"), 1)
+    return jnp.stack([lax.dynamic_index_in_dim(got[s], plane[s], 0, keepdims=False) for s in range(steps)])
 
 
 def on_device(docs, pattern, owners, sizes):

time: 321 us -> 330 us (1.028)
  waiting for transfers between devices: 163 us -> 183 us
  between operations: 36.3 us -> 28.6 us
    all_to_all x5 -> x4, waiting for transfers between devices: 59.2 us -> 80.8 us  [exchange(): lax.all_to_all(buf, name, split_axis=dim, concat_axis=dim, tiled=True)]
    another operation x4 -> x0, local copies, waits for them, and re-layouts: 3.73 us -> none  [the longest x2 2.04 us: scatter_from_owner(): jnp.stack([lax.dynamic_slice_in_dim(got[block_of[s]], coord['y'][s], 1, a...]
    all_to_all x5 -> x4, starting transfers between devices: 24.4 us -> 22.7 us  [exchange(): lax.all_to_all(buf, name, split_axis=dim, concat_axis=dim, tiled=True)]
  transfers between devices with their start and end apart: 6 -> 5, of which waited for: 5 -> 4; matrix products, arithmetic and copies ran while one was open for 6% -> 5% of each run, Pallas kernels for 0% -> 0%
where the time goes in v8:
time: 330 us; the launch traced here: 329 us
  waiting for transfers between devices  183 us (55%)
  blocking collectives  39.6 us (12%)
  between operations  28.6 us (9%)
  local copies, waits for them, and re-layouts  28.5 us (9%)
  starting transfers between devices  22.9 us (7%)
  other arithmetic  15.5 us (5%)
  matrix products  10.4 us (3%)
    all_gather x1, waiting for transfers between devices, on_device(): lax.all_gather(pieces.reshape(STEPS * piece, term_cols), AX, axis=0, tile...  102 us
    all_to_all x4, waiting for transfers between devices, exchange(): lax.all_to_all(buf, name, split_axis=dim, concat_axis=dim, tiled=True)  80.8 us
    all_to_all x2, blocking collectives, exchange(): lax.all_to_all(buf, name, split_axis=dim, concat_axis=dim, tiled=True)  29.3 us
    all_to_all x4, starting transfers between devices, exchange(): lax.all_to_all(buf, name, split_axis=dim, concat_axis=dim, tiled=True)  22.7 us
    dot_general x1, matrix products, on_device(): lax.dot_general(flat_queries, stored, (((1,), (1,)), ((), ())), preferred...  10.4 us
    psum x1, blocking collectives, on_device(): doc_sq = lax.psum(partial_sq, RP)  10.3 us
    reshape x4, local copies, waits for them, and re-layouts, scatter_from_owner(): blk.reshape(nx, nz, ny, rows // (nx * nz * ny), terms)  9.53 us
  transfers between devices with their start and end apart: 5, of which 4 were waited for; matrix products, arithmetic and copies ran while one was open for 5% of the time, Pallas kernels for 0%

profile of v8, /device:TPU:32, one launch (start us, length us, event | category | flops | bytes accessed | tf_op | source)
XLA Modules:
  0.0 328.6 jit_solution(13059116436190043438)
XLA Ops:
  6.5 0.7 convert_element_type.14
  7.2 3.4 %copy.27 = bf16[64,8,32,128]{3,2,1,0:T(8,128)(2,1)S(1)} copy(bf16[64,8,32,128]{3,1,2,0:T(8,128)(2,1)} %bitcast.51) | data formatting | bytes 8388608
  11.0 2.7 fusion.8
  13.8 2.5 reshape.74
  16.3 2.2 copy.13
  18.5 4.5 %all-to-all-start = ((bf16[4,4,4,4,4096]{4,3,1,0,2:T(4,128)(2,1)}), bf16[4,4,4,4,4096]{4,3,1,0,2:T(4,128)(2,1)}, u32[]{:S(2)}, u32[]{:S(2)}) async-start(bf16[4,4,4,4,4096]{4,3,1,0,2:T(4,128)(2,1)} %copy.13), calls=%async_computation | async-start | bytes 4194304 | tf_op jit(solution)/shard_map/all_to_all | solution.py:22
  23.0 2.5 reshape.75
  25.5 2.2 copy.14
  27.8 21.9 %all-to-all-done = bf16[4,4,4,4,4096]{4,3,1,0,2:T(4,128)(2,1)} async-done(((bf16[4,4,4,4,4096]{4,3,1,0,2:T(4,128)(2,1)}), bf16[4,4,4,4,4096]{4,3,1,0,2:T(4,128)(2,1)}, u32[]{:S(2)}, u32[]{:S(2)}) %all-to-all-start) | async-done | bytes 2097184 | tf_op jit(solution)/shard_map/all_to_all | solution.py:22
  49.6 3.6 %all-to-all-start.1 = ((bf16[4,4,4,4,4096]{4,3,1,0,2:T(4,128)(2,1)}), bf16[4,4,4,4,4096]{4,3,1,0,2:T(4,128)(2,1)S(1)}, u32[]{:S(2)}, u32[]{:S(2)}) async-start(bf16[4,4,4,4,4096]{4,3,1,0,2:T(4,128)(2,1)} %copy.14), calls=%async_computation.1 | async-start | bytes 4194304 | tf_op jit(solution)/shard_map/all_to_all | solution.py:22
  53.3 0.7 fusion.10
  61.4 1.6 constant_dynamic-slice_fusion.4
  63.1 15.8 %all-to-all-done.1 = bf16[4,4,4,4,4096]{4,3,1,0,2:T(4,128)(2,1)S(1)} async-done(((bf16[4,4,4,4,4096]{4,3,1,0,2:T(4,128)(2,1)}), bf16[4,4,4,4,4096]{4,3,1,0,2:T(4,128)(2,1)S(1)}, u32[]{:S(2)}, u32[]{:S(2)}) %all-to-all-start.1) | async-done | bytes 2097184 | tf_op jit(solution)/shard_map/all_to_all | solution.py:22
  79.3 2.8 pad_maximum_fusion
  82.1 10.1 %all-to-all-start.2 = ((bf16[4,16,4,4096]{3,2,0,1:T(4,128)(2,1)}), bf16[4,16,4,4096]{3,2,0,1:T(4,128)(2,1)S(1)}, u32[]{:S(2)}, u32[]{:S(2)}) async-start(bf16[4,16,4,4096]{3,2,0,1:T(4,128)(2,1)} %pad_maximum_fusion), calls=%async_computation.2 | async-start | bytes 4194304 | tf_op jit(solution)/shard_map/all_to_all | solution.py:22
  100.0 43.1 %all-to-all-done.2 = bf16[4,16,4,4096]{3,2,0,1:T(4,128)(2,1)S(1)} async-done(((bf16[4,16,4,4096]{3,2,0,1:T(4,128)(2,1)}), bf16[4,16,4,4096]{3,2,0,1:T(4,128)(2,1)S(1)}, u32[]{:S(2)}, u32[]{:S(2)}) %all-to-all-start.2) | async-done | bytes 2097184 | tf_op jit(solution)/shard_map/all_to_all | solution.py:22
  143.0 0.9 fusion.9
  144.2 0.7 reshape.76
  145.5 1.6 copy-done
  147.1 3.7 %fusion.1 = (f32[512]{0:T(512)S(1)}, bf16[512,4096]{1,0:T(8,128)(2,1)}) fusion(bf16[512,4096]{1,0:T(8,128)(2,1)S(1)} %copy-done, bf16[64,8,32,128]{3,2,1,0:T(8,128)(2,1)S(1)} %bitcast.52), kind=kLoop, calls=%fused_computation.3 | loop fusion | flops 8388096 | bytes 12584960 | tf_op jit(solution)/shard_map/dt,dt->d/dot_general | solution.py:52
  150.8 102.3 %all-gather.2.cloned.1.call-done = bf16[1024,4096]{1,0:T(8,128)(2,1)} async-done(((bf16[16,4096]{1,0:T(8,128)(2,1)}), bf16[1024,4096]{1,0:T(8,128)(2,1)}) %all-gather.2.cloned.1.call-update) | async-done | bytes 8388624 | tf_op jit(solution)/shard_map/all_gather | solution.py:60
  253.1 10.4 %fusion.12 = f32[1024,512]{1,0:T(8,128)} fusion(bf16[1024,4096]{1,0:T(8,128)(2,1)} %all-gather.2.cloned.1.call-done, bf16[512,4096]{1,0:T(8,128)(2,1)} %get-tuple-element.8), kind=kOutput, calls=%fused_computation.41 | convolution fusion | flops 4294967296 | bytes 14680064 | tf_op jit(solution)/shard_map/dot_general | solution.py:65
  263.6 2.5 reshape.77
  266.1 1.2 copy.15
  267.3 5.4 %all_to_all.30 = f32[64,4,2,2,1,512]{5,2,1,0,4,3:T(2,128)S(1)} all-to-all(f32[64,4,2,2,1,512]{5,2,1,0,4,3:T(2,128)S(1)} %copy.15), channel_id=1, replica_groups=mesh['x'=4,'zh'=4,'y'=4,'zl'=2,'c'=2] {'c'}, dimensions={3} | all-to-all | bytes 4194304 | tf_op jit(solution)/shard_map/all_to_all | solution.py:22
  272.7 2.1 reduce_sum.22
  274.8 1.3 copy.16
  276.1 4.5 %all-to-all-start.4 = ((f32[64,4,2,1,512]{4,1,0,3,2:T(4,128)}), f32[64,4,2,1,512]{4,1,0,3,2:T(4,128)S(1)}, u32[]{:S(2)}, u32[]{:S(2)}) async-start(f32[64,4,2,1,512]{4,1,0,3,2:T(4,128)} %copy.16), calls=%async_computation.4 | async-start | bytes 2097152 | tf_op jit(solution)/shard_map/all_to_all | solution.py:22
  280.6 5.1 %fusion = f32[1024]{0:T(1024)S(1)} fusion(bf16[1024,4096]{1,0:T(8,128)(2,1)} %all-gather.2.cloned.1.call-done), kind=kLoop, calls=%fused_computation.1 | loop fusion | flops 12581888 | bytes 8392704 | tf_op jit(solution)/shard_map/qt,qt->q/dot_general | solution.py:61
  285.6 10.3 %all-reduce = (f32[512]{0:T(512)S(1)}, f32[1024]{0:T(1024)S(1)}) all-reduce(f32[512]{0:T(512)S(1)} %get-tuple-element.11, f32[1024]{0:T(1024)S(1)} %fusion), channel_id=1, replica_groups=mesh['x'=4,'zh'=4,'y'=4,'zl'=2,'c'=2] {'zl','c'}, use_global_device_ids=true, to_apply=%region_3.4 | all-reduce | flops 1536 | bytes 12288 | tf_op jit(solution)/shard_map/psum | solution.py:53
  297.2 23.9 %all_to_all.31 = bf16[64,4,1,512]{3,1,2,0:T(4,128)(2,1)S(1)} all-to-all(bf16[64,4,1,512]{3,1,2,0:T(4,128)(2,1)S(1)} %fusion.5), channel_id=1, replica_groups=mesh['x'=4,'zh'=4,'y'=4,'zl'=2,'c'=2] {'x','zh','y'}, dimensions={0} | all-to-all | bytes 524288 | tf_op jit(solution)/shard_map/all_to_all | solution.py:22
  321.1 0.7 copy.32
  (23 shorter events, 3.1 us)
Async XLA Ops:
  18.5 31.1 %all-to-all-start = ((bf16[4,4,4,4,4096]{4,3,1,0,2:T(4,128)(2,1)}), bf16[4,4,4,4,4096]{4,3,1,0,2:T(4,128)(2,1)}, u32[]{:S(2)}, u32[]{:S(2)}) async-start(bf16[4,4,4,4,4096]{4,3,1,0,2:T(4,128)(2,1)} %copy.13), calls=%async_computation | async-start | bytes 4194304 | tf_op jit(solution)/shard_map/all_to_all | solution.py:22
  27.8 25.5 %copy-start.1 = (s32[4]{0:T(128)S(1)}, s32[4]{0:T(128)}, u32[]{:S(2)}) copy-start(s32[4]{0:T(128)} %param.5) | copy-start | bytes 52
  49.6 29.3 %all-to-all-start.1 = ((bf16[4,4,4,4,4096]{4,3,1,0,2:T(4,128)(2,1)}), bf16[4,4,4,4,4096]{4,3,1,0,2:T(4,128)(2,1)S(1)}, u32[]{:S(2)}, u32[]{:S(2)}) async-start(bf16[4,4,4,4,4096]{4,3,1,0,2:T(4,128)(2,1)} %copy.14), calls=%async_computation.1 | async-start | bytes 4194304 | tf_op jit(solution)/shard_map/all_to_all | solution.py:22
  82.1 60.9 %all-to-all-start.2 = ((bf16[4,16,4,4096]{3,2,0,1:T(4,128)(2,1)}), bf16[4,16,4,4096]{3,2,0,1:T(4,128)(2,1)S(1)}, u32[]{:S(2)}, u32[]{:S(2)}) async-start(bf16[4,16,4,4096]{3,2,0,1:T(4,128)(2,1)} %pad_maximum_fusion), calls=%async_computation.2 | async-start | bytes 4194304 | tf_op jit(solution)/shard_map/all_to_all | solution.py:22
  92.3 160.9 %all-gather.2.cloned.1.call-start = ((), (), s32[]{:S(2)}) async-start(), calls=%async_computation.6 | async-start | bytes 8519680 | tf_op jit(solution)/shard_map/all_gather | solution.py:60
  144.9 2.2 copy-start
  276.1 20.4 %all-to-all-start.4 = ((f32[64,4,2,1,512]{4,1,0,3,2:T(4,128)}), f32[64,4,2,1,512]{4,1,0,3,2:T(4,128)S(1)}, u32[]{:S(2)}, u32[]{:S(2)}) async-start(f32[64,4,2,1,512]{4,1,0,3,2:T(4,128)} %copy.16), calls=%async_computation.4 | async-start | bytes 2097152 | tf_op jit(solution)/shard_map/all_to_all | solution.py:22
Sparse Core Ops, SparseCore 0:
  145.0 108.0 all-gather.1

commit v9 on v6

--- a/solution.py
+++ b/solution.py
@@ -28,7 +28,8 @@
     steps = len(block_of)
     coord = {"x": owners // (nz * ny), "zh": (owners // ny) % nz, "y": owners % ny}
     dim = AX.index("y")
-    got = [exchange(blk.reshape(nx, nz, ny, rows // (nx * nz * ny), terms), "y", dim) for blk in blocks]
+    stacked = jnp.stack(blocks).reshape(len(blocks), nx, nz, ny, rows // (nx * nz * ny), terms)
+    got = exchange(stacked, "y", 1 + dim)
     buf = jnp.stack(
         [lax.dynamic_slice_in_dim(got[block_of[s]], coord["y"][s], 1, axis=dim) for s in range(steps)]
     )

time: 321 us -> 332 us (1.034)
  waiting for transfers between devices: 163 us -> 168 us
  local copies, waits for them, and re-layouts: 30.6 us -> 35.2 us
  other arithmetic: 16.2 us -> 20.5 us
    another operation x0 -> x3, local copies, waits for them, and re-layouts: none -> 9.96 us  [scatter_from_owner(): jnp.stack(blocks)]
    reshape x4 -> x0, local copies, waits for them, and re-layouts: 9.55 us -> none  [scatter_from_owner(): blk.reshape(nx, nz, ny, rows // (nx * nz * ny), terms)]
    another operation x0 -> x1, other arithmetic: none -> 5.36 us  [scatter_from_owner(): jnp.stack(blocks)]
    all_to_all x5 -> x4, waiting for transfers between devices: 59.2 us -> 64.1 us  [exchange(): lax.all_to_all(buf, name, split_axis=dim, concat_axis=dim, tiled=True)]
    slice x0 -> x1, local copies, waits for them, and re-layouts: none -> 3.39 us  [scatter_from_owner(): got[block_of[s]]]
    all_to_all x5 -> x4, starting transfers between devices: 24.4 us -> 21.3 us  [exchange(): lax.all_to_all(buf, name, split_axis=dim, concat_axis=dim, tiled=True)]
  transfers between devices with their start and end apart: 6 -> 5, of which waited for: 5 -> 4; matrix products, arithmetic and copies ran while one was open for 6% -> 3% of each run, Pallas kernels for 0% -> 0%
where the time goes in v9:
time: 332 us; the launch traced here: 331 us
  waiting for transfers between devices  168 us (51%)
  blocking collectives  39.5 us (12%)
  between operations  36.5 us (11%)
  local copies, waits for them, and re-layouts  35.2 us (11%)
  starting transfers between devices  21.3 us (6%)
  other arithmetic  20.5 us (6%)
  matrix products  10.4 us (3%)
    all_gather x1, waiting for transfers between devices, on_device(): lax.all_gather(pieces.reshape(STEPS * piece, term_cols), AX, axis=0, tile...  104 us
    all_to_all x4, waiting for transfers between devices, exchange(): lax.all_to_all(buf, name, split_axis=dim, concat_axis=dim, tiled=True)  64.1 us
    all_to_all x2, blocking collectives, exchange(): lax.all_to_all(buf, name, split_axis=dim, concat_axis=dim, tiled=True)  29.1 us
    all_to_all x4, starting transfers between devices, exchange(): lax.all_to_all(buf, name, split_axis=dim, concat_axis=dim, tiled=True)  21.3 us
    dot_general x1, matrix products, on_device(): lax.dot_general(flat_queries, stored, (((1,), (1,)), ((), ())), preferred...  10.4 us
    psum x1, blocking collectives, on_device(): doc_sq = lax.psum(partial_sq, RP)  10.4 us
    another operation x3, local copies, waits for them, and re-layouts, scatter_from_owner(): jnp.stack(blocks)  9.96 us
  transfers between devices with their start and end apart: 5, of which 4 were waited for; matrix products, arithmetic and copies ran while one was open for 3% of the time, Pallas kernels for 0%

profile of v9, /device:TPU:32, one launch (start us, length us, event | category | flops | bytes accessed | tf_op | source)
XLA Modules:
  0.0 331.1 jit_solution(14741055710166936129)
XLA Ops:
  7.2 3.4 %copy.31 = bf16[64,8,32,128]{3,2,1,0:T(8,128)(2,1)S(1)} copy(bf16[64,8,32,128]{3,1,2,0:T(8,128)(2,1)} %bitcast.45) | data formatting | bytes 8388608
  11.0 2.2 fusion.8
  13.2 4.0 %stack.12 = bf16[1,4,4,4,4,4096]{5,4,3,2,1,0:T(4,128)(2,1)} reshape(bf16[2,128,32,128]{3,2,1,0:T(8,128)(2,1)} %get-tuple-element.15) | data formatting | bytes 4194304 | tf_op jit(solution)/shard_map/stack | solution.py:31
  17.2 2.0 stack.13
  19.2 5.4 %pad_maximum_fusion = bf16[2,4,4,4,4,4096]{5,4,3,2,1,0:T(4,128)(2,1)S(1)} fusion(bf16[1,4,4,4,4,4096]{5,4,3,2,1,0:T(4,128)(2,1)} %stack.13, bf16[1,4,4,4,4,4096]{5,4,3,2,1,0:T(4,128)(2,1)} %stack.12), kind=kLoop, calls=%fused_computation.6 | loop fusion | flops 2097152 | bytes 8388608 | tf_op jit(solution)/shard_map/stack | solution.py:31
  24.6 4.0 %copy.16 = bf16[2,4,4,4,4,4096]{5,4,2,1,0,3:T(4,128)(2,1)} copy(bf16[2,4,4,4,4,4096]{5,4,3,2,1,0:T(4,128)(2,1)S(1)} %pad_maximum_fusion) | data formatting | bytes 8388608 | tf_op jit(solution)/shard_map/stack | solution.py:31
  28.6 5.0 %all-to-all-start = ((bf16[2,4,4,4,4,4096]{5,4,2,1,0,3:T(4,128)(2,1)}), bf16[2,4,4,4,4,4096]{5,4,2,1,0,3:T(4,128)(2,1)}, u32[]{:S(2)}, u32[]{:S(2)}) async-start(bf16[2,4,4,4,4,4096]{5,4,2,1,0,3:T(4,128)(2,1)} %copy.16), calls=%async_computation | async-start | bytes 8388608 | tf_op jit(solution)/shard_map/all_to_all | solution.py:22
  42.0 40.7 %all-to-all-done = bf16[2,4,4,4,4,4096]{5,4,2,1,0,3:T(4,128)(2,1)} async-done(((bf16[2,4,4,4,4,4096]{5,4,2,1,0,3:T(4,128)(2,1)}), bf16[2,4,4,4,4,4096]{5,4,2,1,0,3:T(4,128)(2,1)}, u32[]{:S(2)}, u32[]{:S(2)}) %all-to-all-start) | async-done | bytes 4194336 | tf_op jit(solution)/shard_map/all_to_all | solution.py:22
  82.7 3.4 %fusion.7 = (bf16[1,4,4,4,4,4096]{5,4,2,1,0,3:T(4,128)(2,1)S(1)}, bf16[1,4,4,4,4,4096]{5,4,2,1,0,3:T(4,128)(2,1)S(1)}) fusion(bf16[2,4,4,4,4,4096]{5,4,2,1,0,3:T(4,128)(2,1)} %all-to-all-done), kind=kLoop, calls=%fused_computation.43 | loop fusion | bytes 8388608 | tf_op jit(solution)/shard_map/slice | solution.py:34
  86.1 1.1 constant_dynamic-slice_fusion.11
  87.2 2.0 pad_maximum_fusion.1
  89.2 2.3 copy.17
  91.4 4.3 %all-to-all-start.1 = ((bf16[4,4,4,1,4,4096]{5,4,3,2,0,1:T(4,128)(2,1)}), bf16[4,4,4,1,4,4096]{5,4,3,2,0,1:T(4,128)(2,1)S(1)}, u32[]{:S(2)}, u32[]{:S(2)}) async-start(bf16[4,4,4,1,4,4096]{5,4,3,2,0,1:T(4,128)(2,1)} %copy.17), calls=%async_computation.1 | async-start | bytes 4194304 | tf_op jit(solution)/shard_map/all_to_all | solution.py:22
  103.8 17.4 %all-to-all-done.1 = bf16[4,4,4,1,4,4096]{5,4,3,2,0,1:T(4,128)(2,1)S(1)} async-done(((bf16[4,4,4,1,4,4096]{5,4,3,2,0,1:T(4,128)(2,1)}), bf16[4,4,4,1,4,4096]{5,4,3,2,0,1:T(4,128)(2,1)S(1)}, u32[]{:S(2)}, u32[]{:S(2)}) %all-to-all-start.1) | async-done | bytes 2097184 | tf_op jit(solution)/shard_map/all_to_all | solution.py:22
  121.2 0.9 fusion.9
  122.8 1.0 copy.18
  123.8 7.6 %all-to-all-start.2 = ((bf16[4,1,4,1,4,4096]{5,4,3,1,0,2:T(4,128)(2,1)}), bf16[4,1,4,1,4,4096]{5,4,3,1,0,2:T(4,128)(2,1)S(1)}, u32[]{:S(2)}, u32[]{:S(2)}) async-start(bf16[4,1,4,1,4,4096]{5,4,3,1,0,2:T(4,128)(2,1)} %copy.18), calls=%async_computation.2 | async-start | bytes 1048576 | tf_op jit(solution)/shard_map/all_to_all | solution.py:22
  139.1 6.0 %all-to-all-done.2 = bf16[4,1,4,1,4,4096]{5,4,3,1,0,2:T(4,128)(2,1)S(1)} async-done(((bf16[4,1,4,1,4,4096]{5,4,3,1,0,2:T(4,128)(2,1)}), bf16[4,1,4,1,4,4096]{5,4,3,1,0,2:T(4,128)(2,1)S(1)}, u32[]{:S(2)}, u32[]{:S(2)}) %all-to-all-start.2) | async-done | bytes 524320 | tf_op jit(solution)/shard_map/all_to_all | solution.py:22
  146.9 1.6 copy-done
  148.5 3.7 %fusion.1 = (f32[512]{0:T(512)S(1)}, bf16[512,4096]{1,0:T(8,128)(2,1)}) fusion(bf16[512,4096]{1,0:T(8,128)(2,1)S(1)} %copy-done, bf16[64,8,32,128]{3,2,1,0:T(8,128)(2,1)S(1)} %bitcast.46), kind=kLoop, calls=%fused_computation.3 | loop fusion | flops 8388096 | bytes 12584960 | tf_op jit(solution)/shard_map/dt,dt->d/dot_general | solution.py:57
  152.2 103.6 %all-gather.2.cloned.1.call-done = bf16[1024,4096]{1,0:T(8,128)(2,1)} async-done(((bf16[16,4096]{1,0:T(8,128)(2,1)}), bf16[1024,4096]{1,0:T(8,128)(2,1)}) %all-gather.2.cloned.1.call-update) | async-done | bytes 8388624 | tf_op jit(solution)/shard_map/all_gather | solution.py:65
  255.7 10.4 %fusion.14 = f32[1024,512]{1,0:T(8,128)} fusion(bf16[1024,4096]{1,0:T(8,128)(2,1)} %all-gather.2.cloned.1.call-done, bf16[512,4096]{1,0:T(8,128)(2,1)} %get-tuple-element.8), kind=kOutput, calls=%fused_computation.50 | convolution fusion | flops 4294967296 | bytes 14680064 | tf_op jit(solution)/shard_map/dot_general | solution.py:70
  266.2 2.5 reshape.81
  268.7 1.2 copy.19
  269.8 5.4 %all_to_all.30 = f32[64,4,2,2,1,512]{5,2,1,0,4,3:T(2,128)S(1)} all-to-all(f32[64,4,2,2,1,512]{5,2,1,0,4,3:T(2,128)S(1)} %copy.19), channel_id=1, replica_groups=mesh['x'=4,'zh'=4,'y'=4,'zl'=2,'c'=2] {'c'}, dimensions={3} | all-to-all | bytes 4194304 | tf_op jit(solution)/shard_map/all_to_all | solution.py:22
  275.3 2.1 reduce_sum.22
  277.3 1.3 copy.20
  278.7 4.5 %all-to-all-start.4 = ((f32[64,4,2,1,512]{4,1,0,3,2:T(4,128)}), f32[64,4,2,1,512]{4,1,0,3,2:T(4,128)S(1)}, u32[]{:S(2)}, u32[]{:S(2)}) async-start(f32[64,4,2,1,512]{4,1,0,3,2:T(4,128)} %copy.20), calls=%async_computation.4 | async-start | bytes 2097152 | tf_op jit(solution)/shard_map/all_to_all | solution.py:22
  283.2 5.1 %fusion = f32[1024]{0:T(1024)S(1)} fusion(bf16[1024,4096]{1,0:T(8,128)(2,1)} %all-gather.2.cloned.1.call-done), kind=kLoop, calls=%fused_computation.1 | loop fusion | flops 12581888 | bytes 8392704 | tf_op jit(solution)/shard_map/qt,qt->q/dot_general | solution.py:66
  288.2 10.4 %all-reduce = (f32[512]{0:T(512)S(1)}, f32[1024]{0:T(1024)S(1)}) all-reduce(f32[512]{0:T(512)S(1)} %get-tuple-element.11, f32[1024]{0:T(1024)S(1)} %fusion), channel_id=1, replica_groups=mesh['x'=4,'zh'=4,'y'=4,'zl'=2,'c'=2] {'zl','c'}, use_global_device_ids=true, to_apply=%region_3.4 | all-reduce | flops 1536 | bytes 12288 | tf_op jit(solution)/shard_map/psum | solution.py:58
  299.9 23.7 %all_to_all.31 = bf16[64,4,1,512]{3,1,2,0:T(4,128)(2,1)S(1)} all-to-all(bf16[64,4,1,512]{3,1,2,0:T(4,128)(2,1)S(1)} %fusion.5), channel_id=1, replica_groups=mesh['x'=4,'zh'=4,'y'=4,'zl'=2,'c'=2] {'x','zh','y'}, dimensions={0} | all-to-all | bytes 524288 | tf_op jit(solution)/shard_map/all_to_all | solution.py:22
  323.6 0.7 copy.36
  (32 shorter events, 6.0 us)
Async XLA Ops:
  28.6 5.0 %copy-start.1 = (s32[4]{0:T(128)S(1)}, s32[4]{0:T(128)}, u32[]{:S(2)}) copy-start(s32[4]{0:T(128)} %param.5) | copy-start | bytes 52
  28.6 54.1 %all-to-all-start = ((bf16[2,4,4,4,4,4096]{5,4,2,1,0,3:T(4,128)(2,1)}), bf16[2,4,4,4,4,4096]{5,4,2,1,0,3:T(4,128)(2,1)}, u32[]{:S(2)}, u32[]{:S(2)}) async-start(bf16[2,4,4,4,4,4096]{5,4,2,1,0,3:T(4,128)(2,1)} %copy.16), calls=%async_computation | async-start | bytes 8388608 | tf_op jit(solution)/shard_map/all_to_all | solution.py:22
  91.4 29.8 %all-to-all-start.1 = ((bf16[4,4,4,1,4,4096]{5,4,3,2,0,1:T(4,128)(2,1)}), bf16[4,4,4,1,4,4096]{5,4,3,2,0,1:T(4,128)(2,1)S(1)}, u32[]{:S(2)}, u32[]{:S(2)}) async-start(bf16[4,4,4,1,4,4096]{5,4,3,2,0,1:T(4,128)(2,1)} %copy.17), calls=%async_computation.1 | async-start | bytes 4194304 | tf_op jit(solution)/shard_map/all_to_all | solution.py:22
  123.8 21.2 %all-to-all-start.2 = ((bf16[4,1,4,1,4,4096]{5,4,3,1,0,2:T(4,128)(2,1)}), bf16[4,1,4,1,4,4096]{5,4,3,1,0,2:T(4,128)(2,1)S(1)}, u32[]{:S(2)}, u32[]{:S(2)}) async-start(bf16[4,1,4,1,4,4096]{5,4,3,1,0,2:T(4,128)(2,1)} %copy.18), calls=%async_computation.2 | async-start | bytes 1048576 | tf_op jit(solution)/shard_map/all_to_all | solution.py:22
  131.4 124.3 %all-gather.2.cloned.1.call-start = ((), (), s32[]{:S(2)}) async-start(), calls=%async_computation.6 | async-start | bytes 8519680 | tf_op jit(solution)/shard_map/all_gather | solution.py:65
  146.3 2.2 copy-start
  278.7 20.5 %all-to-all-start.4 = ((f32[64,4,2,1,512]{4,1,0,3,2:T(4,128)}), f32[64,4,2,1,512]{4,1,0,3,2:T(4,128)S(1)}, u32[]{:S(2)}, u32[]{:S(2)}) async-start(f32[64,4,2,1,512]{4,1,0,3,2:T(4,128)} %copy.20), calls=%async_computation.4 | async-start | bytes 2097152 | tf_op jit(solution)/shard_map/all_to_all | solution.py:22
Sparse Core Ops, SparseCore 0:
  146.4 109.3 all-gather.1

commit v10 on v6

--- a/solution.py
+++ b/solution.py
@@ -63,6 +63,7 @@
     piece = pieces.shape[1]
     flat_queries = lax.all_gather(pieces.reshape(STEPS * piece, term_cols), AX, axis=0, tiled=True)
     q_sq = jnp.einsum("qt,qt->q", flat_queries, flat_queries, preferred_element_type=jnp.float32)
+    q_sq, inverse = lax.optimization_barrier((q_sq, inverse))
     q_inv = lax.rsqrt(lax.psum(q_sq, RP) + EPSILON).reshape(n_shard, STEPS, piece)
     flat_queries, stored = lax.optimization_barrier((flat_queries, masked))
     similar = lax.optimization_barrier(

time: 321 us -> 321 us (level)
  waiting for transfers between devices: 163 us -> 157 us
  blocking collectives: 39.6 us -> 45.1 us
    psum x0 -> x1, blocking collectives: none -> 10.2 us  [on_device(): lax.psum(q_sq, RP) + EPSILON]
    all_gather x1, waiting for transfers between devices: 104 us -> 97.7 us  [on_device(): lax.all_gather(pieces.reshape(STEPS * piece, term_cols), AX, axis=0, tile...]
    psum x1, blocking collectives: 10.3 us -> 5.82 us  [on_device(): doc_sq = lax.psum(partial_sq, RP)]
where the time goes in v10:
time: 321 us; the launch traced here: 320 us
  waiting for transfers between devices  157 us (49%)
  blocking collectives  45.1 us (14%)
  between operations  36.6 us (11%)
  local copies, waits for them, and re-layouts  30.5 us (10%)
  starting transfers between devices  24.4 us (8%)
  other arithmetic  16.2 us (5%)
  matrix products  10.4 us (3%)
    all_gather x1, waiting for transfers between devices, on_device(): lax.all_gather(pieces.reshape(STEPS * piece, term_cols), AX, axis=0, tile...  97.7 us
    all_to_all x5, waiting for transfers between devices, exchange(): lax.all_to_all(buf, name, split_axis=dim, concat_axis=dim, tiled=True)  59 us
    all_to_all x2, blocking collectives, exchange(): lax.all_to_all(buf, name, split_axis=dim, concat_axis=dim, tiled=True)  29.1 us
    all_to_all x5, starting transfers between devices, exchange(): lax.all_to_all(buf, name, split_axis=dim, concat_axis=dim, tiled=True)  24.4 us
    dot_general x1, matrix products, on_device(): lax.dot_general(flat_queries, stored, (((1,), (1,)), ((), ())), preferred...  10.4 us
    psum x1, blocking collectives, on_device(): lax.psum(q_sq, RP) + EPSILON  10.2 us
    reshape x4, local copies, waits for them, and re-layouts, scatter_from_owner(): blk.reshape(nx, nz, ny, rows // (nx * nz * ny), terms)  9.53 us
  transfers between devices with their start and end apart: 6, of which 5 were waited for; matrix products, arithmetic and copies ran while one was open for 6% of the time, Pallas kernels for 0%

profile of v10, /device:TPU:32, one launch (start us, length us, event | category | flops | bytes accessed | tf_op | source)
XLA Modules:
  0.0 319.9 jit_solution(12856579485684318604)
XLA Ops:
  7.2 3.4 %copy.30 = bf16[64,8,32,128]{3,2,1,0:T(8,128)(2,1)S(1)} copy(bf16[64,8,32,128]{3,1,2,0:T(8,128)(2,1)} %bitcast.53) | data formatting | bytes 8388608
  11.0 2.7 fusion.7
  13.8 2.5 reshape.74
  16.3 2.2 copy.15
  18.5 4.5 %all-to-all-start = ((bf16[4,4,4,4,4096]{4,3,1,0,2:T(4,128)(2,1)}), bf16[4,4,4,4,4096]{4,3,1,0,2:T(4,128)(2,1)}, u32[]{:S(2)}, u32[]{:S(2)}) async-start(bf16[4,4,4,4,4096]{4,3,1,0,2:T(4,128)(2,1)} %copy.15), calls=%async_computation | async-start | bytes 4194304 | tf_op jit(solution)/shard_map/all_to_all | solution.py:22
  23.0 2.5 reshape.75
  25.5 2.2 copy.16
  27.8 21.9 %all-to-all-done = bf16[4,4,4,4,4096]{4,3,1,0,2:T(4,128)(2,1)} async-done(((bf16[4,4,4,4,4096]{4,3,1,0,2:T(4,128)(2,1)}), bf16[4,4,4,4,4096]{4,3,1,0,2:T(4,128)(2,1)}, u32[]{:S(2)}, u32[]{:S(2)}) %all-to-all-start) | async-done | bytes 2097184 | tf_op jit(solution)/shard_map/all_to_all | solution.py:22
  49.6 3.6 %all-to-all-start.1 = ((bf16[4,4,4,4,4096]{4,3,1,0,2:T(4,128)(2,1)}), bf16[4,4,4,4,4096]{4,3,1,0,2:T(4,128)(2,1)S(1)}, u32[]{:S(2)}, u32[]{:S(2)}) async-start(bf16[4,4,4,4,4096]{4,3,1,0,2:T(4,128)(2,1)} %copy.16), calls=%async_computation.1 | async-start | bytes 4194304 | tf_op jit(solution)/shard_map/all_to_all | solution.py:22
  61.4 1.6 dynamic-slice_bitcast_fusion.3
  63.0 15.9 %all-to-all-done.1 = bf16[4,4,4,4,4096]{4,3,1,0,2:T(4,128)(2,1)S(1)} async-done(((bf16[4,4,4,4,4096]{4,3,1,0,2:T(4,128)(2,1)}), bf16[4,4,4,4,4096]{4,3,1,0,2:T(4,128)(2,1)S(1)}, u32[]{:S(2)}, u32[]{:S(2)}) %all-to-all-start.1) | async-done | bytes 2097184 | tf_op jit(solution)/shard_map/all_to_all | solution.py:22
  79.3 3.0 pad_maximum_fusion
  82.3 4.3 %all-to-all-start.2 = ((bf16[4,4,4,1,4,4096]{5,4,2,3,0,1:T(4,128)(2,1)}), bf16[4,4,4,1,4,4096]{5,4,2,3,0,1:T(4,128)(2,1)S(1)}, u32[]{:S(2)}, u32[]{:S(2)}) async-start(bf16[4,4,4,1,4,4096]{5,4,2,3,0,1:T(4,128)(2,1)} %pad_maximum_fusion), calls=%async_computation.2 | async-start | bytes 4194304 | tf_op jit(solution)/shard_map/all_to_all | solution.py:22
  94.8 16.3 %all-to-all-done.2 = bf16[4,4,4,1,4,4096]{5,4,2,3,0,1:T(4,128)(2,1)S(1)} async-done(((bf16[4,4,4,1,4,4096]{5,4,2,3,0,1:T(4,128)(2,1)}), bf16[4,4,4,1,4,4096]{5,4,2,3,0,1:T(4,128)(2,1)S(1)}, u32[]{:S(2)}, u32[]{:S(2)}) %all-to-all-start.2) | async-done | bytes 2097184 | tf_op jit(solution)/shard_map/all_to_all | solution.py:22
  111.2 0.9 fusion.8
  112.8 1.0 copy.17
  113.8 7.6 %all-to-all-start.3 = ((bf16[4,1,4,1,4,4096]{5,4,1,3,0,2:T(4,128)(2,1)}), bf16[4,1,4,1,4,4096]{5,4,1,3,0,2:T(4,128)(2,1)S(1)}, u32[]{:S(2)}, u32[]{:S(2)}) async-start(bf16[4,1,4,1,4,4096]{5,4,1,3,0,2:T(4,128)(2,1)} %copy.17), calls=%async_computation.3 | async-start | bytes 1048576 | tf_op jit(solution)/shard_map/all_to_all | solution.py:22
  129.3 4.9 %all-to-all-done.3 = bf16[4,1,4,1,4,4096]{5,4,1,3,0,2:T(4,128)(2,1)S(1)} async-done(((bf16[4,1,4,1,4,4096]{5,4,1,3,0,2:T(4,128)(2,1)}), bf16[4,1,4,1,4,4096]{5,4,1,3,0,2:T(4,128)(2,1)S(1)}, u32[]{:S(2)}, u32[]{:S(2)}) %all-to-all-start.3) | async-done | bytes 524320 | tf_op jit(solution)/shard_map/all_to_all | solution.py:22
  135.9 1.6 copy-done
  137.5 3.7 %fusion.1 = (f32[512]{0:T(512)S(1)}, bf16[512,4096]{1,0:T(8,128)(2,1)}) fusion(bf16[512,4096]{1,0:T(8,128)(2,1)S(1)} %copy-done, bf16[64,8,32,128]{3,2,1,0:T(8,128)(2,1)S(1)} %bitcast.54), kind=kLoop, calls=%fused_computation.3 | loop fusion | flops 8388096 | bytes 12584960 | tf_op jit(solution)/shard_map/dt,dt->d/dot_general | solution.py:56
  141.3 5.8 %psum.14 = f32[512]{0:T(512)S(1)} all-reduce(f32[512]{0:T(512)S(1)} %get-tuple-element.13), channel_id=1, replica_groups=mesh['x'=4,'zh'=4,'y'=4,'zl'=2,'c'=2] {'zl','c'}, use_global_device_ids=true, to_apply=%region_2.3 | all-reduce | flops 512 | bytes 4096 | tf_op jit(solution)/shard_map/psum | solution.py:57
  147.1 97.7 %all-gather.2.cloned.1.call-done = bf16[1024,4096]{1,0:T(8,128)(2,1)} async-done(((bf16[16,4096]{1,0:T(8,128)(2,1)}), bf16[1024,4096]{1,0:T(8,128)(2,1)}) %all-gather.2.cloned.1.call-update) | async-done | bytes 8388624 | tf_op jit(solution)/shard_map/all_gather | solution.py:64
  244.8 10.4 %fusion.13 = f32[1024,512]{1,0:T(8,128)} fusion(bf16[1024,4096]{1,0:T(8,128)(2,1)} %all-gather.2.cloned.1.call-done, bf16[512,4096]{1,0:T(8,128)(2,1)} %get-tuple-element.10), kind=kOutput, calls=%fused_computation.48 | convolution fusion | flops 4294967296 | bytes 14680064 | tf_op jit(solution)/shard_map/dot_general | solution.py:70
  255.2 2.5 reshape.76
  257.7 1.2 copy.18
  258.9 5.4 %all_to_all.35 = f32[64,4,2,2,1,512]{5,2,1,0,4,3:T(2,128)S(1)} all-to-all(f32[64,4,2,2,1,512]{5,2,1,0,4,3:T(2,128)S(1)} %copy.18), channel_id=1, replica_groups=mesh['x'=4,'zh'=4,'y'=4,'zl'=2,'c'=2] {'c'}, dimensions={3} | all-to-all | bytes 4194304 | tf_op jit(solution)/shard_map/all_to_all | solution.py:22
  264.3 2.1 reduce_sum.22
  266.4 1.3 copy.19
  267.7 4.5 %all-to-all-start.5 = ((f32[64,4,2,1,512]{4,1,0,3,2:T(4,128)}), f32[64,4,2,1,512]{4,1,0,3,2:T(4,128)S(1)}, u32[]{:S(2)}, u32[]{:S(2)}) async-start(f32[64,4,2,1,512]{4,1,0,3,2:T(4,128)} %copy.19), calls=%async_computation.5 | async-start | bytes 2097152 | tf_op jit(solution)/shard_map/all_to_all | solution.py:22
  272.2 5.1 %fusion = f32[1024]{0:T(1024)S(1)} fusion(bf16[1024,4096]{1,0:T(8,128)(2,1)} %all-gather.2.cloned.1.call-done), kind=kLoop, calls=%fused_computation.1 | loop fusion | flops 12581888 | bytes 8392704 | tf_op jit(solution)/shard_map/qt,qt->q/dot_general | solution.py:65
  277.3 10.2 %psum.15 = f32[1024]{0:T(1024)S(1)} all-reduce(f32[1024]{0:T(1024)S(1)} %fusion), channel_id=1, replica_groups=mesh['x'=4,'zh'=4,'y'=4,'zl'=2,'c'=2] {'zl','c'}, use_global_device_ids=true, to_apply=%region_3.4 | all-reduce | flops 1024 | bytes 8192 | tf_op jit(solution)/shard_map/psum | solution.py:67
  288.7 23.7 %all_to_all.36 = bf16[64,4,1,512]{3,1,2,0:T(4,128)(2,1)S(1)} all-to-all(bf16[64,4,1,512]{3,1,2,0:T(4,128)(2,1)S(1)} %fusion.5), channel_id=1, replica_groups=mesh['x'=4,'zh'=4,'y'=4,'zl'=2,'c'=2] {'x','zh','y'}, dimensions={0} | all-to-all | bytes 524288 | tf_op jit(solution)/shard_map/all_to_all | solution.py:22
  (34 shorter events, 7.1 us)
Async XLA Ops:
  18.5 31.1 %all-to-all-start = ((bf16[4,4,4,4,4096]{4,3,1,0,2:T(4,128)(2,1)}), bf16[4,4,4,4,4096]{4,3,1,0,2:T(4,128)(2,1)}, u32[]{:S(2)}, u32[]{:S(2)}) async-start(bf16[4,4,4,4,4096]{4,3,1,0,2:T(4,128)(2,1)} %copy.15), calls=%async_computation | async-start | bytes 4194304 | tf_op jit(solution)/shard_map/all_to_all | solution.py:22
  27.8 25.5 %copy-start.1 = (s32[4]{0:T(128)S(1)}, s32[4]{0:T(128)}, u32[]{:S(2)}) copy-start(s32[4]{0:T(128)} %param.5) | copy-start | bytes 52
  49.6 29.3 %all-to-all-start.1 = ((bf16[4,4,4,4,4096]{4,3,1,0,2:T(4,128)(2,1)}), bf16[4,4,4,4,4096]{4,3,1,0,2:T(4,128)(2,1)S(1)}, u32[]{:S(2)}, u32[]{:S(2)}) async-start(bf16[4,4,4,4,4096]{4,3,1,0,2:T(4,128)(2,1)} %copy.16), calls=%async_computation.1 | async-start | bytes 4194304 | tf_op jit(solution)/shard_map/all_to_all | solution.py:22
  82.3 28.9 %all-to-all-start.2 = ((bf16[4,4,4,1,4,4096]{5,4,2,3,0,1:T(4,128)(2,1)}), bf16[4,4,4,1,4,4096]{5,4,2,3,0,1:T(4,128)(2,1)S(1)}, u32[]{:S(2)}, u32[]{:S(2)}) async-start(bf16[4,4,4,1,4,4096]{5,4,2,3,0,1:T(4,128)(2,1)} %pad_maximum_fusion), calls=%async_computation.2 | async-start | bytes 4194304 | tf_op jit(solution)/shard_map/all_to_all | solution.py:22
  113.8 20.4 %all-to-all-start.3 = ((bf16[4,1,4,1,4,4096]{5,4,1,3,0,2:T(4,128)(2,1)}), bf16[4,1,4,1,4,4096]{5,4,1,3,0,2:T(4,128)(2,1)S(1)}, u32[]{:S(2)}, u32[]{:S(2)}) async-start(bf16[4,1,4,1,4,4096]{5,4,1,3,0,2:T(4,128)(2,1)} %copy.17), calls=%async_computation.3 | async-start | bytes 1048576 | tf_op jit(solution)/shard_map/all_to_all | solution.py:22
  121.3 123.4 %all-gather.2.cloned.1.call-start = ((), (), s32[]{:S(2)}) async-start(), calls=%async_computation.7 | async-start | bytes 8519680 | tf_op jit(solution)/shard_map/all_gather | solution.py:64
  135.3 2.2 copy-start
  267.7 20.3 %all-to-all-start.5 = ((f32[64,4,2,1,512]{4,1,0,3,2:T(4,128)}), f32[64,4,2,1,512]{4,1,0,3,2:T(4,128)S(1)}, u32[]{:S(2)}, u32[]{:S(2)}) async-start(f32[64,4,2,1,512]{4,1,0,3,2:T(4,128)} %copy.19), calls=%async_computation.5 | async-start | bytes 2097152 | tf_op jit(solution)/shard_map/all_to_all | solution.py:22
Sparse Core Ops, SparseCore 0:
  135.4 109.2 all-gather.1

commit v11 on v6

--- a/solution.py
+++ b/solution.py
@@ -61,22 +61,22 @@
     block_of = [s % (doc_rows // QUERY) for s in range(STEPS)]
     pieces = scatter_from_owner(blocks, block_of, owners, sizes)
     piece = pieces.shape[1]
+    row_share = piece // n_rep
+    own_sq = lax.psum(jnp.einsum("spt,spt->sp", pieces, pieces, preferred_element_type=jnp.float32), RP)
+    own_inv = lax.dynamic_slice_in_dim(lax.rsqrt(own_sq + EPSILON), rep_index * row_share, row_share, axis=1)
     flat_queries = lax.all_gather(pieces.reshape(STEPS * piece, term_cols), AX, axis=0, tiled=True)
-    q_sq = jnp.einsum("qt,qt->q", flat_queries, flat_queries, preferred_element_type=jnp.float32)
-    q_inv = lax.rsqrt(lax.psum(q_sq, RP) + EPSILON).reshape(n_shard, STEPS, piece)
     flat_queries, stored = lax.optimization_barrier((flat_queries, masked))
     similar = lax.optimization_barrier(
         lax.dot_general(flat_queries, stored, (((1,), (1,)), ((), ())), preferred_element_type=jnp.float32)
     )
-    row_share = piece // n_rep
     similar = similar.reshape(n_shard, STEPS, 2, 2, row_share, doc_rows)
     similar = jnp.sum(exchange(similar, "c", 3), axis=3)
     mine = jnp.sum(exchange(similar, "zl", 2), axis=2)
-    my_inv = lax.dynamic_slice_in_dim(q_inv, rep_index * row_share, row_share, axis=2)
-    scaled = mine * my_inv[..., None] * inverse[None, None, None, :] * sharpen
+    weighted = mine * inverse[None, None, None, :]
+    got = exchange(weighted, AX, 0)
+    scaled = got * own_inv[None, :, :, None] * sharpen
     scores = jnp.clip(scaled, -CLIP_LEVEL, CLIP_LEVEL).astype(jnp.bfloat16)
-    got = exchange(scores, AX, 0)
-    return got.transpose(1, 2, 0, 3).reshape(STEPS, row_share, n_shard * doc_rows)
+    return scores.transpose(1, 2, 0, 3).reshape(STEPS, row_share, n_shard * doc_rows)
 
 
 def solution(mesh):

time: 321 us -> 327 us (1.019)
  blocking collectives: 39.6 us -> 20.6 us
  waiting for transfers between devices: 163 us -> 180 us
  starting transfers between devices: 24.4 us -> 34.2 us
  other arithmetic: 16.2 us -> 12.7 us
    all_to_all x2 -> x1, blocking collectives: 29.3 us -> 5.42 us  [exchange(): lax.all_to_all(buf, name, split_axis=dim, concat_axis=dim, tiled=True)]
    all_to_all x5 -> x6, waiting for transfers between devices: 59.2 us -> 76.6 us  [exchange(): lax.all_to_all(buf, name, split_axis=dim, concat_axis=dim, tiled=True)]
    all_to_all x5 -> x6, starting transfers between devices: 24.4 us -> 34.2 us  [exchange(): lax.all_to_all(buf, name, split_axis=dim, concat_axis=dim, tiled=True)]
    dot_general x1 -> x0, other arithmetic: 5.07 us -> none  [on_device(): jnp.einsum('qt,qt->q', flat_queries, flat_queries, preferred_element_type...]
    psum x1, blocking collectives: 10.3 us -> 15.2 us  [on_device(): doc_sq = lax.psum(partial_sq, RP)]
  transfers between devices with their start and end apart: 6 -> 7, of which waited for: 5 -> 6; matrix products, arithmetic and copies ran while one was open for 6% -> 4% of each run, Pallas kernels for 0% -> 0%
where the time goes in v11:
time: 327 us; the launch traced here: 323 us
  waiting for transfers between devices  180 us (55%)
  between operations  35.9 us (11%)
  starting transfers between devices  34.2 us (10%)
  local copies, waits for them, and re-layouts  29.4 us (9%)
  blocking collectives  20.6 us (6%)
  other arithmetic  12.7 us (4%)
  matrix products  10.4 us (3%)
    all_gather x1, waiting for transfers between devices, on_device(): lax.all_gather(pieces.reshape(STEPS * piece, term_cols), AX, axis=0, tile...  104 us
    all_to_all x6, waiting for transfers between devices, exchange(): lax.all_to_all(buf, name, split_axis=dim, concat_axis=dim, tiled=True)  76.6 us
    all_to_all x6, starting transfers between devices, exchange(): lax.all_to_all(buf, name, split_axis=dim, concat_axis=dim, tiled=True)  34.2 us
    psum x1, blocking collectives, on_device(): doc_sq = lax.psum(partial_sq, RP)  15.2 us
    dot_general x1, matrix products, on_device(): lax.dot_general(flat_queries, stored, (((1,), (1,)), ((), ())), preferred...  10.4 us
    reshape x4, local copies, waits for them, and re-layouts, scatter_from_owner(): blk.reshape(nx, nz, ny, rows // (nx * nz * ny), terms)  9.54 us
  transfers between devices with their start and end apart: 7, of which 6 were waited for; matrix products, arithmetic and copies ran while one was open for 4% of the time, Pallas kernels for 0%

profile of v11, /device:TPU:32, one launch (start us, length us, event | category | flops | bytes accessed | tf_op | source)
XLA Modules:
  0.0 323.4 jit_solution(16367541808137207156)
XLA Ops:
  7.2 3.4 %copy.24 = bf16[64,8,32,128]{3,2,1,0:T(8,128)(2,1)S(1)} copy(bf16[64,8,32,128]{3,1,2,0:T(8,128)(2,1)} %bitcast.48) | data formatting | bytes 8388608
  11.0 2.7 fusion.4
  13.8 2.5 reshape.58
  16.3 2.3 copy.10
  18.5 4.5 %all-to-all-start = ((bf16[4,4,4,4,4096]{4,3,1,0,2:T(4,128)(2,1)}), bf16[4,4,4,4,4096]{4,3,1,0,2:T(4,128)(2,1)}, u32[]{:S(2)}, u32[]{:S(2)}) async-start(bf16[4,4,4,4,4096]{4,3,1,0,2:T(4,128)(2,1)} %copy.10), calls=%async_computation | async-start | bytes 4194304 | tf_op jit(solution)/shard_map/all_to_all | solution.py:22
  23.0 2.5 reshape.59
  25.6 2.2 copy.11
  27.8 21.9 %all-to-all-done = bf16[4,4,4,4,4096]{4,3,1,0,2:T(4,128)(2,1)} async-done(((bf16[4,4,4,4,4096]{4,3,1,0,2:T(4,128)(2,1)}), bf16[4,4,4,4,4096]{4,3,1,0,2:T(4,128)(2,1)}, u32[]{:S(2)}, u32[]{:S(2)}) %all-to-all-start) | async-done | bytes 2097184 | tf_op jit(solution)/shard_map/all_to_all | solution.py:22
  49.7 3.6 %all-to-all-start.1 = ((bf16[4,4,4,4,4096]{4,3,1,0,2:T(4,128)(2,1)}), bf16[4,4,4,4,4096]{4,3,1,0,2:T(4,128)(2,1)S(1)}, u32[]{:S(2)}, u32[]{:S(2)}) async-start(bf16[4,4,4,4,4096]{4,3,1,0,2:T(4,128)(2,1)} %copy.11), calls=%async_computation.1 | async-start | bytes 4194304 | tf_op jit(solution)/shard_map/all_to_all | solution.py:22
  61.3 1.6 dynamic-slice_bitcast_fusion.3
  62.9 16.0 %all-to-all-done.1 = bf16[4,4,4,4,4096]{4,3,1,0,2:T(4,128)(2,1)S(1)} async-done(((bf16[4,4,4,4,4096]{4,3,1,0,2:T(4,128)(2,1)}), bf16[4,4,4,4,4096]{4,3,1,0,2:T(4,128)(2,1)S(1)}, u32[]{:S(2)}, u32[]{:S(2)}) %all-to-all-start.1) | async-done | bytes 2097184 | tf_op jit(solution)/shard_map/all_to_all | solution.py:22
  79.4 2.9 pad_maximum_fusion
  82.3 4.3 %all-to-all-start.2 = ((bf16[4,4,4,1,4,4096]{5,4,2,3,0,1:T(4,128)(2,1)}), bf16[4,4,4,1,4,4096]{5,4,2,3,0,1:T(4,128)(2,1)S(1)}, u32[]{:S(2)}, u32[]{:S(2)}) async-start(bf16[4,4,4,1,4,4096]{5,4,2,3,0,1:T(4,128)(2,1)} %pad_maximum_fusion), calls=%async_computation.2 | async-start | bytes 4194304 | tf_op jit(solution)/shard_map/all_to_all | solution.py:22
  94.9 16.3 %all-to-all-done.2 = bf16[4,4,4,1,4,4096]{5,4,2,3,0,1:T(4,128)(2,1)S(1)} async-done(((bf16[4,4,4,1,4,4096]{5,4,2,3,0,1:T(4,128)(2,1)}), bf16[4,4,4,1,4,4096]{5,4,2,3,0,1:T(4,128)(2,1)S(1)}, u32[]{:S(2)}, u32[]{:S(2)}) %all-to-all-start.2) | async-done | bytes 2097184 | tf_op jit(solution)/shard_map/all_to_all | solution.py:22
  111.1 0.9 fusion.5
  112.8 1.0 copy.12
  113.8 7.6 %all-to-all-start.3 = ((bf16[4,1,4,1,4,4096]{5,4,1,3,0,2:T(4,128)(2,1)}), bf16[4,1,4,1,4,4096]{5,4,1,3,0,2:T(4,128)(2,1)S(1)}, u32[]{:S(2)}, u32[]{:S(2)}) async-start(bf16[4,1,4,1,4,4096]{5,4,1,3,0,2:T(4,128)(2,1)} %copy.12), calls=%async_computation.3 | async-start | bytes 1048576 | tf_op jit(solution)/shard_map/all_to_all | solution.py:22
  128.7 5.5 %all-to-all-done.3 = bf16[4,1,4,1,4,4096]{5,4,1,3,0,2:T(4,128)(2,1)S(1)} async-done(((bf16[4,1,4,1,4,4096]{5,4,1,3,0,2:T(4,128)(2,1)}), bf16[4,1,4,1,4,4096]{5,4,1,3,0,2:T(4,128)(2,1)S(1)}, u32[]{:S(2)}, u32[]{:S(2)}) %all-to-all-start.3) | async-done | bytes 524320 | tf_op jit(solution)/shard_map/all_to_all | solution.py:22
  136.0 1.6 copy-done
  137.6 3.7 %fusion = (f32[512]{0:T(512)S(1)}, bf16[512,4096]{1,0:T(8,128)(2,1)}) fusion(bf16[512,4096]{1,0:T(8,128)(2,1)S(1)} %copy-done, bf16[64,8,32,128]{3,2,1,0:T(8,128)(2,1)S(1)} %bitcast.49), kind=kLoop, calls=%fused_computation.1 | loop fusion | flops 8388096 | bytes 12584960 | tf_op jit(solution)/shard_map/dt,dt->d/dot_general | solution.py:56
  141.3 103.5 %all-gather.2.cloned.1.call-done = bf16[1024,4096]{1,0:T(8,128)(2,1)} async-done(((bf16[16,4096]{1,0:T(8,128)(2,1)}), bf16[1024,4096]{1,0:T(8,128)(2,1)}) %all-gather.2.cloned.1.call-update) | async-done | bytes 8388624 | tf_op jit(solution)/shard_map/all_gather | solution.py:67
  244.8 10.4 %fusion.10 = f32[1024,512]{1,0:T(8,128)} fusion(bf16[1024,4096]{1,0:T(8,128)(2,1)} %all-gather.2.cloned.1.call-done, bf16[512,4096]{1,0:T(8,128)(2,1)} %get-tuple-element.8), kind=kOutput, calls=%fused_computation.46 | convolution fusion | flops 4294967296 | bytes 14680064 | tf_op jit(solution)/shard_map/dot_general | solution.py:70
  255.2 2.5 reshape.60
  257.7 1.2 copy.13
  258.9 5.4 %all_to_all.35 = f32[64,4,2,2,1,512]{5,2,1,0,4,3:T(2,128)S(1)} all-to-all(f32[64,4,2,2,1,512]{5,2,1,0,4,3:T(2,128)S(1)} %copy.13), channel_id=1, replica_groups=mesh['x'=4,'zh'=4,'y'=4,'zl'=2,'c'=2] {'c'}, dimensions={3} | all-to-all | bytes 4194304 | tf_op jit(solution)/shard_map/all_to_all | solution.py:22
  264.3 2.1 reduce_sum.22
  266.4 1.2 copy.14
  267.7 4.5 %all-to-all-start.5 = ((f32[64,4,2,1,512]{4,1,0,3,2:T(4,128)}), f32[64,4,2,1,512]{4,1,0,3,2:T(4,128)S(1)}, u32[]{:S(2)}, u32[]{:S(2)}) async-start(f32[64,4,2,1,512]{4,1,0,3,2:T(4,128)} %copy.14), calls=%async_computation.5 | async-start | bytes 2097152 | tf_op jit(solution)/shard_map/all_to_all | solution.py:22
  272.3 15.2 %all-reduce = (f32[512]{0:T(512)S(1)}, f32[4,4]{0,1:T(4,128)S(1)}) all-reduce(f32[512]{0:T(512)S(1)} %get-tuple-element.13, f32[4,4]{0,1:T(4,128)S(1)} %copy.21), channel_id=1, replica_groups=mesh['x'=4,'zh'=4,'y'=4,'zl'=2,'c'=2] {'zl','c'}, use_global_device_ids=true, to_apply=%region_2.3 | all-reduce | flops 528 | bytes 4224 | tf_op jit(solution)/shard_map/psum | solution.py:57
  288.8 9.8 %all-to-all-start.6 = ((f32[64,4,1,512]{3,1,2,0:T(4,128)}), f32[64,4,1,512]{3,1,2,0:T(4,128)S(1)}, u32[]{:S(2)}, u32[]{:S(2)}) async-start(f32[64,4,1,512]{3,1,2,0:T(4,128)} %bitcast_multiply_fusion.2), calls=%async_computation.6 | async-start | bytes 1048576 | tf_op jit(solution)/shard_map/all_to_all | solution.py:22
  298.6 17.0 %all-to-all-done.6 = f32[64,4,1,512]{3,1,2,0:T(4,128)S(1)} async-done(((f32[64,4,1,512]{3,1,2,0:T(4,128)}), f32[64,4,1,512]{3,1,2,0:T(4,128)S(1)}, u32[]{:S(2)}, u32[]{:S(2)}) %all-to-all-start.6) | async-done | bytes 524320 | tf_op jit(solution)/shard_map/all_to_all | solution.py:22
  315.6 0.9 clamp_convert_fusion
  (31 shorter events, 6.7 us)
Async XLA Ops:
  18.5 31.1 %all-to-all-start = ((bf16[4,4,4,4,4096]{4,3,1,0,2:T(4,128)(2,1)}), bf16[4,4,4,4,4096]{4,3,1,0,2:T(4,128)(2,1)}, u32[]{:S(2)}, u32[]{:S(2)}) async-start(bf16[4,4,4,4,4096]{4,3,1,0,2:T(4,128)(2,1)} %copy.10), calls=%async_computation | async-start | bytes 4194304 | tf_op jit(solution)/shard_map/all_to_all | solution.py:22
  27.8 25.5 %copy-start.1 = (s32[4]{0:T(128)S(1)}, s32[4]{0:T(128)}, u32[]{:S(2)}) copy-start(s32[4]{0:T(128)} %param.5) | copy-start | bytes 52
  49.7 29.3 %all-to-all-start.1 = ((bf16[4,4,4,4,4096]{4,3,1,0,2:T(4,128)(2,1)}), bf16[4,4,4,4,4096]{4,3,1,0,2:T(4,128)(2,1)S(1)}, u32[]{:S(2)}, u32[]{:S(2)}) async-start(bf16[4,4,4,4,4096]{4,3,1,0,2:T(4,128)(2,1)} %copy.11), calls=%async_computation.1 | async-start | bytes 4194304 | tf_op jit(solution)/shard_map/all_to_all | solution.py:22
  82.3 28.9 %all-to-all-start.2 = ((bf16[4,4,4,1,4,4096]{5,4,2,3,0,1:T(4,128)(2,1)}), bf16[4,4,4,1,4,4096]{5,4,2,3,0,1:T(4,128)(2,1)S(1)}, u32[]{:S(2)}, u32[]{:S(2)}) async-start(bf16[4,4,4,1,4,4096]{5,4,2,3,0,1:T(4,128)(2,1)} %pad_maximum_fusion), calls=%async_computation.2 | async-start | bytes 4194304 | tf_op jit(solution)/shard_map/all_to_all | solution.py:22
  113.8 20.4 %all-to-all-start.3 = ((bf16[4,1,4,1,4,4096]{5,4,1,3,0,2:T(4,128)(2,1)}), bf16[4,1,4,1,4,4096]{5,4,1,3,0,2:T(4,128)(2,1)S(1)}, u32[]{:S(2)}, u32[]{:S(2)}) async-start(bf16[4,1,4,1,4,4096]{5,4,1,3,0,2:T(4,128)(2,1)} %copy.12), calls=%async_computation.3 | async-start | bytes 1048576 | tf_op jit(solution)/shard_map/all_to_all | solution.py:22
  121.3 123.5 %all-gather.2.cloned.1.call-start = ((), (), s32[]{:S(2)}) async-start(), calls=%async_computation.7 | async-start | bytes 8519680 | tf_op jit(solution)/shard_map/all_gather | solution.py:67
  135.4 2.2 copy-start
  267.7 19.8 %all-to-all-start.5 = ((f32[64,4,2,1,512]{4,1,0,3,2:T(4,128)}), f32[64,4,2,1,512]{4,1,0,3,2:T(4,128)S(1)}, u32[]{:S(2)}, u32[]{:S(2)}) async-start(f32[64,4,2,1,512]{4,1,0,3,2:T(4,128)} %copy.14), calls=%async_computation.5 | async-start | bytes 2097152 | tf_op jit(solution)/shard_map/all_to_all | solution.py:22
  288.8 26.8 %all-to-all-start.6 = ((f32[64,4,1,512]{3,1,2,0:T(4,128)}), f32[64,4,1,512]{3,1,2,0:T(4,128)S(1)}, u32[]{:S(2)}, u32[]{:S(2)}) async-start(f32[64,4,1,512]{3,1,2,0:T(4,128)} %bitcast_multiply_fusion.2), calls=%async_computation.6 | async-start | bytes 1048576 | tf_op jit(solution)/shard_map/all_to_all | solution.py:22
Sparse Core Ops, SparseCore 0:
  135.5 109.2 all-gather.1

commit v12 on v11

--- a/solution.py
+++ b/solution.py
@@ -64,7 +64,10 @@
     row_share = piece // n_rep
     own_sq = lax.psum(jnp.einsum("spt,spt->sp", pieces, pieces, preferred_element_type=jnp.float32), RP)
     own_inv = lax.dynamic_slice_in_dim(lax.rsqrt(own_sq + EPSILON), rep_index * row_share, row_share, axis=1)
-    flat_queries = lax.all_gather(pieces.reshape(STEPS * piece, term_cols), AX, axis=0, tiled=True)
+    flat_pieces, inverse, own_inv = lax.optimization_barrier(
+        (pieces.reshape(STEPS * piece, term_cols), inverse, own_inv)
+    )
+    flat_queries = lax.all_gather(flat_pieces, AX, axis=0, tiled=True)
     flat_queries, stored = lax.optimization_barrier((flat_queries, masked))
     similar = lax.optimization_barrier(
         lax.dot_general(flat_queries, stored, (((1,), (1,)), ((), ())), preferred_element_type=jnp.float32)

time: 327 us -> 333 us (1.018)
  blocking collectives: 20.6 us -> 54.9 us
  starting transfers between devices: 34.2 us -> 19.9 us
  waiting for transfers between devices: 180 us -> 168 us
    all_to_all x1 -> x3, blocking collectives: 5.42 us -> 49 us  [exchange(): lax.all_to_all(buf, name, split_axis=dim, concat_axis=dim, tiled=True)]
    all_to_all x6 -> x4, waiting for transfers between devices: 76.6 us -> 54.7 us  [exchange(): lax.all_to_all(buf, name, split_axis=dim, concat_axis=dim, tiled=True)]
    all_to_all x6 -> x4, starting transfers between devices: 34.2 us -> 19.9 us  [exchange(): lax.all_to_all(buf, name, split_axis=dim, concat_axis=dim, tiled=True)]
    all_gather x1, waiting for transfers between devices: 104 us -> 113 us  [on_device(): flat_queries = lax.all_gather(flat_pieces, AX, axis=0, tiled=True)]
    psum x1, blocking collectives: 15.2 us -> 5.82 us  [on_device(): doc_sq = lax.psum(partial_sq, RP)]
  transfers between devices with their start and end apart: 7 -> 5, of which waited for: 6 -> 4; matrix products, arithmetic and copies ran while one was open for 4% -> 4% of each run, Pallas kernels for 0% -> 0%
where the time goes in v12:
time: 333 us; the launch traced here: 329 us
  waiting for transfers between devices  168 us (50%)
  blocking collectives  54.9 us (16%)
  between operations  35.9 us (11%)
  local copies, waits for them, and re-layouts  28.4 us (9%)
  starting transfers between devices  19.9 us (6%)
  other arithmetic  11.9 us (4%)
  matrix products  10.4 us (3%)
    all_gather x1, waiting for transfers between devices, on_device(): flat_queries = lax.all_gather(flat_pieces, AX, axis=0, tiled=True)  113 us
    all_to_all x4, waiting for transfers between devices, exchange(): lax.all_to_all(buf, name, split_axis=dim, concat_axis=dim, tiled=True)  54.7 us
    all_to_all x3, blocking collectives, exchange(): lax.all_to_all(buf, name, split_axis=dim, concat_axis=dim, tiled=True)  49 us
    all_to_all x4, starting transfers between devices, exchange(): lax.all_to_all(buf, name, split_axis=dim, concat_axis=dim, tiled=True)  19.9 us
    dot_general x1, matrix products, on_device(): lax.dot_general(flat_queries, stored, (((1,), (1,)), ((), ())), preferred...  10.4 us
    reshape x4, local copies, waits for them, and re-layouts, scatter_from_owner(): blk.reshape(nx, nz, ny, rows // (nx * nz * ny), terms)  9.54 us
  transfers between devices with their start and end apart: 5, of which 4 were waited for; matrix products, arithmetic and copies ran while one was open for 4% of the time, Pallas kernels for 0%

profile of v12, /device:TPU:32, one launch (start us, length us, event | category | flops | bytes accessed | tf_op | source)
XLA Modules:
  0.0 329.2 jit_solution(9126084872864156713)
XLA Ops:
  6.5 0.7 convert_element_type.6
  7.2 3.4 %copy.24 = bf16[64,8,32,128]{3,2,1,0:T(8,128)(2,1)S(1)} copy(bf16[64,8,32,128]{3,1,2,0:T(8,128)(2,1)} %bitcast.47) | data formatting | bytes 8388608
  11.0 2.7 fusion.3
  13.8 2.5 reshape.58
  16.3 2.2 copy.10
  18.5 4.5 %all-to-all-start = ((bf16[4,4,4,4,4096]{4,3,1,0,2:T(4,128)(2,1)}), bf16[4,4,4,4,4096]{4,3,1,0,2:T(4,128)(2,1)}, u32[]{:S(2)}, u32[]{:S(2)}) async-start(bf16[4,4,4,4,4096]{4,3,1,0,2:T(4,128)(2,1)} %copy.10), calls=%async_computation | async-start | bytes 4194304 | tf_op jit(solution)/shard_map/all_to_all | solution.py:22
  23.0 2.5 reshape.59
  25.5 2.2 copy.11
  27.8 21.9 %all-to-all-done = bf16[4,4,4,4,4096]{4,3,1,0,2:T(4,128)(2,1)} async-done(((bf16[4,4,4,4,4096]{4,3,1,0,2:T(4,128)(2,1)}), bf16[4,4,4,4,4096]{4,3,1,0,2:T(4,128)(2,1)}, u32[]{:S(2)}, u32[]{:S(2)}) %all-to-all-start) | async-done | bytes 2097184 | tf_op jit(solution)/shard_map/all_to_all | solution.py:22
  49.7 3.6 %all-to-all-start.1 = ((bf16[4,4,4,4,4096]{4,3,1,0,2:T(4,128)(2,1)}), bf16[4,4,4,4,4096]{4,3,1,0,2:T(4,128)(2,1)S(1)}, u32[]{:S(2)}, u32[]{:S(2)}) async-start(bf16[4,4,4,4,4096]{4,3,1,0,2:T(4,128)(2,1)} %copy.11), calls=%async_computation.1 | async-start | bytes 4194304 | tf_op jit(solution)/shard_map/all_to_all | solution.py:22
  61.3 1.6 dynamic-slice_bitcast_fusion.3
  63.0 16.0 %all-to-all-done.1 = bf16[4,4,4,4,4096]{4,3,1,0,2:T(4,128)(2,1)S(1)} async-done(((bf16[4,4,4,4,4096]{4,3,1,0,2:T(4,128)(2,1)}), bf16[4,4,4,4,4096]{4,3,1,0,2:T(4,128)(2,1)S(1)}, u32[]{:S(2)}, u32[]{:S(2)}) %all-to-all-start.1) | async-done | bytes 2097184 | tf_op jit(solution)/shard_map/all_to_all | solution.py:22
  79.4 2.9 pad_maximum_fusion
  82.3 4.3 %all-to-all-start.2 = ((bf16[4,4,4,1,4,4096]{5,4,2,3,0,1:T(4,128)(2,1)}), bf16[4,4,4,1,4,4096]{5,4,2,3,0,1:T(4,128)(2,1)S(1)}, u32[]{:S(2)}, u32[]{:S(2)}) async-start(bf16[4,4,4,1,4,4096]{5,4,2,3,0,1:T(4,128)(2,1)} %pad_maximum_fusion), calls=%async_computation.2 | async-start | bytes 4194304 | tf_op jit(solution)/shard_map/all_to_all | solution.py:22
  86.6 0.7 fusion.6
  94.3 16.9 %all-to-all-done.2 = bf16[4,4,4,1,4,4096]{5,4,2,3,0,1:T(4,128)(2,1)S(1)} async-done(((bf16[4,4,4,1,4,4096]{5,4,2,3,0,1:T(4,128)(2,1)}), bf16[4,4,4,1,4,4096]{5,4,2,3,0,1:T(4,128)(2,1)S(1)}, u32[]{:S(2)}, u32[]{:S(2)}) %all-to-all-start.2) | async-done | bytes 2097184 | tf_op jit(solution)/shard_map/all_to_all | solution.py:22
  111.2 0.9 fusion.4
  112.8 1.0 copy.12
  113.8 7.6 %all-to-all-start.3 = ((bf16[4,1,4,1,4,4096]{5,4,1,3,0,2:T(4,128)(2,1)}), bf16[4,1,4,1,4,4096]{5,4,1,3,0,2:T(4,128)(2,1)S(1)}, u32[]{:S(2)}, u32[]{:S(2)}) async-start(bf16[4,1,4,1,4,4096]{5,4,1,3,0,2:T(4,128)(2,1)} %copy.12), calls=%async_computation.3 | async-start | bytes 1048576 | tf_op jit(solution)/shard_map/all_to_all | solution.py:22
  129.8 1.6 copy-done
  131.4 3.7 %fusion = (f32[512]{0:T(512)S(1)}, bf16[512,4096]{1,0:T(8,128)(2,1)}) fusion(bf16[512,4096]{1,0:T(8,128)(2,1)S(1)} %copy-done, bf16[64,8,32,128]{3,2,1,0:T(8,128)(2,1)S(1)} %bitcast.48), kind=kLoop, calls=%fused_computation.1 | loop fusion | flops 8388096 | bytes 12584960 | tf_op jit(solution)/shard_map/dt,dt->d/dot_general | solution.py:56
  135.7 5.8 %all-reduce = (f32[512]{0:T(512)S(1)}, f32[4,4]{0,1:T(4,128)S(1)}) all-reduce(f32[512]{0:T(512)S(1)} %get-tuple-element.19, f32[4,4]{0,1:T(4,128)S(1)} %copy.21), channel_id=1, replica_groups=mesh['x'=4,'zh'=4,'y'=4,'zl'=2,'c'=2] {'zl','c'}, use_global_device_ids=true, to_apply=%region_0.0 | all-reduce | flops 528 | bytes 4224 | tf_op jit(solution)/shard_map/psum | solution.py:57
  141.6 0.7 reshape_reshape.3
  142.3 113.0 %all-gather.2.cloned.1.call-done = bf16[1024,4096]{1,0:T(8,128)(2,1)} async-done(((bf16[16,4096]{1,0:T(8,128)(2,1)}), bf16[1024,4096]{1,0:T(8,128)(2,1)}) %all-gather.2.cloned.1.call-update) | async-done | bytes 8388624 | tf_op jit(solution)/shard_map/all_gather | solution.py:70
  255.3 10.4 %fusion.9 = f32[1024,512]{1,0:T(8,128)} fusion(bf16[1024,4096]{1,0:T(8,128)(2,1)} %all-gather.2.cloned.1.call-done, bf16[512,4096]{1,0:T(8,128)(2,1)} %get-tuple-element.12), kind=kOutput, calls=%fused_computation.45 | convolution fusion | flops 4294967296 | bytes 14680064 | tf_op jit(solution)/shard_map/dot_general | solution.py:73
  265.8 2.5 reshape.61
  268.2 1.2 copy.13
  269.4 5.4 %all_to_all.35 = f32[64,4,2,2,1,512]{5,2,1,0,4,3:T(2,128)S(1)} all-to-all(f32[64,4,2,2,1,512]{5,2,1,0,4,3:T(2,128)S(1)} %copy.13), channel_id=1, replica_groups=mesh['x'=4,'zh'=4,'y'=4,'zl'=2,'c'=2] {'c'}, dimensions={3} | all-to-all | bytes 4194304 | tf_op jit(solution)/shard_map/all_to_all | solution.py:22
  274.9 2.1 reduce_sum.22
  277.2 15.8 %all_to_all.36 = f32[64,4,2,1,512]{4,1,0,3,2:T(4,128)S(1)} all-to-all(f32[64,4,2,1,512]{4,1,0,3,2:T(4,128)S(1)} %copy.14), channel_id=1, replica_groups=mesh['x'=4,'zh'=4,'y'=4,'zl'=2,'c'=2] {'zl'}, dimensions={2} | all-to-all | bytes 2097152 | tf_op jit(solution)/shard_map/all_to_all | solution.py:22
  293.6 27.8 %all_to_all.37 = f32[64,4,1,512]{3,1,2,0:T(4,128)S(1)} all-to-all(f32[64,4,1,512]{3,1,2,0:T(4,128)S(1)} %bitcast_multiply_fusion.2), channel_id=1, replica_groups=mesh['x'=4,'zh'=4,'y'=4,'zl'=2,'c'=2] {'x','zh','y'}, dimensions={0} | all-to-all | bytes 1048576 | tf_op jit(solution)/shard_map/all_to_all | solution.py:22
  321.4 0.9 clamp_convert_fusion
  (29 shorter events, 4.1 us)
Async XLA Ops:
  18.5 31.1 %all-to-all-start = ((bf16[4,4,4,4,4096]{4,3,1,0,2:T(4,128)(2,1)}), bf16[4,4,4,4,4096]{4,3,1,0,2:T(4,128)(2,1)}, u32[]{:S(2)}, u32[]{:S(2)}) async-start(bf16[4,4,4,4,4096]{4,3,1,0,2:T(4,128)(2,1)} %copy.10), calls=%async_computation | async-start | bytes 4194304 | tf_op jit(solution)/shard_map/all_to_all | solution.py:22
  27.8 25.5 %copy-start.1 = (s32[4]{0:T(128)S(1)}, s32[4]{0:T(128)}, u32[]{:S(2)}) copy-start(s32[4]{0:T(128)} %param.5) | copy-start | bytes 52
  49.7 29.3 %all-to-all-start.1 = ((bf16[4,4,4,4,4096]{4,3,1,0,2:T(4,128)(2,1)}), bf16[4,4,4,4,4096]{4,3,1,0,2:T(4,128)(2,1)S(1)}, u32[]{:S(2)}, u32[]{:S(2)}) async-start(bf16[4,4,4,4,4096]{4,3,1,0,2:T(4,128)(2,1)} %copy.11), calls=%async_computation.1 | async-start | bytes 4194304 | tf_op jit(solution)/shard_map/all_to_all | solution.py:22
  82.3 28.9 %all-to-all-start.2 = ((bf16[4,4,4,1,4,4096]{5,4,2,3,0,1:T(4,128)(2,1)}), bf16[4,4,4,1,4,4096]{5,4,2,3,0,1:T(4,128)(2,1)S(1)}, u32[]{:S(2)}, u32[]{:S(2)}) async-start(bf16[4,4,4,1,4,4096]{5,4,2,3,0,1:T(4,128)(2,1)} %pad_maximum_fusion), calls=%async_computation.2 | async-start | bytes 4194304 | tf_op jit(solution)/shard_map/all_to_all | solution.py:22
  113.8 21.3 %all-to-all-start.3 = ((bf16[4,1,4,1,4,4096]{5,4,1,3,0,2:T(4,128)(2,1)}), bf16[4,1,4,1,4,4096]{5,4,1,3,0,2:T(4,128)(2,1)S(1)}, u32[]{:S(2)}, u32[]{:S(2)}) async-start(bf16[4,1,4,1,4,4096]{5,4,1,3,0,2:T(4,128)(2,1)} %copy.12), calls=%async_computation.3 | async-start | bytes 1048576 | tf_op jit(solution)/shard_map/all_to_all | solution.py:22
  121.4 134.0 %all-gather.2.cloned.1.call-start = ((), (), s32[]{:S(2)}) async-start(), calls=%async_computation.7 | async-start | bytes 8519680 | tf_op jit(solution)/shard_map/all_gather | solution.py:70
  129.2 2.2 copy-start
Sparse Core Ops, SparseCore 0:
  142.4 112.8 all-gather.1
